TPU v7x, 512 devices: a whole 4x8x8 slice. The times are simulated.
512 devices in a mesh: section: 16 (over y, core), expert: 32 (over z, x).
Axes of the slice: x: 4, y: 8, z: 8, core: 2. Of those that a mesh axis runs over, the one named last changes fastest.
Arguments:
- acts: bfloat16 [16, 4, 1024, 1024], P('section', None, 'expert'), may hold values from -6 to 6
- carried: bfloat16 [16, 1024, 1024], P('section', 'expert'), may hold values from -6 to 6
- loss_grad: bfloat16 [4, 1024, 1024], P(None, 'expert'), may hold values from -6 to 6
- expert_ids: int32 [16, 4, 1024, 8], P('section', None, 'expert'), may hold values from 0 to 31, all different within a row; in each aligned block of 32 rows (0 to 31, 32 to 63, ..., all dimensions but the last counted through in order) at most 12 rows name the same one
- probs: float32 [16, 4, 1024, 8], P('section', None, 'expert'), may hold values from 0.1 to 0.4
- w_gate: bfloat16 [16, 32, 1024, 384], P('section', 'expert'), may hold values from -0.1875 to 0.1875
- w_up: bfloat16 [16, 32, 1024, 384], P('section', 'expert'), may hold values from -0.1875 to 0.1875
- w_down: bfloat16 [16, 32, 384, 1024], P('section', 'expert'), may hold values from -0.3125 to 0.3125
Outputs:
- out_grad: bfloat16 [16, 4, 1024, 1024], P('section', None, 'expert')
- down_grad: bfloat16 [16, 32, 384, 1024], P('section', 'expert')
Inputs may be any that keep to these rules, and one draw needn't show every extreme that they name: `expert_ids`: in each aligned block of 32 tokens of one section and tick, no expert is named by more than 12 of the block's pairs, and in every draw some block has an expert named by exactly 12.
All inputs are finite; a program needn't handle non-finite values.
Results may differ from a plain program's by a relative error of at most 0.0095.
Values may be sent and summed in bfloat16 or wider, within the bound.
No kernel may reach another device: no remote copies, remote signals or barrier semaphores. Data moves between devices by JAX's collectives and lax.ppermute only.
A program may use at most 64 MiB of HBM per device.

v0:
```python
import jax
import jax.numpy as jnp
from jax import lax
from jax.sharding import PartitionSpec as P

TOPK = 8


def passed_along(value, axis, steps):
    count = lax.axis_size(axis)
    leading, last = (max(0, -steps), min(count, count - steps))
    return lax.ppermute(value, axis, [(source, source + steps) for source in range(leading, last)])


def slot_tables(expert_ids, probs, experts, slot_rows):
    tokens_here, choices_here = expert_ids.shape
    onehot = (expert_ids[:, :, None] == jnp.arange(experts, dtype=jnp.int32)[None, None, :]).astype(
        jnp.int32
    )
    pairs = onehot.reshape(tokens_here * choices_here, experts)
    before = jnp.cumsum(pairs, axis=0) - pairs
    position = jnp.sum(before * pairs, axis=1).reshape(tokens_here, choices_here)
    target = expert_ids * slot_rows + position
    match = target[None, :, :] == jnp.arange(experts * slot_rows, dtype=jnp.int32)[:, None, None]
    select = jnp.any(match, axis=2).astype(jnp.bfloat16)
    weight = jnp.sum(jnp.where(match, probs[None, :, :], 0.0), axis=(1, 2))
    return (select, weight)


def select_rows(select, source):
    return jnp.dot(select, source, preferred_element_type=jnp.float32)


def forward_parts(input_rows, gate_weight, up_weight):
    gate_pre = jnp.dot(input_rows, gate_weight, preferred_element_type=jnp.float32)
    up_pre = jnp.dot(input_rows, up_weight, preferred_element_type=jnp.float32)
    return (gate_pre, up_pre)


def expert_backward(gate_pre, up_pre, grad_rows, gate_weight, up_weight, down_weight):
    contract = (((1,), (1,)), ((), ()))
    sigma = jax.nn.sigmoid(gate_pre)
    active = gate_pre * sigma
    hidden = (active * up_pre).astype(jnp.bfloat16)
    hidden_grad = lax.dot_general(
        grad_rows, down_weight, contract, preferred_element_type=jnp.float32
    )
    gate_grad = (hidden_grad * up_pre * sigma * (1.0 + gate_pre * (1.0 - sigma))).astype(
        jnp.bfloat16
    )
    up_grad = (hidden_grad * active).astype(jnp.bfloat16)
    row_grad = lax.dot_general(gate_grad, gate_weight, contract, preferred_element_type=jnp.float32)
    row_grad = row_grad + lax.dot_general(
        up_grad, up_weight, contract, preferred_element_type=jnp.float32
    )
    return (row_grad.astype(jnp.bfloat16), hidden)


def per_device(acts, carried, loss_grad, expert_ids, probs, w_gate, w_up, w_down):
    experts = lax.axis_size("expert")
    ticks_here = acts.shape[1]
    tokens_here = acts.shape[2]
    width = acts.shape[3]
    slot_rows = min(tokens_here, 3 * tokens_here * TOPK // (2 * experts))
    gate_weight = w_gate[0, 0]
    up_weight = w_up[0, 0]
    down_weight = w_down[0, 0]
    is_last = lax.axis_index("section") == lax.axis_size("section") - 1
    tables = [
        slot_tables(expert_ids[0, moment], probs[0, moment], experts, slot_rows)
        for moment in range(ticks_here)
    ]
    rows_contract = (((0,), (0,)), ((), ()))
    incoming = jnp.where(is_last, loss_grad[0], carried[0])
    results = []
    down_sum = jnp.zeros((down_weight.shape[0], width), jnp.float32)
    for moment in range(ticks_here):
        select, weight = tables[moment]
        grad_rows = (
            (select_rows(select, incoming) * weight[:, None])
            .astype(jnp.bfloat16)
            .reshape(experts, slot_rows, width)
        )
        input_rows = (
            select_rows(select, acts[0, moment])
            .astype(jnp.bfloat16)
            .reshape(experts, slot_rows, width)
        )
        received_input, received_grad = (
            lax.all_to_all(input_rows, "expert", split_axis=0, concat_axis=0, tiled=True),
            lax.all_to_all(grad_rows, "expert", split_axis=0, concat_axis=0, tiled=True),
        )
        gate_pre, up_pre = forward_parts(received_input.reshape(-1, width), gate_weight, up_weight)
        flat_grad = received_grad.reshape(-1, width)
        row_grad, hidden = expert_backward(
            gate_pre, up_pre, flat_grad, gate_weight, up_weight, down_weight
        )
        returned = lax.all_to_all(
            row_grad.reshape(experts, slot_rows, width),
            "expert",
            split_axis=0,
            concat_axis=0,
            tiled=True,
        )
        gathered = lax.dot_general(
            select, returned.reshape(-1, width), rows_contract, preferred_element_type=jnp.float32
        )
        result = (incoming.astype(jnp.float32) + gathered).astype(jnp.bfloat16)
        results.append(result)
        down_sum = down_sum + lax.dot_general(
            hidden, flat_grad, rows_contract, preferred_element_type=jnp.float32
        )
        if moment + 1 < ticks_here:
            arriving = passed_along(result, "section", -1)
            incoming = jnp.where(is_last, loss_grad[moment + 1], arriving)
    out_grad = jnp.stack(results, axis=0)[None]
    return (out_grad, down_sum.astype(jnp.bfloat16)[None, None])


def solution(mesh):
    return jax.shard_map(
        per_device,
        mesh=mesh,
        in_specs=(
            P("section", None, "expert", None),
            P("section", "expert", None),
            P(None, "expert", None),
            P("section", None, "expert", None),
            P("section", None, "expert", None),
            P("section", "expert", None, None),
            P("section", "expert", None, None),
            P("section", "expert", None, None),
        ),
        out_specs=(P("section", None, "expert", None), P("section", "expert", None, None)),
        check_vma=False,
    )
```

profile of v0, /device:TPU:36, one launch (start us, length us, event | category | flops | bytes accessed | tf_op | source)
XLA Modules:
  0.0 431.7 jit_solution(2735775261610312197)
XLA Ops:
  6.0 13.4 %all-to-all-start.1 = ((bf16[32,12,1024]{2,1,0:T(8,128)(2,1)}), bf16[32,12,1024]{2,1,0:T(8,128)(2,1)S(1)}, u32[]{:S(2)}, u32[]{:S(2)}) async-start(bf16[32,12,1024]{2,1,0:T(8,128)(2,1)} %reshape.222), calls=%async_computation.1 | async-start | bytes 2097152 | tf_op jit(solution)/shard_map/all_to_all | solution.py:90
  22.8 24.8 %all-to-all-done.1 = bf16[32,12,1024]{2,1,0:T(8,128)(2,1)S(1)} async-done(((bf16[32,12,1024]{2,1,0:T(8,128)(2,1)}), bf16[32,12,1024]{2,1,0:T(8,128)(2,1)S(1)}, u32[]{:S(2)}, u32[]{:S(2)}) %all-to-all-start.1) | async-done | bytes 786464 | tf_op jit(solution)/shard_map/all_to_all | solution.py:90
  48.5 5.6 %all-to-all-start = ((bf16[32,12,1024]{2,1,0:T(8,128)(2,1)}), bf16[32,12,1024]{2,1,0:T(8,128)(2,1)}, u32[]{:S(2)}, u32[]{:S(2)}) async-start(bf16[32,12,1024]{2,1,0:T(8,128)(2,1)} %reshape.220), calls=%async_computation | async-start | bytes 2097152 | tf_op jit(solution)/shard_map/all_to_all | solution.py:91
  58.4 22.8 %all-to-all-done = bf16[32,12,1024]{2,1,0:T(8,128)(2,1)} async-done(((bf16[32,12,1024]{2,1,0:T(8,128)(2,1)}), bf16[32,12,1024]{2,1,0:T(8,128)(2,1)}, u32[]{:S(2)}, u32[]{:S(2)}) %all-to-all-start) | async-done | bytes 786464 | tf_op jit(solution)/shard_map/all_to_all | solution.py:91
  88.4 5.6 %all-to-all-start.2 = ((bf16[32,12,1024]{2,1,0:T(8,128)(2,1)}), bf16[32,12,1024]{2,1,0:T(8,128)(2,1)S(1)}, u32[]{:S(2)}, u32[]{:S(2)}) async-start(bf16[32,12,1024]{2,1,0:T(8,128)(2,1)} %reshape.224), calls=%async_computation.2 | async-start | bytes 2097152 | tf_op jit(solution)/shard_map/all_to_all | solution.py:98
  101.1 19.5 %all-to-all-done.2 = bf16[32,12,1024]{2,1,0:T(8,128)(2,1)S(1)} async-done(((bf16[32,12,1024]{2,1,0:T(8,128)(2,1)}), bf16[32,12,1024]{2,1,0:T(8,128)(2,1)S(1)}, u32[]{:S(2)}, u32[]{:S(2)}) %all-to-all-start.2) | async-done | bytes 786464 | tf_op jit(solution)/shard_map/all_to_all | solution.py:98
  120.6 5.6 %all-to-all-start.4 = ((bf16[32,12,1024]{2,1,0:T(8,128)(2,1)}), bf16[32,12,1024]{2,1,0:T(8,128)(2,1)}, u32[]{:S(2)}, u32[]{:S(2)}) async-start(bf16[32,12,1024]{2,1,0:T(8,128)(2,1)} %reshape.230), calls=%async_computation.4 | async-start | bytes 2097152 | tf_op jit(solution)/shard_map/all_to_all | solution.py:90
  135.0 17.8 %all-to-all-done.4 = bf16[32,12,1024]{2,1,0:T(8,128)(2,1)} async-done(((bf16[32,12,1024]{2,1,0:T(8,128)(2,1)}), bf16[32,12,1024]{2,1,0:T(8,128)(2,1)}, u32[]{:S(2)}, u32[]{:S(2)}) %all-to-all-start.4) | async-done | bytes 786464 | tf_op jit(solution)/shard_map/all_to_all | solution.py:90
  152.8 5.6 %all-to-all-start.3 = ((bf16[32,12,1024]{2,1,0:T(8,128)(2,1)}), bf16[32,12,1024]{2,1,0:T(8,128)(2,1)}, u32[]{:S(2)}, u32[]{:S(2)}) async-start(bf16[32,12,1024]{2,1,0:T(8,128)(2,1)} %reshape.228), calls=%async_computation.3 | async-start | bytes 2097152 | tf_op jit(solution)/shard_map/all_to_all | solution.py:91
  162.5 22.4 %all-to-all-done.3 = bf16[32,12,1024]{2,1,0:T(8,128)(2,1)} async-done(((bf16[32,12,1024]{2,1,0:T(8,128)(2,1)}), bf16[32,12,1024]{2,1,0:T(8,128)(2,1)}, u32[]{:S(2)}, u32[]{:S(2)}) %all-to-all-start.3) | async-done | bytes 786464 | tf_op jit(solution)/shard_map/all_to_all | solution.py:91
  192.2 5.7 %all-to-all-start.5 = ((bf16[32,12,1024]{2,1,0:T(8,128)(2,1)}), bf16[32,12,1024]{2,1,0:T(8,128)(2,1)S(1)}, u32[]{:S(2)}, u32[]{:S(2)}) async-start(bf16[32,12,1024]{2,1,0:T(8,128)(2,1)} %reshape.232), calls=%async_computation.5 | async-start | bytes 2097152 | tf_op jit(solution)/shard_map/all_to_all | solution.py:98
  205.1 19.4 %all-to-all-done.5 = bf16[32,12,1024]{2,1,0:T(8,128)(2,1)S(1)} async-done(((bf16[32,12,1024]{2,1,0:T(8,128)(2,1)}), bf16[32,12,1024]{2,1,0:T(8,128)(2,1)S(1)}, u32[]{:S(2)}, u32[]{:S(2)}) %all-to-all-start.5) | async-done | bytes 786464 | tf_op jit(solution)/shard_map/all_to_all | solution.py:98
  224.5 5.6 %all-to-all-start.7 = ((bf16[32,12,1024]{2,1,0:T(8,128)(2,1)}), bf16[32,12,1024]{2,1,0:T(8,128)(2,1)}, u32[]{:S(2)}, u32[]{:S(2)}) async-start(bf16[32,12,1024]{2,1,0:T(8,128)(2,1)} %reshape.238), calls=%async_computation.7 | async-start | bytes 2097152 | tf_op jit(solution)/shard_map/all_to_all | solution.py:90
  238.9 17.8 %all-to-all-done.7 = bf16[32,12,1024]{2,1,0:T(8,128)(2,1)} async-done(((bf16[32,12,1024]{2,1,0:T(8,128)(2,1)}), bf16[32,12,1024]{2,1,0:T(8,128)(2,1)}, u32[]{:S(2)}, u32[]{:S(2)}) %all-to-all-start.7) | async-done | bytes 786464 | tf_op jit(solution)/shard_map/all_to_all | solution.py:90
  256.7 5.6 %all-to-all-start.6 = ((bf16[32,12,1024]{2,1,0:T(8,128)(2,1)}), bf16[32,12,1024]{2,1,0:T(8,128)(2,1)}, u32[]{:S(2)}, u32[]{:S(2)}) async-start(bf16[32,12,1024]{2,1,0:T(8,128)(2,1)} %reshape.236), calls=%async_computation.6 | async-start | bytes 2097152 | tf_op jit(solution)/shard_map/all_to_all | solution.py:91
  266.5 22.4 %all-to-all-done.6 = bf16[32,12,1024]{2,1,0:T(8,128)(2,1)} async-done(((bf16[32,12,1024]{2,1,0:T(8,128)(2,1)}), bf16[32,12,1024]{2,1,0:T(8,128)(2,1)}, u32[]{:S(2)}, u32[]{:S(2)}) %all-to-all-start.6) | async-done | bytes 786464 | tf_op jit(solution)/shard_map/all_to_all | solution.py:91
  296.1 5.6 %all-to-all-start.8 = ((bf16[32,12,1024]{2,1,0:T(8,128)(2,1)}), bf16[32,12,1024]{2,1,0:T(8,128)(2,1)S(1)}, u32[]{:S(2)}, u32[]{:S(2)}) async-start(bf16[32,12,1024]{2,1,0:T(8,128)(2,1)} %reshape.240), calls=%async_computation.8 | async-start | bytes 2097152 | tf_op jit(solution)/shard_map/all_to_all | solution.py:98
  308.8 19.4 %all-to-all-done.8 = bf16[32,12,1024]{2,1,0:T(8,128)(2,1)S(1)} async-done(((bf16[32,12,1024]{2,1,0:T(8,128)(2,1)}), bf16[32,12,1024]{2,1,0:T(8,128)(2,1)S(1)}, u32[]{:S(2)}, u32[]{:S(2)}) %all-to-all-start.8) | async-done | bytes 786464 | tf_op jit(solution)/shard_map/all_to_all | solution.py:98
  328.2 5.6 %all-to-all-start.10 = ((bf16[32,12,1024]{2,1,0:T(8,128)(2,1)}), bf16[32,12,1024]{2,1,0:T(8,128)(2,1)}, u32[]{:S(2)}, u32[]{:S(2)}) async-start(bf16[32,12,1024]{2,1,0:T(8,128)(2,1)} %reshape.246), calls=%async_computation.10 | async-start | bytes 2097152 | tf_op jit(solution)/shard_map/all_to_all | solution.py:90
  342.5 17.8 %all-to-all-done.10 = bf16[32,12,1024]{2,1,0:T(8,128)(2,1)} async-done(((bf16[32,12,1024]{2,1,0:T(8,128)(2,1)}), bf16[32,12,1024]{2,1,0:T(8,128)(2,1)}, u32[]{:S(2)}, u32[]{:S(2)}) %all-to-all-start.10) | async-done | bytes 786464 | tf_op jit(solution)/shard_map/all_to_all | solution.py:90
  360.4 5.6 %all-to-all-start.9 = ((bf16[32,12,1024]{2,1,0:T(8,128)(2,1)}), bf16[32,12,1024]{2,1,0:T(8,128)(2,1)}, u32[]{:S(2)}, u32[]{:S(2)}) async-start(bf16[32,12,1024]{2,1,0:T(8,128)(2,1)} %reshape.244), calls=%async_computation.9 | async-start | bytes 2097152 | tf_op jit(solution)/shard_map/all_to_all | solution.py:91
  370.1 22.4 %all-to-all-done.9 = bf16[32,12,1024]{2,1,0:T(8,128)(2,1)} async-done(((bf16[32,12,1024]{2,1,0:T(8,128)(2,1)}), bf16[32,12,1024]{2,1,0:T(8,128)(2,1)}, u32[]{:S(2)}, u32[]{:S(2)}) %all-to-all-start.9) | async-done | bytes 786464 | tf_op jit(solution)/shard_map/all_to_all | solution.py:91
  397.6 5.6 %all-to-all-start.11 = ((bf16[32,12,1024]{2,1,0:T(8,128)(2,1)}), bf16[32,12,1024]{2,1,0:T(8,128)(2,1)S(1)}, u32[]{:S(2)}, u32[]{:S(2)}) async-start(bf16[32,12,1024]{2,1,0:T(8,128)(2,1)} %reshape.248), calls=%async_computation.11 | async-start | bytes 2097152 | tf_op jit(solution)/shard_map/all_to_all | solution.py:98
  409.8 19.9 %all-to-all-done.11 = bf16[32,12,1024]{2,1,0:T(8,128)(2,1)S(1)} async-done(((bf16[32,12,1024]{2,1,0:T(8,128)(2,1)}), bf16[32,12,1024]{2,1,0:T(8,128)(2,1)S(1)}, u32[]{:S(2)}, u32[]{:S(2)}) %all-to-all-start.11) | async-done | bytes 786464 | tf_op jit(solution)/shard_map/all_to_all | solution.py:98
  (189 shorter events, 108.6 us)
Async XLA Ops:
  0.6 54.9 %copy-start = (bf16[1,1,1024,384]{3,2,1,0:T(8,128)(2,1)S(1)}, bf16[1,1,1024,384]{3,2,1,0:T(8,128)(2,1)}, u32[]{:S(2)}) copy-start(bf16[1,1,1024,384]{3,2,1,0:T(8,128)(2,1)} %param.13) | copy-start | bytes 2359300
  4.8 14.7 %copy-start.28 = (f32[1,4,32,8]{2,3,1,0:T(8,128)S(1)}, f32[1,4,32,8]{2,3,1,0:T(8,128)}, u32[]{:S(2)}) copy-start(f32[1,4,32,8]{2,3,1,0:T(8,128)} %param.12) | copy-start | bytes 12292
  4.8 15.5 %copy-start.23 = (bf16[1,32,1024]{2,1,0:T(8,128)(2,1)S(1)}, bf16[1,32,1024]{2,1,0:T(8,128)(2,1)}, u32[]{:S(2)}) copy-start(bf16[1,32,1024]{2,1,0:T(8,128)(2,1)} %param.9) | copy-start | bytes 196612
  6.0 41.5 %all-to-all-start.1 = ((bf16[32,12,1024]{2,1,0:T(8,128)(2,1)}), bf16[32,12,1024]{2,1,0:T(8,128)(2,1)S(1)}, u32[]{:S(2)}, u32[]{:S(2)}) async-start(bf16[32,12,1024]{2,1,0:T(8,128)(2,1)} %reshape.222), calls=%async_computation.1 | async-start | bytes 2097152 | tf_op jit(solution)/shard_map/all_to_all | solution.py:90
  48.5 32.7 %all-to-all-start = ((bf16[32,12,1024]{2,1,0:T(8,128)(2,1)}), bf16[32,12,1024]{2,1,0:T(8,128)(2,1)}, u32[]{:S(2)}, u32[]{:S(2)}) async-start(bf16[32,12,1024]{2,1,0:T(8,128)(2,1)} %reshape.220), calls=%async_computation | async-start | bytes 2097152 | tf_op jit(solution)/shard_map/all_to_all | solution.py:91
  57.0 25.5 %copy-start.1 = (bf16[1,1,384,1024]{3,2,1,0:T(8,128)(2,1)S(1)}, bf16[1,1,384,1024]{3,2,1,0:T(8,128)(2,1)}, u32[]{:S(2)}) copy-start(bf16[1,1,384,1024]{3,2,1,0:T(8,128)(2,1)} %param.15) | copy-start | bytes 2359300
  88.4 32.2 %all-to-all-start.2 = ((bf16[32,12,1024]{2,1,0:T(8,128)(2,1)}), bf16[32,12,1024]{2,1,0:T(8,128)(2,1)S(1)}, u32[]{:S(2)}, u32[]{:S(2)}) async-start(bf16[32,12,1024]{2,1,0:T(8,128)(2,1)} %reshape.224), calls=%async_computation.2 | async-start | bytes 2097152 | tf_op jit(solution)/shard_map/all_to_all | solution.py:98
  99.0 27.3 %copy-start.31 = (f32[32,8]{0,1:T(8,128)S(1)}, f32[32,8]{0,1:T(8,128)}, u32[]{:S(2)}) copy-start(f32[32,8]{0,1:T(8,128)} %get-tuple-element.3) | copy-start | bytes 3076
  120.6 32.2 %all-to-all-start.4 = ((bf16[32,12,1024]{2,1,0:T(8,128)(2,1)}), bf16[32,12,1024]{2,1,0:T(8,128)(2,1)}, u32[]{:S(2)}, u32[]{:S(2)}) async-start(bf16[32,12,1024]{2,1,0:T(8,128)(2,1)} %reshape.230), calls=%async_computation.4 | async-start | bytes 2097152 | tf_op jit(solution)/shard_map/all_to_all | solution.py:90
  128.8 3.8 collective-permute-start
  152.8 32.2 %all-to-all-start.3 = ((bf16[32,12,1024]{2,1,0:T(8,128)(2,1)}), bf16[32,12,1024]{2,1,0:T(8,128)(2,1)}, u32[]{:S(2)}, u32[]{:S(2)}) async-start(bf16[32,12,1024]{2,1,0:T(8,128)(2,1)} %reshape.228), calls=%async_computation.3 | async-start | bytes 2097152 | tf_op jit(solution)/shard_map/all_to_all | solution.py:91
  190.1 7.9 %copy-start.29 = (s32[1,1,32,8]{2,3,1,0:T(8,128)S(1)}, s32[1,1,32,8]{2,3,1,0:T(8,128)}, u32[]{:S(2)}) copy-start(s32[1,1,32,8]{2,3,1,0:T(8,128)} %get-tuple-element.7) | copy-start | bytes 3076
  192.2 32.3 %all-to-all-start.5 = ((bf16[32,12,1024]{2,1,0:T(8,128)(2,1)}), bf16[32,12,1024]{2,1,0:T(8,128)(2,1)S(1)}, u32[]{:S(2)}, u32[]{:S(2)}) async-start(bf16[32,12,1024]{2,1,0:T(8,128)(2,1)} %reshape.232), calls=%async_computation.5 | async-start | bytes 2097152 | tf_op jit(solution)/shard_map/all_to_all | solution.py:98
  202.9 27.2 %copy-start.30 = (f32[32,8]{0,1:T(8,128)S(1)}, f32[32,8]{0,1:T(8,128)}, u32[]{:S(2)}) copy-start(f32[32,8]{0,1:T(8,128)} %get-tuple-element.5) | copy-start | bytes 3076
  224.5 32.2 %all-to-all-start.7 = ((bf16[32,12,1024]{2,1,0:T(8,128)(2,1)}), bf16[32,12,1024]{2,1,0:T(8,128)(2,1)}, u32[]{:S(2)}, u32[]{:S(2)}) async-start(bf16[32,12,1024]{2,1,0:T(8,128)(2,1)} %reshape.238), calls=%async_computation.7 | async-start | bytes 2097152 | tf_op jit(solution)/shard_map/all_to_all | solution.py:90
  232.6 3.8 collective-permute-start.1
  256.7 32.2 %all-to-all-start.6 = ((bf16[32,12,1024]{2,1,0:T(8,128)(2,1)}), bf16[32,12,1024]{2,1,0:T(8,128)(2,1)}, u32[]{:S(2)}, u32[]{:S(2)}) async-start(bf16[32,12,1024]{2,1,0:T(8,128)(2,1)} %reshape.236), calls=%async_computation.6 | async-start | bytes 2097152 | tf_op jit(solution)/shard_map/all_to_all | solution.py:91
  296.1 32.1 %all-to-all-start.8 = ((bf16[32,12,1024]{2,1,0:T(8,128)(2,1)}), bf16[32,12,1024]{2,1,0:T(8,128)(2,1)S(1)}, u32[]{:S(2)}, u32[]{:S(2)}) async-start(bf16[32,12,1024]{2,1,0:T(8,128)(2,1)} %reshape.240), calls=%async_computation.8 | async-start | bytes 2097152 | tf_op jit(solution)/shard_map/all_to_all | solution.py:98
  328.2 32.2 %all-to-all-start.10 = ((bf16[32,12,1024]{2,1,0:T(8,128)(2,1)}), bf16[32,12,1024]{2,1,0:T(8,128)(2,1)}, u32[]{:S(2)}, u32[]{:S(2)}) async-start(bf16[32,12,1024]{2,1,0:T(8,128)(2,1)} %reshape.246), calls=%async_computation.10 | async-start | bytes 2097152 | tf_op jit(solution)/shard_map/all_to_all | solution.py:90
  336.3 3.8 collective-permute-start.2
  360.4 32.2 %all-to-all-start.9 = ((bf16[32,12,1024]{2,1,0:T(8,128)(2,1)}), bf16[32,12,1024]{2,1,0:T(8,128)(2,1)}, u32[]{:S(2)}, u32[]{:S(2)}) async-start(bf16[32,12,1024]{2,1,0:T(8,128)(2,1)} %reshape.244), calls=%async_computation.9 | async-start | bytes 2097152 | tf_op jit(solution)/shard_map/all_to_all | solution.py:91
  397.6 32.1 %all-to-all-start.11 = ((bf16[32,12,1024]{2,1,0:T(8,128)(2,1)}), bf16[32,12,1024]{2,1,0:T(8,128)(2,1)S(1)}, u32[]{:S(2)}, u32[]{:S(2)}) async-start(bf16[32,12,1024]{2,1,0:T(8,128)(2,1)} %reshape.248), calls=%async_computation.11 | async-start | bytes 2097152 | tf_op jit(solution)/shard_map/all_to_all | solution.py:98
  409.8 21.2 %copy-start.25 = (bf16[32,1024]{1,0:T(8,128)(2,1)S(1)}, bf16[32,1024]{1,0:T(8,128)(2,1)}, u32[]{:S(2)}) copy-start(bf16[32,1024]{1,0:T(8,128)(2,1)} %copy-done.24) | copy-start | bytes 196612
  409.8 21.2 %copy-start.27 = (bf16[32,1024]{1,0:T(8,128)(2,1)S(1)}, bf16[32,1024]{1,0:T(8,128)(2,1)}, u32[]{:S(2)}) copy-start(bf16[32,1024]{1,0:T(8,128)(2,1)} %copy-done.26) | copy-start | bytes 196612
  (23 other events, 38.7 us)
where the time goes:
time: 434 us; the launch traced here: 432 us
  waiting for transfers between devices  252 us (58%)
  starting transfers between devices  81 us (19%)
  matrix products  44.5 us (10%)
  local copies, waits for them, and re-layouts  44.1 us (10%)
  other arithmetic  9.04 us (2%)
    all_to_all x4, waiting for transfers between devices, per_device(): lax.all_to_all(grad_rows, 'expert', split_axis=0, concat_axis=0, tiled=True)  90.1 us
    all_to_all x4, waiting for transfers between devices, per_device(): lax.all_to_all(row_grad.reshape(experts, slot_rows, width), 'expert', spl...  78.2 us
    all_to_all x4, waiting for transfers between devices, per_device(): lax.all_to_all(input_rows, 'expert', split_axis=0, concat_axis=0, tiled=T...  78.2 us
    all_to_all x4, starting transfers between devices, per_device(): lax.all_to_all(input_rows, 'expert', split_axis=0, concat_axis=0, tiled=T...  30.3 us
    all_to_all x4, starting transfers between devices, per_device(): lax.all_to_all(grad_rows, 'expert', split_axis=0, concat_axis=0, tiled=True)  22.5 us
    all_to_all x4, starting transfers between devices, per_device(): lax.all_to_all(row_grad.reshape(experts, slot_rows, width), 'expert', spl...  22.4 us
    dot_general x8, matrix products, select_rows(): return jnp.dot(select, source, preferred_element_type=jnp.float32)  12.7 us
  transfers between devices with their start and end apart: 15, of which 15 were waited for; matrix products, arithmetic and copies ran while one was open for 14% of the time, Pallas kernels for 0%

commit v1 on v0

--- a/solution.py
+++ b/solution.py
@@ -4,6 +4,7 @@
 from jax.sharding import PartitionSpec as P
 
 TOPK = 8
+LANES = 128
 
 
 def passed_along(value, axis, steps):
@@ -31,17 +32,21 @@
     return jnp.dot(select, source, preferred_element_type=jnp.float32)
 
 
-def forward_parts(input_rows, gate_weight, up_weight):
-    gate_pre = jnp.dot(input_rows, gate_weight, preferred_element_type=jnp.float32)
-    up_pre = jnp.dot(input_rows, up_weight, preferred_element_type=jnp.float32)
-    return (gate_pre, up_pre)
+def pack(rows, experts):
+    return rows.reshape(experts, -1, LANES)
 
 
-def expert_backward(gate_pre, up_pre, grad_rows, gate_weight, up_weight, down_weight):
+def unpack(block, width):
+    return block.reshape(-1, width)
+
+
+def exchange(block):
+    return lax.all_to_all(block, "expert", split_axis=0, concat_axis=0, tiled=True)
+
+
+def expert_backward(gate_pre, up_pre, sigma, grad_rows, gate_weight, up_weight, down_weight):
     contract = (((1,), (1,)), ((), ()))
-    sigma = jax.nn.sigmoid(gate_pre)
     active = gate_pre * sigma
-    hidden = (active * up_pre).astype(jnp.bfloat16)
     hidden_grad = lax.dot_general(
         grad_rows, down_weight, contract, preferred_element_type=jnp.float32
     )
@@ -53,7 +58,7 @@
     row_grad = row_grad + lax.dot_general(
         up_grad, up_weight, contract, preferred_element_type=jnp.float32
     )
-    return (row_grad.astype(jnp.bfloat16), hidden)
+    return row_grad.astype(jnp.bfloat16)
 
 
 def per_device(acts, carried, loss_grad, expert_ids, probs, w_gate, w_up, w_down):
@@ -62,6 +67,7 @@
     tokens_here = acts.shape[2]
     width = acts.shape[3]
     slot_rows = min(tokens_here, 3 * tokens_here * TOPK // (2 * experts))
+    rows_here = experts * slot_rows
     gate_weight = w_gate[0, 0]
     up_weight = w_up[0, 0]
     down_weight = w_down[0, 0]
@@ -71,48 +77,51 @@
         for moment in range(ticks_here)
     ]
     rows_contract = (((0,), (0,)), ((), ()))
+
+    def grad_rows_of(moment, incoming):
+        select, weight = tables[moment]
+        return (select_rows(select, incoming) * weight[:, None]).astype(jnp.bfloat16)
+
     incoming = jnp.where(is_last, loss_grad[0], carried[0])
+    parts = [
+        select_rows(tables[moment][0], acts[0, moment]).astype(jnp.bfloat16)
+        for moment in range(ticks_here)
+    ]
+    parts.append(grad_rows_of(0, incoming))
+    send = jnp.stack([pack(part, experts) for part in parts], axis=1)
+    count = len(parts)
+    received = exchange(send.reshape(experts, -1, LANES)).reshape(experts, count, -1, LANES)
+    received_inputs = jnp.concatenate(
+        [unpack(received[:, moment], width) for moment in range(ticks_here)], axis=0
+    )
+    flat_grad = unpack(received[:, ticks_here], width)
+
+    gate_all = jnp.dot(received_inputs, gate_weight, preferred_element_type=jnp.float32)
+    up_all = jnp.dot(received_inputs, up_weight, preferred_element_type=jnp.float32)
+    sigma_all = jax.nn.sigmoid(gate_all)
+    hidden_all = (gate_all * sigma_all * up_all).astype(jnp.bfloat16)
+
     results = []
     down_sum = jnp.zeros((down_weight.shape[0], width), jnp.float32)
     for moment in range(ticks_here):
-        select, weight = tables[moment]
-        grad_rows = (
-            (select_rows(select, incoming) * weight[:, None])
-            .astype(jnp.bfloat16)
-            .reshape(experts, slot_rows, width)
+        rows = slice(moment * rows_here, (moment + 1) * rows_here)
+        row_grad = expert_backward(
+            gate_all[rows], up_all[rows], sigma_all[rows], flat_grad, gate_weight, up_weight,
+            down_weight,
         )
-        input_rows = (
-            select_rows(select, acts[0, moment])
-            .astype(jnp.bfloat16)
-            .reshape(experts, slot_rows, width)
-        )
-        received_input, received_grad = (
-            lax.all_to_all(input_rows, "expert", split_axis=0, concat_axis=0, tiled=True),
-            lax.all_to_all(grad_rows, "expert", split_axis=0, concat_axis=0, tiled=True),
-        )
-        gate_pre, up_pre = forward_parts(received_input.reshape(-1, width), gate_weight, up_weight)
-        flat_grad = received_grad.reshape(-1, width)
-        row_grad, hidden = expert_backward(
-            gate_pre, up_pre, flat_grad, gate_weight, up_weight, down_weight
-        )
-        returned = lax.all_to_all(
-            row_grad.reshape(experts, slot_rows, width),
-            "expert",
-            split_axis=0,
-            concat_axis=0,
-            tiled=True,
-        )
+        returned = unpack(exchange(pack(row_grad, experts)), width)
         gathered = lax.dot_general(
-            select, returned.reshape(-1, width), rows_contract, preferred_element_type=jnp.float32
+            tables[moment][0], returned, rows_contract, preferred_element_type=jnp.float32
         )
         result = (incoming.astype(jnp.float32) + gathered).astype(jnp.bfloat16)
         results.append(result)
         down_sum = down_sum + lax.dot_general(
-            hidden, flat_grad, rows_contract, preferred_element_type=jnp.float32
+            hidden_all[rows], flat_grad, rows_contract, preferred_element_type=jnp.float32
         )
         if moment + 1 < ticks_here:
             arriving = passed_along(result, "section", -1)
             incoming = jnp.where(is_last, loss_grad[moment + 1], arriving)
+            flat_grad = unpack(exchange(pack(grad_rows_of(moment + 1, incoming), experts)), width)
     out_grad = jnp.stack(results, axis=0)[None]
     return (out_grad, down_sum.astype(jnp.bfloat16)[None, None])
 

time: 434 us -> 409 us (0.942)
  the two profiles are of different devices: /device:TPU:36 before, /device:TPU:26 now
where the time goes in v1:
time: 409 us; the launch traced here: 407 us
  blocking collectives  187 us (46%)
  waiting for transfers between devices  88.1 us (22%)
  local copies, waits for them, and re-layouts  51.6 us (13%)
  matrix products  41.8 us (10%)
  starting transfers between devices  29.8 us (7%)
  other arithmetic  7.86 us (2%)
    all_to_all x4, blocking collectives, exchange(): lax.all_to_all(block, 'expert', split_axis=0, concat_axis=0, tiled=True)  187 us
    all_to_all x4, waiting for transfers between devices, exchange(): lax.all_to_all(block, 'expert', split_axis=0, concat_axis=0, tiled=True)  85.1 us
    all_to_all x4, starting transfers between devices, exchange(): lax.all_to_all(block, 'expert', split_axis=0, concat_axis=0, tiled=True)  24 us
    reshape x7, local copies, waits for them, and re-layouts, pack(): return rows.reshape(experts, -1, LANES)  10.4 us
    unnamed x71, local copies, waits for them, and re-layouts  10 us
    reshape x7, local copies, waits for them, and re-layouts, unpack(): return block.reshape(-1, width)  9.32 us
    dot_general x8, matrix products, select_rows(): return jnp.dot(select, source, preferred_element_type=jnp.float32)  8.85 us
  transfers between devices with their start and end apart: 7, of which 7 were waited for; matrix products, arithmetic and copies ran while one was open for 2% of the time, Pallas kernels for 0%

profile of v1, /device:TPU:26, one launch (start us, length us, event | category | flops | bytes accessed | tf_op | source)
XLA Modules:
  0.0 407.5 jit_solution(4640305622411034797)
XLA Ops:
  12.7 2.1 convolution_convert_fusion
  21.1 2.2 stack_reshape.19
  27.5 103.3 %all_to_all.40 = bf16[32,480,128]{2,1,0:T(8,128)(2,1)S(1)} all-to-all(bf16[32,480,128]{2,1,0:T(8,128)(2,1)} %bitcast.230), channel_id=1, replica_groups=mesh['section'=16,'expert'=32] {'expert'}, dimensions={0} | all-to-all | bytes 7864320 | tf_op jit(solution)/shard_map/all_to_all | solution.py:44
  135.4 2.2 reshape_squeeze.18
  137.5 2.2 reshape_squeeze.19
  143.2 3.8 fusion.10
  147.1 3.1 multiply_convert_fusion
  154.2 5.6 %all-to-all-start.1 = ((bf16[32,96,128]{2,1,0:T(8,128)(2,1)}), bf16[32,96,128]{2,1,0:T(8,128)(2,1)S(1)}, u32[]{:S(2)}, u32[]{:S(2)}) async-start(bf16[32,96,128]{2,1,0:T(8,128)(2,1)} %reshape.204), calls=%async_computation.1 | async-start | bytes 1572864 | tf_op jit(solution)/shard_map/all_to_all | solution.py:44
  160.5 20.8 %all-to-all-done.1 = bf16[32,96,128]{2,1,0:T(8,128)(2,1)S(1)} async-done(((bf16[32,96,128]{2,1,0:T(8,128)(2,1)}), bf16[32,96,128]{2,1,0:T(8,128)(2,1)S(1)}, u32[]{:S(2)}, u32[]{:S(2)}) %all-to-all-start.1) | async-done | bytes 786464 | tf_op jit(solution)/shard_map/all_to_all | solution.py:44
  190.1 27.7 %all_to_all.41 = bf16[32,96,128]{2,1,0:T(8,128)(2,1)} all-to-all(bf16[32,96,128]{2,1,0:T(8,128)(2,1)} %reshape.206), channel_id=1, replica_groups=mesh['section'=16,'expert'=32] {'expert'}, dimensions={0} | all-to-all | bytes 1572864 | tf_op jit(solution)/shard_map/all_to_all | solution.py:44
  219.8 2.1 fusion.6
  221.9 2.8 add_convert_fusion.3
  224.6 2.1 reshape.208
  226.8 6.3 %all-to-all-start.3 = ((bf16[32,96,128]{2,1,0:T(8,128)(2,1)}), bf16[32,96,128]{2,1,0:T(8,128)(2,1)S(1)}, u32[]{:S(2)}, u32[]{:S(2)}) async-start(bf16[32,96,128]{2,1,0:T(8,128)(2,1)} %reshape.208), calls=%async_computation.3 | async-start | bytes 1572864 | tf_op jit(solution)/shard_map/all_to_all | solution.py:44
  234.4 22.2 %all-to-all-done.3 = bf16[32,96,128]{2,1,0:T(8,128)(2,1)S(1)} async-done(((bf16[32,96,128]{2,1,0:T(8,128)(2,1)}), bf16[32,96,128]{2,1,0:T(8,128)(2,1)S(1)}, u32[]{:S(2)}, u32[]{:S(2)}) %all-to-all-start.3) | async-done | bytes 786464 | tf_op jit(solution)/shard_map/all_to_all | solution.py:44
  265.4 27.9 %all_to_all.42 = bf16[32,96,128]{2,1,0:T(8,128)(2,1)} all-to-all(bf16[32,96,128]{2,1,0:T(8,128)(2,1)} %reshape.210), channel_id=1, replica_groups=mesh['section'=16,'expert'=32] {'expert'}, dimensions={0} | all-to-all | bytes 1572864 | tf_op jit(solution)/shard_map/all_to_all | solution.py:44
  295.4 2.1 fusion.4
  297.5 2.8 add_convert_fusion.2
  300.2 2.2 reshape.212
  302.4 6.0 %all-to-all-start.5 = ((bf16[32,96,128]{2,1,0:T(8,128)(2,1)}), bf16[32,96,128]{2,1,0:T(8,128)(2,1)S(1)}, u32[]{:S(2)}, u32[]{:S(2)}) async-start(bf16[32,96,128]{2,1,0:T(8,128)(2,1)} %reshape.212), calls=%async_computation.5 | async-start | bytes 1572864 | tf_op jit(solution)/shard_map/all_to_all | solution.py:44
  309.1 22.9 %all-to-all-done.5 = bf16[32,96,128]{2,1,0:T(8,128)(2,1)S(1)} async-done(((bf16[32,96,128]{2,1,0:T(8,128)(2,1)}), bf16[32,96,128]{2,1,0:T(8,128)(2,1)S(1)}, u32[]{:S(2)}, u32[]{:S(2)}) %all-to-all-start.5) | async-done | bytes 786464 | tf_op jit(solution)/shard_map/all_to_all | solution.py:44
  340.0 28.0 %all_to_all.43 = bf16[32,96,128]{2,1,0:T(8,128)(2,1)} all-to-all(bf16[32,96,128]{2,1,0:T(8,128)(2,1)} %reshape.214), channel_id=1, replica_groups=mesh['section'=16,'expert'=32] {'expert'}, dimensions={0} | all-to-all | bytes 1572864 | tf_op jit(solution)/shard_map/all_to_all | solution.py:44
  375.2 6.2 %all-to-all-start.7 = ((bf16[32,96,128]{2,1,0:T(8,128)(2,1)}), bf16[32,96,128]{2,1,0:T(8,128)(2,1)}, u32[]{:S(2)}, u32[]{:S(2)}) async-start(bf16[32,96,128]{2,1,0:T(8,128)(2,1)} %reshape.216), calls=%async_computation.7 | async-start | bytes 1572864 | tf_op jit(solution)/shard_map/all_to_all | solution.py:44
  385.8 19.2 %all-to-all-done.7 = bf16[32,96,128]{2,1,0:T(8,128)(2,1)} async-done(((bf16[32,96,128]{2,1,0:T(8,128)(2,1)}), bf16[32,96,128]{2,1,0:T(8,128)(2,1)}, u32[]{:S(2)}, u32[]{:S(2)}) %all-to-all-start.7) | async-done | bytes 786464 | tf_op jit(solution)/shard_map/all_to_all | solution.py:44
  (177 shorter events, 80.5 us)
Async XLA Ops:
  0.6 146.4 %copy-start = (bf16[1,1,1024,384]{3,2,1,0:T(8,128)(2,1)S(1)}, bf16[1,1,1024,384]{3,2,1,0:T(8,128)(2,1)}, u32[]{:S(2)}) copy-start(bf16[1,1,1024,384]{3,2,1,0:T(8,128)(2,1)} %param.14) | copy-start | bytes 2359300
  1.7 5.9 %copy-start.22 = (bf16[1,4,32,1024]{3,2,1,0:T(8,128)(2,1)S(1)}, bf16[1,4,32,1024]{3,2,1,0:T(8,128)(2,1)}, u32[]{:S(2)}) copy-start(bf16[1,4,32,1024]{3,2,1,0:T(8,128)(2,1)} %param.8) | copy-start | bytes 786436
  3.7 15.3 %copy-start.25 = (pred[384,32]{0,1:T(8,128)(4,1)}, pred[384,32]{0,1:T(8,128)(4,1)S(1)}, u32[]{:S(2)}) copy-start(pred[384,32]{0,1:T(8,128)(4,1)S(1)} %fusion.41) | copy-start | bytes 36868
  11.1 8.0 %copy-start.16 = (bf16[4,32,1024]{2,1,0:T(8,128)(2,1)S(1)}, bf16[4,32,1024]{2,1,0:T(8,128)(2,1)}, u32[]{:S(2)}) copy-start(bf16[4,32,1024]{2,1,0:T(8,128)(2,1)} %param.10) | copy-start | bytes 786436
  11.1 8.0 %copy-start.17 = (bf16[1,32,1024]{2,1,0:T(8,128)(2,1)S(1)}, bf16[1,32,1024]{2,1,0:T(8,128)(2,1)}, u32[]{:S(2)}) copy-start(bf16[1,32,1024]{2,1,0:T(8,128)(2,1)} %param.9) | copy-start | bytes 196612
  12.5 10.7 %copy-start.27 = (s32[32,8]{1,0:T(8,128)}, s32[32,8]{1,0:T(8,128)S(1)}, u32[]{:S(2)}) copy-start(s32[32,8]{1,0:T(8,128)S(1)} %bitcast_add_fusion) | copy-start | bytes 3076
  23.2 3.2 copy-start.11
  132.6 7.1 %copy-start.5 = (bf16[384,1024]{1,0:T(8,128)(2,1)}, bf16[384,1024]{1,0:T(8,128)(2,1)S(1)}, u32[]{:S(2)}) copy-start(bf16[384,1024]{1,0:T(8,128)(2,1)S(1)} %reshape_squeeze.15) | copy-start | bytes 2359300
  133.9 5.8 %copy-start.2 = (bf16[1,1,384,1024]{3,2,1,0:T(8,128)(2,1)S(1)}, bf16[1,1,384,1024]{3,2,1,0:T(8,128)(2,1)}, u32[]{:S(2)}) copy-start(bf16[1,1,384,1024]{3,2,1,0:T(8,128)(2,1)} %param.15) | copy-start | bytes 2359300
  140.3 2.9 copy-start.1
  143.2 3.9 copy-start.26
  147.0 3.8 copy-start.3
  154.2 27.1 %all-to-all-start.1 = ((bf16[32,96,128]{2,1,0:T(8,128)(2,1)}), bf16[32,96,128]{2,1,0:T(8,128)(2,1)S(1)}, u32[]{:S(2)}, u32[]{:S(2)}) async-start(bf16[32,96,128]{2,1,0:T(8,128)(2,1)} %reshape.204), calls=%async_computation.1 | async-start | bytes 1572864 | tf_op jit(solution)/shard_map/all_to_all | solution.py:44
  183.9 3.8 collective-permute-start
  226.8 29.9 %all-to-all-start.3 = ((bf16[32,96,128]{2,1,0:T(8,128)(2,1)}), bf16[32,96,128]{2,1,0:T(8,128)(2,1)S(1)}, u32[]{:S(2)}, u32[]{:S(2)}) async-start(bf16[32,96,128]{2,1,0:T(8,128)(2,1)} %reshape.208), calls=%async_computation.3 | async-start | bytes 1572864 | tf_op jit(solution)/shard_map/all_to_all | solution.py:44
  259.2 3.8 collective-permute-start.1
  302.4 29.6 %all-to-all-start.5 = ((bf16[32,96,128]{2,1,0:T(8,128)(2,1)}), bf16[32,96,128]{2,1,0:T(8,128)(2,1)S(1)}, u32[]{:S(2)}, u32[]{:S(2)}) async-start(bf16[32,96,128]{2,1,0:T(8,128)(2,1)} %reshape.212), calls=%async_computation.5 | async-start | bytes 1572864 | tf_op jit(solution)/shard_map/all_to_all | solution.py:44
  334.6 2.8 copy-start.20
  334.6 3.8 collective-permute-start.2
  374.0 7.5 %copy-start.6 = (bf16[384,1024]{1,0:T(8,128)(2,1)S(1)}, bf16[384,1024]{1,0:T(8,128)(2,1)}, u32[]{:S(2)}) copy-start(bf16[384,1024]{1,0:T(8,128)(2,1)} %copy-done.5) | copy-start | bytes 2359300
  375.2 7.9 %copy-start.8 = (bf16[384,1024]{1,0:T(8,128)(2,1)S(1)}, bf16[384,1024]{1,0:T(8,128)(2,1)}, u32[]{:S(2)}) copy-start(bf16[384,1024]{1,0:T(8,128)(2,1)} %copy-done.7) | copy-start | bytes 2359300
  375.2 29.8 %all-to-all-start.7 = ((bf16[32,96,128]{2,1,0:T(8,128)(2,1)}), bf16[32,96,128]{2,1,0:T(8,128)(2,1)}, u32[]{:S(2)}, u32[]{:S(2)}) async-start(bf16[32,96,128]{2,1,0:T(8,128)(2,1)} %reshape.216), calls=%async_computation.7 | async-start | bytes 1572864 | tf_op jit(solution)/shard_map/all_to_all | solution.py:44
  385.8 20.9 %copy-start.19 = (bf16[32,1024]{1,0:T(8,128)(2,1)S(1)}, bf16[32,1024]{1,0:T(8,128)(2,1)}, u32[]{:S(2)}) copy-start(bf16[32,1024]{1,0:T(8,128)(2,1)} %copy-done.18) | copy-start | bytes 196612
  385.8 20.9 %copy-start.21 = (bf16[32,1024]{1,0:T(8,128)(2,1)S(1)}, bf16[32,1024]{1,0:T(8,128)(2,1)}, u32[]{:S(2)}) copy-start(bf16[32,1024]{1,0:T(8,128)(2,1)} %copy-done.20) | copy-start | bytes 196612
  (13 other events, 24.9 us)

commit v2 on v1

--- a/solution.py
+++ b/solution.py
@@ -67,7 +67,6 @@
     tokens_here = acts.shape[2]
     width = acts.shape[3]
     slot_rows = min(tokens_here, 3 * tokens_here * TOPK // (2 * experts))
-    rows_here = experts * slot_rows
     gate_weight = w_gate[0, 0]
     up_weight = w_up[0, 0]
     down_weight = w_down[0, 0]
@@ -91,23 +90,18 @@
     send = jnp.stack([pack(part, experts) for part in parts], axis=1)
     count = len(parts)
     received = exchange(send.reshape(experts, -1, LANES)).reshape(experts, count, -1, LANES)
-    received_inputs = jnp.concatenate(
-        [unpack(received[:, moment], width) for moment in range(ticks_here)], axis=0
-    )
     flat_grad = unpack(received[:, ticks_here], width)
-
-    gate_all = jnp.dot(received_inputs, gate_weight, preferred_element_type=jnp.float32)
-    up_all = jnp.dot(received_inputs, up_weight, preferred_element_type=jnp.float32)
-    sigma_all = jax.nn.sigmoid(gate_all)
-    hidden_all = (gate_all * sigma_all * up_all).astype(jnp.bfloat16)
 
     results = []
     down_sum = jnp.zeros((down_weight.shape[0], width), jnp.float32)
     for moment in range(ticks_here):
-        rows = slice(moment * rows_here, (moment + 1) * rows_here)
+        received_input = unpack(received[:, moment], width)
+        gate_pre = jnp.dot(received_input, gate_weight, preferred_element_type=jnp.float32)
+        up_pre = jnp.dot(received_input, up_weight, preferred_element_type=jnp.float32)
+        sigma = jax.nn.sigmoid(gate_pre)
+        hidden = (gate_pre * sigma * up_pre).astype(jnp.bfloat16)
         row_grad = expert_backward(
-            gate_all[rows], up_all[rows], sigma_all[rows], flat_grad, gate_weight, up_weight,
-            down_weight,
+            gate_pre, up_pre, sigma, flat_grad, gate_weight, up_weight, down_weight
         )
         returned = unpack(exchange(pack(row_grad, experts)), width)
         gathered = lax.dot_general(
@@ -116,7 +110,7 @@
         result = (incoming.astype(jnp.float32) + gathered).astype(jnp.bfloat16)
         results.append(result)
         down_sum = down_sum + lax.dot_general(
-            hidden_all[rows], flat_grad, rows_contract, preferred_element_type=jnp.float32
+            hidden, flat_grad, rows_contract, preferred_element_type=jnp.float32
         )
         if moment + 1 < ticks_here:
             arriving = passed_along(result, "section", -1)

time: 409 us -> 392 us (0.958)
  blocking collectives: 187 us -> 103 us
  waiting for transfers between devices: 88.1 us -> 140 us
  starting transfers between devices: 29.8 us -> 46.9 us
    all_to_all x4 -> x1, blocking collectives: 187 us -> 103 us  [exchange(): lax.all_to_all(block, 'expert', split_axis=0, concat_axis=0, tiled=True)]
    all_to_all x4 -> x7, waiting for transfers between devices: 85.1 us -> 137 us  [exchange(): lax.all_to_all(block, 'expert', split_axis=0, concat_axis=0, tiled=True)]
    all_to_all x4 -> x7, starting transfers between devices: 24 us -> 40.8 us  [exchange(): lax.all_to_all(block, 'expert', split_axis=0, concat_axis=0, tiled=True)]
    dot_general x6 -> x12, matrix products: 11.3 us -> 16 us  [the longest x4 5.64 us: per_device(): jnp.dot(received_input, up_weight, preferred_element_type=jnp.float32)]
    unnamed x71 -> x82, local copies, waits for them, and re-layouts: 10 us -> 9.6 us
  transfers between devices with their start and end apart: 7 -> 10, of which waited for: 7 -> 10; matrix products, arithmetic and copies ran while one was open for 2% -> 6% of each run, Pallas kernels for 0% -> 0%
where the time goes in v2:
time: 392 us; the launch traced here: 390 us
  waiting for transfers between devices  140 us (36%)
  blocking collectives  103 us (26%)
  local copies, waits for them, and re-layouts  51 us (13%)
  starting transfers between devices  46.9 us (12%)
  matrix products  39.5 us (10%)
  other arithmetic  7.86 us (2%)
    all_to_all x7, waiting for transfers between devices, exchange(): lax.all_to_all(block, 'expert', split_axis=0, concat_axis=0, tiled=True)  137 us
    all_to_all x1, blocking collectives, exchange(): lax.all_to_all(block, 'expert', split_axis=0, concat_axis=0, tiled=True)  103 us
    all_to_all x7, starting transfers between devices, exchange(): lax.all_to_all(block, 'expert', split_axis=0, concat_axis=0, tiled=True)  40.8 us
    reshape x7, local copies, waits for them, and re-layouts, pack(): return rows.reshape(experts, -1, LANES)  11.3 us
    unnamed x82, local copies, waits for them, and re-layouts  9.6 us
    reshape x7, local copies, waits for them, and re-layouts, unpack(): return block.reshape(-1, width)  9.32 us
    dot_general x8, matrix products, select_rows(): return jnp.dot(select, source, preferred_element_type=jnp.float32)  8.85 us
  transfers between devices with their start and end apart: 10, of which 10 were waited for; matrix products, arithmetic and copies ran while one was open for 6% of the time, Pallas kernels for 0%

profile of v2, /device:TPU:26, one launch (start us, length us, event | category | flops | bytes accessed | tf_op | source)
XLA Modules:
  0.0 389.9 jit_solution(12154388353789280889)
XLA Ops:
  11.9 2.1 convolution_convert_fusion
  18.3 2.0 multiply_convert_fusion.3
  20.3 2.2 stack_reshape.19
  26.6 103.3 %all_to_all.40 = bf16[32,480,128]{2,1,0:T(8,128)(2,1)S(1)} all-to-all(bf16[32,480,128]{2,1,0:T(8,128)(2,1)} %bitcast.246), channel_id=1, replica_groups=mesh['section'=16,'expert'=32] {'expert'}, dimensions={0} | all-to-all | bytes 7864320 | tf_op jit(solution)/shard_map/all_to_all | solution.py:44
  140.0 2.2 reshape.204
  142.2 5.6 %all-to-all-start.1 = ((bf16[32,96,128]{2,1,0:T(8,128)(2,1)}), bf16[32,96,128]{2,1,0:T(8,128)(2,1)S(1)}, u32[]{:S(2)}, u32[]{:S(2)}) async-start(bf16[32,96,128]{2,1,0:T(8,128)(2,1)} %reshape.204), calls=%async_computation.1 | async-start | bytes 1572864 | tf_op jit(solution)/shard_map/all_to_all | solution.py:44
  148.4 20.8 %all-to-all-done.1 = bf16[32,96,128]{2,1,0:T(8,128)(2,1)S(1)} async-done(((bf16[32,96,128]{2,1,0:T(8,128)(2,1)}), bf16[32,96,128]{2,1,0:T(8,128)(2,1)S(1)}, u32[]{:S(2)}, u32[]{:S(2)}) %all-to-all-start.1) | async-done | bytes 786464 | tf_op jit(solution)/shard_map/all_to_all | solution.py:44
  171.8 2.1 collective-permute-start
  178.0 5.6 %all-to-all-start.2 = ((bf16[32,96,128]{2,1,0:T(8,128)(2,1)}), bf16[32,96,128]{2,1,0:T(8,128)(2,1)}, u32[]{:S(2)}, u32[]{:S(2)}) async-start(bf16[32,96,128]{2,1,0:T(8,128)(2,1)} %reshape.206), calls=%async_computation.2 | async-start | bytes 1572864 | tf_op jit(solution)/shard_map/all_to_all | solution.py:44
  187.9 17.8 %all-to-all-done.2 = bf16[32,96,128]{2,1,0:T(8,128)(2,1)} async-done(((bf16[32,96,128]{2,1,0:T(8,128)(2,1)}), bf16[32,96,128]{2,1,0:T(8,128)(2,1)}, u32[]{:S(2)}, u32[]{:S(2)}) %all-to-all-start.2) | async-done | bytes 786464 | tf_op jit(solution)/shard_map/all_to_all | solution.py:44
  210.9 2.2 reshape.208
  213.0 6.3 %all-to-all-start.3 = ((bf16[32,96,128]{2,1,0:T(8,128)(2,1)}), bf16[32,96,128]{2,1,0:T(8,128)(2,1)S(1)}, u32[]{:S(2)}, u32[]{:S(2)}) async-start(bf16[32,96,128]{2,1,0:T(8,128)(2,1)} %reshape.208), calls=%async_computation.3 | async-start | bytes 1572864 | tf_op jit(solution)/shard_map/all_to_all | solution.py:44
  220.7 22.2 %all-to-all-done.3 = bf16[32,96,128]{2,1,0:T(8,128)(2,1)S(1)} async-done(((bf16[32,96,128]{2,1,0:T(8,128)(2,1)}), bf16[32,96,128]{2,1,0:T(8,128)(2,1)S(1)}, u32[]{:S(2)}, u32[]{:S(2)}) %all-to-all-start.3) | async-done | bytes 786464 | tf_op jit(solution)/shard_map/all_to_all | solution.py:44
  251.7 5.6 %all-to-all-start.4 = ((bf16[32,96,128]{2,1,0:T(8,128)(2,1)}), bf16[32,96,128]{2,1,0:T(8,128)(2,1)}, u32[]{:S(2)}, u32[]{:S(2)}) async-start(bf16[32,96,128]{2,1,0:T(8,128)(2,1)} %reshape.210), calls=%async_computation.4 | async-start | bytes 1572864 | tf_op jit(solution)/shard_map/all_to_all | solution.py:44
  261.5 18.1 %all-to-all-done.4 = bf16[32,96,128]{2,1,0:T(8,128)(2,1)} async-done(((bf16[32,96,128]{2,1,0:T(8,128)(2,1)}), bf16[32,96,128]{2,1,0:T(8,128)(2,1)}, u32[]{:S(2)}, u32[]{:S(2)}) %all-to-all-start.4) | async-done | bytes 786464 | tf_op jit(solution)/shard_map/all_to_all | solution.py:44
  284.8 2.2 reshape.212
  286.9 6.0 %all-to-all-start.5 = ((bf16[32,96,128]{2,1,0:T(8,128)(2,1)}), bf16[32,96,128]{2,1,0:T(8,128)(2,1)S(1)}, u32[]{:S(2)}, u32[]{:S(2)}) async-start(bf16[32,96,128]{2,1,0:T(8,128)(2,1)} %reshape.212), calls=%async_computation.5 | async-start | bytes 1572864 | tf_op jit(solution)/shard_map/all_to_all | solution.py:44
  293.6 22.9 %all-to-all-done.5 = bf16[32,96,128]{2,1,0:T(8,128)(2,1)S(1)} async-done(((bf16[32,96,128]{2,1,0:T(8,128)(2,1)}), bf16[32,96,128]{2,1,0:T(8,128)(2,1)S(1)}, u32[]{:S(2)}, u32[]{:S(2)}) %all-to-all-start.5) | async-done | bytes 786464 | tf_op jit(solution)/shard_map/all_to_all | solution.py:44
  319.2 2.1 collective-permute-start.2
  324.6 5.6 %all-to-all-start.6 = ((bf16[32,96,128]{2,1,0:T(8,128)(2,1)}), bf16[32,96,128]{2,1,0:T(8,128)(2,1)}, u32[]{:S(2)}, u32[]{:S(2)}) async-start(bf16[32,96,128]{2,1,0:T(8,128)(2,1)} %reshape.214), calls=%async_computation.6 | async-start | bytes 1572864 | tf_op jit(solution)/shard_map/all_to_all | solution.py:44
  334.5 18.1 %all-to-all-done.6 = bf16[32,96,128]{2,1,0:T(8,128)(2,1)} async-done(((bf16[32,96,128]{2,1,0:T(8,128)(2,1)}), bf16[32,96,128]{2,1,0:T(8,128)(2,1)}, u32[]{:S(2)}, u32[]{:S(2)}) %all-to-all-start.6) | async-done | bytes 786464 | tf_op jit(solution)/shard_map/all_to_all | solution.py:44
  357.8 6.1 %all-to-all-start.7 = ((bf16[32,96,128]{2,1,0:T(8,128)(2,1)}), bf16[32,96,128]{2,1,0:T(8,128)(2,1)}, u32[]{:S(2)}, u32[]{:S(2)}) async-start(bf16[32,96,128]{2,1,0:T(8,128)(2,1)} %reshape.216), calls=%async_computation.7 | async-start | bytes 1572864 | tf_op jit(solution)/shard_map/all_to_all | solution.py:44
  363.9 2.0 fusion.46
  370.2 17.3 %all-to-all-done.7 = bf16[32,96,128]{2,1,0:T(8,128)(2,1)} async-done(((bf16[32,96,128]{2,1,0:T(8,128)(2,1)}), bf16[32,96,128]{2,1,0:T(8,128)(2,1)}, u32[]{:S(2)}, u32[]{:S(2)}) %all-to-all-start.7) | async-done | bytes 786464 | tf_op jit(solution)/shard_map/all_to_all | solution.py:44
  (196 shorter events, 88.2 us)
Async XLA Ops:
  0.6 131.4 %copy-start = (bf16[1,1,1024,384]{3,2,1,0:T(8,128)(2,1)S(1)}, bf16[1,1,1024,384]{3,2,1,0:T(8,128)(2,1)}, u32[]{:S(2)}) copy-start(bf16[1,1,1024,384]{3,2,1,0:T(8,128)(2,1)} %param.13) | copy-start | bytes 2359300
  3.7 14.5 %copy-start.33 = (pred[384,32]{0,1:T(8,128)(4,1)}, pred[384,32]{0,1:T(8,128)(4,1)S(1)}, u32[]{:S(2)}) copy-start(pred[384,32]{0,1:T(8,128)(4,1)S(1)} %fusion.45) | copy-start | bytes 36868
  5.0 2.6 copy-start.30
  10.6 7.7 %copy-start.14 = (bf16[4,32,1024]{2,1,0:T(8,128)(2,1)S(1)}, bf16[4,32,1024]{2,1,0:T(8,128)(2,1)}, u32[]{:S(2)}) copy-start(bf16[4,32,1024]{2,1,0:T(8,128)(2,1)} %param.10) | copy-start | bytes 786436
  10.6 7.7 %copy-start.25 = (bf16[1,32,1024]{2,1,0:T(8,128)(2,1)S(1)}, bf16[1,32,1024]{2,1,0:T(8,128)(2,1)}, u32[]{:S(2)}) copy-start(bf16[1,32,1024]{2,1,0:T(8,128)(2,1)} %param.9) | copy-start | bytes 196612
  11.7 8.6 %copy-start.34 = (s32[32,8]{1,0:T(8,128)}, s32[32,8]{1,0:T(8,128)S(1)}, u32[]{:S(2)}) copy-start(s32[32,8]{1,0:T(8,128)S(1)} %bitcast_add_fusion) | copy-start | bytes 3076
  133.4 2.8 copy-start.1
  142.2 27.1 %all-to-all-start.1 = ((bf16[32,96,128]{2,1,0:T(8,128)(2,1)}), bf16[32,96,128]{2,1,0:T(8,128)(2,1)S(1)}, u32[]{:S(2)}, u32[]{:S(2)}) async-start(bf16[32,96,128]{2,1,0:T(8,128)(2,1)} %reshape.204), calls=%async_computation.1 | async-start | bytes 1572864 | tf_op jit(solution)/shard_map/all_to_all | solution.py:44
  171.8 3.8 collective-permute-start
  178.0 27.7 %all-to-all-start.2 = ((bf16[32,96,128]{2,1,0:T(8,128)(2,1)}), bf16[32,96,128]{2,1,0:T(8,128)(2,1)}, u32[]{:S(2)}, u32[]{:S(2)}) async-start(bf16[32,96,128]{2,1,0:T(8,128)(2,1)} %reshape.206), calls=%async_computation.2 | async-start | bytes 1572864 | tf_op jit(solution)/shard_map/all_to_all | solution.py:44
  207.1 2.2 copy-start.5
  213.0 29.9 %all-to-all-start.3 = ((bf16[32,96,128]{2,1,0:T(8,128)(2,1)}), bf16[32,96,128]{2,1,0:T(8,128)(2,1)S(1)}, u32[]{:S(2)}, u32[]{:S(2)}) async-start(bf16[32,96,128]{2,1,0:T(8,128)(2,1)} %reshape.208), calls=%async_computation.3 | async-start | bytes 1572864 | tf_op jit(solution)/shard_map/all_to_all | solution.py:44
  245.5 2.8 copy-start.26
  245.5 3.8 collective-permute-start.1
  251.7 28.0 %all-to-all-start.4 = ((bf16[32,96,128]{2,1,0:T(8,128)(2,1)}), bf16[32,96,128]{2,1,0:T(8,128)(2,1)}, u32[]{:S(2)}, u32[]{:S(2)}) async-start(bf16[32,96,128]{2,1,0:T(8,128)(2,1)} %reshape.210), calls=%async_computation.4 | async-start | bytes 1572864 | tf_op jit(solution)/shard_map/all_to_all | solution.py:44
  281.0 2.2 copy-start.7
  286.9 29.6 %all-to-all-start.5 = ((bf16[32,96,128]{2,1,0:T(8,128)(2,1)}), bf16[32,96,128]{2,1,0:T(8,128)(2,1)S(1)}, u32[]{:S(2)}, u32[]{:S(2)}) async-start(bf16[32,96,128]{2,1,0:T(8,128)(2,1)} %reshape.212), calls=%async_computation.5 | async-start | bytes 1572864 | tf_op jit(solution)/shard_map/all_to_all | solution.py:44
  319.1 3.0 copy-start.28
  319.2 3.8 collective-permute-start.2
  324.6 28.0 %all-to-all-start.6 = ((bf16[32,96,128]{2,1,0:T(8,128)(2,1)}), bf16[32,96,128]{2,1,0:T(8,128)(2,1)}, u32[]{:S(2)}, u32[]{:S(2)}) async-start(bf16[32,96,128]{2,1,0:T(8,128)(2,1)} %reshape.214), calls=%async_computation.6 | async-start | bytes 1572864 | tf_op jit(solution)/shard_map/all_to_all | solution.py:44
  356.6 7.3 %copy-start.4 = (bf16[384,1024]{1,0:T(8,128)(2,1)S(1)}, bf16[384,1024]{1,0:T(8,128)(2,1)}, u32[]{:S(2)}) copy-start(bf16[384,1024]{1,0:T(8,128)(2,1)} %copy-done.3) | copy-start | bytes 2359300
  357.8 29.7 %all-to-all-start.7 = ((bf16[32,96,128]{2,1,0:T(8,128)(2,1)}), bf16[32,96,128]{2,1,0:T(8,128)(2,1)}, u32[]{:S(2)}, u32[]{:S(2)}) async-start(bf16[32,96,128]{2,1,0:T(8,128)(2,1)} %reshape.216), calls=%async_computation.7 | async-start | bytes 1572864 | tf_op jit(solution)/shard_map/all_to_all | solution.py:44
  370.2 19.0 %copy-start.27 = (bf16[32,1024]{1,0:T(8,128)(2,1)S(1)}, bf16[32,1024]{1,0:T(8,128)(2,1)}, u32[]{:S(2)}) copy-start(bf16[32,1024]{1,0:T(8,128)(2,1)} %copy-done.26) | copy-start | bytes 196612
  370.2 19.0 %copy-start.29 = (bf16[32,1024]{1,0:T(8,128)(2,1)S(1)}, bf16[32,1024]{1,0:T(8,128)(2,1)}, u32[]{:S(2)}) copy-start(bf16[32,1024]{1,0:T(8,128)(2,1)} %copy-done.28) | copy-start | bytes 196612
  (23 other events, 34.2 us)

commit v3 on v2

--- a/solution.py
+++ b/solution.py
@@ -14,17 +14,16 @@
 
 
 def slot_tables(expert_ids, probs, experts, slot_rows):
-    tokens_here, choices_here = expert_ids.shape
-    onehot = (expert_ids[:, :, None] == jnp.arange(experts, dtype=jnp.int32)[None, None, :]).astype(
-        jnp.int32
-    )
-    pairs = onehot.reshape(tokens_here * choices_here, experts)
-    before = jnp.cumsum(pairs, axis=0) - pairs
-    position = jnp.sum(before * pairs, axis=1).reshape(tokens_here, choices_here)
+    ticks_here, tokens_here, choices_here = expert_ids.shape
+    onehot = (expert_ids[..., None] == jnp.arange(experts, dtype=jnp.int32)).astype(jnp.int32)
+    pairs = onehot.reshape(ticks_here, tokens_here * choices_here, experts)
+    before = jnp.cumsum(pairs, axis=1) - pairs
+    position = jnp.sum(before * pairs, axis=2).reshape(ticks_here, tokens_here, choices_here)
     target = expert_ids * slot_rows + position
-    match = target[None, :, :] == jnp.arange(experts * slot_rows, dtype=jnp.int32)[:, None, None]
-    select = jnp.any(match, axis=2).astype(jnp.bfloat16)
-    weight = jnp.sum(jnp.where(match, probs[None, :, :], 0.0), axis=(1, 2))
+    slots = jnp.arange(experts * slot_rows, dtype=jnp.int32)
+    match = target[:, None, :, :] == slots[None, :, None, None]
+    select = jnp.any(match, axis=3).astype(jnp.bfloat16)
+    weight = jnp.sum(jnp.where(match, probs[:, None, :, :], 0.0), axis=(2, 3))
     return (select, weight)
 
 
@@ -71,24 +70,25 @@
     up_weight = w_up[0, 0]
     down_weight = w_down[0, 0]
     is_last = lax.axis_index("section") == lax.axis_size("section") - 1
-    tables = [
-        slot_tables(expert_ids[0, moment], probs[0, moment], experts, slot_rows)
-        for moment in range(ticks_here)
-    ]
+    select_all, weight_all = slot_tables(expert_ids[0], probs[0], experts, slot_rows)
     rows_contract = (((0,), (0,)), ((), ()))
 
     def grad_rows_of(moment, incoming):
-        select, weight = tables[moment]
+        select, weight = select_all[moment], weight_all[moment]
         return (select_rows(select, incoming) * weight[:, None]).astype(jnp.bfloat16)
 
     incoming = jnp.where(is_last, loss_grad[0], carried[0])
-    parts = [
-        select_rows(tables[moment][0], acts[0, moment]).astype(jnp.bfloat16)
-        for moment in range(ticks_here)
-    ]
-    parts.append(grad_rows_of(0, incoming))
-    send = jnp.stack([pack(part, experts) for part in parts], axis=1)
-    count = len(parts)
+    count = ticks_here + 1
+    chooser = jnp.concatenate([select_all, select_all[:1]], axis=0)
+    sources = jnp.concatenate([acts[0], incoming[None]], axis=0)
+    scale = jnp.concatenate(
+        [jnp.ones((ticks_here, select_all.shape[1]), jnp.float32), weight_all[:1]], axis=0
+    )
+    picked = lax.dot_general(
+        chooser, sources, (((2,), (1,)), ((0,), (0,))), preferred_element_type=jnp.float32
+    )
+    picked = (picked * scale[:, :, None]).astype(jnp.bfloat16)
+    send = picked.reshape(count, experts, -1, LANES).transpose(1, 0, 2, 3)
     received = exchange(send.reshape(experts, -1, LANES)).reshape(experts, count, -1, LANES)
     flat_grad = unpack(received[:, ticks_here], width)
 
@@ -105,7 +105,7 @@
         )
         returned = unpack(exchange(pack(row_grad, experts)), width)
         gathered = lax.dot_general(
-            tables[moment][0], returned, rows_contract, preferred_element_type=jnp.float32
+            select_all[moment], returned, rows_contract, preferred_element_type=jnp.float32
         )
         result = (incoming.astype(jnp.float32) + gathered).astype(jnp.bfloat16)
         results.append(result)

time: 392 us -> 377 us (0.962)
  the two profiles are of different devices: /device:TPU:26 before, /device:TPU:18 now
where the time goes in v3:
time: 377 us; the launch traced here: 375 us
  blocking collectives  187 us (50%)
  waiting for transfers between devices  79.6 us (21%)
  local copies, waits for them, and re-layouts  43.1 us (11%)
  matrix products  31.5 us (8%)
  starting transfers between devices  28.3 us (8%)
  other arithmetic  4.16 us (1%)
    all_to_all x4, blocking collectives, exchange(): lax.all_to_all(block, 'expert', split_axis=0, concat_axis=0, tiled=True)  187 us
    all_to_all x4, waiting for transfers between devices, exchange(): lax.all_to_all(block, 'expert', split_axis=0, concat_axis=0, tiled=True)  73.9 us
    all_to_all x4, starting transfers between devices, exchange(): lax.all_to_all(block, 'expert', split_axis=0, concat_axis=0, tiled=True)  22.5 us
    reshape x7, local copies, waits for them, and re-layouts, unpack(): return block.reshape(-1, width)  9.95 us
    reshape x2, local copies, waits for them, and re-layouts, per_device(): send = picked.reshape(count, experts, -1, LANES).transpose(1, 0, 2, 3)  9.84 us
    reshape x7, local copies, waits for them, and re-layouts, pack(): return rows.reshape(experts, -1, LANES)  9.12 us
  transfers between devices with their start and end apart: 7, of which 7 were waited for; matrix products, arithmetic and copies ran while one was open for 5% of the time, Pallas kernels for 0%

profile of v3, /device:TPU:18, one launch (start us, length us, event | category | flops | bytes accessed | tf_op | source)
XLA Modules:
  0.0 375.3 jit_solution(12343243809257411166)
XLA Ops:
  1.8 2.3 reduce-window.6
  5.8 3.1 multiply_convert_fusion
  8.9 7.1 %reshape.96 = bf16[5,32,96,128]{3,2,1,0:T(8,128)(2,1)} reshape(bf16[5,384,1024]{2,1,0:T(8,128)(2,1)} %multiply_convert_fusion) | data formatting | bytes 7864320 | tf_op jit(solution)/shard_map/reshape | solution.py:91
  15.9 2.8 copy.27
  18.7 103.1 %all_to_all.40 = bf16[32,480,128]{2,1,0:T(8,128)(2,1)S(1)} all-to-all(bf16[32,480,128]{2,1,0:T(8,128)(2,1)S(1)} %bitcast.156), channel_id=1, replica_groups=mesh['section'=16,'expert'=32] {'expert'}, dimensions={0} | all-to-all | bytes 7864320 | tf_op jit(solution)/shard_map/all_to_all | solution.py:43
  121.9 1.7 fusion.87
  133.3 27.0 %all_to_all.41 = bf16[32,96,128]{2,1,0:T(8,128)(2,1)} all-to-all(bf16[32,96,128]{2,1,0:T(8,128)(2,1)S(1)} %reshape.99), channel_id=1, replica_groups=mesh['section'=16,'expert'=32] {'expert'}, dimensions={0} | all-to-all | bytes 1572864 | tf_op jit(solution)/shard_map/all_to_all | solution.py:43
  162.0 1.9 collective-permute-start
  163.9 1.9 collective-permute-done
  167.4 5.6 %all-to-all-start.2 = ((bf16[32,96,128]{2,1,0:T(8,128)(2,1)}), bf16[32,96,128]{2,1,0:T(8,128)(2,1)}, u32[]{:S(2)}, u32[]{:S(2)}) async-start(bf16[32,96,128]{2,1,0:T(8,128)(2,1)} %reshape.101), calls=%async_computation.2 | async-start | bytes 1572864 | tf_op jit(solution)/shard_map/all_to_all | solution.py:43
  177.4 18.9 %all-to-all-done.2 = bf16[32,96,128]{2,1,0:T(8,128)(2,1)} async-done(((bf16[32,96,128]{2,1,0:T(8,128)(2,1)}), bf16[32,96,128]{2,1,0:T(8,128)(2,1)}, u32[]{:S(2)}, u32[]{:S(2)}) %all-to-all-start.2) | async-done | bytes 786464 | tf_op jit(solution)/shard_map/all_to_all | solution.py:43
  202.9 28.6 %all_to_all.42 = bf16[32,96,128]{2,1,0:T(8,128)(2,1)} all-to-all(bf16[32,96,128]{2,1,0:T(8,128)(2,1)S(1)} %reshape.103), channel_id=1, replica_groups=mesh['section'=16,'expert'=32] {'expert'}, dimensions={0} | all-to-all | bytes 1572864 | tf_op jit(solution)/shard_map/all_to_all | solution.py:43
  233.2 1.9 collective-permute-start.1
  235.1 1.9 collective-permute-done.1
  238.6 5.6 %all-to-all-start.4 = ((bf16[32,96,128]{2,1,0:T(8,128)(2,1)}), bf16[32,96,128]{2,1,0:T(8,128)(2,1)}, u32[]{:S(2)}, u32[]{:S(2)}) async-start(bf16[32,96,128]{2,1,0:T(8,128)(2,1)} %reshape.105), calls=%async_computation.4 | async-start | bytes 1572864 | tf_op jit(solution)/shard_map/all_to_all | solution.py:43
  248.5 19.0 %all-to-all-done.4 = bf16[32,96,128]{2,1,0:T(8,128)(2,1)} async-done(((bf16[32,96,128]{2,1,0:T(8,128)(2,1)}), bf16[32,96,128]{2,1,0:T(8,128)(2,1)}, u32[]{:S(2)}, u32[]{:S(2)}) %all-to-all-start.4) | async-done | bytes 786464 | tf_op jit(solution)/shard_map/all_to_all | solution.py:43
  274.1 28.6 %all_to_all.43 = bf16[32,96,128]{2,1,0:T(8,128)(2,1)} all-to-all(bf16[32,96,128]{2,1,0:T(8,128)(2,1)S(1)} %reshape.107), channel_id=1, replica_groups=mesh['section'=16,'expert'=32] {'expert'}, dimensions={0} | all-to-all | bytes 1572864 | tf_op jit(solution)/shard_map/all_to_all | solution.py:43
  304.4 1.9 collective-permute-start.2
  306.3 1.9 collective-permute-done.2
  309.8 5.6 %all-to-all-start.6 = ((bf16[32,96,128]{2,1,0:T(8,128)(2,1)}), bf16[32,96,128]{2,1,0:T(8,128)(2,1)}, u32[]{:S(2)}, u32[]{:S(2)}) async-start(bf16[32,96,128]{2,1,0:T(8,128)(2,1)} %reshape.109), calls=%async_computation.6 | async-start | bytes 1572864 | tf_op jit(solution)/shard_map/all_to_all | solution.py:43
  319.8 18.9 %all-to-all-done.6 = bf16[32,96,128]{2,1,0:T(8,128)(2,1)} async-done(((bf16[32,96,128]{2,1,0:T(8,128)(2,1)}), bf16[32,96,128]{2,1,0:T(8,128)(2,1)}, u32[]{:S(2)}, u32[]{:S(2)}) %all-to-all-start.6) | async-done | bytes 786464 | tf_op jit(solution)/shard_map/all_to_all | solution.py:43
  343.9 5.7 %all-to-all-start.7 = ((bf16[32,96,128]{2,1,0:T(8,128)(2,1)}), bf16[32,96,128]{2,1,0:T(8,128)(2,1)}, u32[]{:S(2)}, u32[]{:S(2)}) async-start(bf16[32,96,128]{2,1,0:T(8,128)(2,1)} %reshape.111), calls=%async_computation.7 | async-start | bytes 1572864 | tf_op jit(solution)/shard_map/all_to_all | solution.py:43
  349.7 1.8 fusion.46
  355.8 17.1 %all-to-all-done.7 = bf16[32,96,128]{2,1,0:T(8,128)(2,1)} async-done(((bf16[32,96,128]{2,1,0:T(8,128)(2,1)}), bf16[32,96,128]{2,1,0:T(8,128)(2,1)}, u32[]{:S(2)}, u32[]{:S(2)}) %all-to-all-start.7) | async-done | bytes 786464 | tf_op jit(solution)/shard_map/all_to_all | solution.py:43
  (138 shorter events, 59.9 us)
Async XLA Ops:
  0.6 123.3 %copy-start = (bf16[1,1,1024,384]{3,2,1,0:T(8,128)(2,1)S(1)}, bf16[1,1,1024,384]{3,2,1,0:T(8,128)(2,1)}, u32[]{:S(2)}) copy-start(bf16[1,1,1024,384]{3,2,1,0:T(8,128)(2,1)} %param.13) | copy-start | bytes 2359300
  0.6 4.6 %copy-start.33 = (f32[1,4,32,8]{2,3,1,0:T(8,128)S(1)}, f32[1,4,32,8]{2,3,1,0:T(8,128)}, u32[]{:S(2)}) copy-start(f32[1,4,32,8]{2,3,1,0:T(8,128)} %param.12) | copy-start | bytes 12292
  0.7 5.1 %copy-start.13 = (bf16[4,32,1024]{2,1,0:T(8,128)(2,1)S(1)}, bf16[4,32,1024]{2,1,0:T(8,128)(2,1)}, u32[]{:S(2)}) copy-start(bf16[4,32,1024]{2,1,0:T(8,128)(2,1)} %param.10) | copy-start | bytes 786436
  0.7 5.1 %copy-start.32 = (bf16[1,32,1024]{2,1,0:T(8,128)(2,1)S(1)}, bf16[1,32,1024]{2,1,0:T(8,128)(2,1)}, u32[]{:S(2)}) copy-start(bf16[1,32,1024]{2,1,0:T(8,128)(2,1)} %param.9) | copy-start | bytes 196612
  0.7 5.1 %copy-start.27 = (bf16[1,4,32,1024]{3,2,1,0:T(8,128)(2,1)S(1)}, bf16[1,4,32,1024]{3,2,1,0:T(8,128)(2,1)}, u32[]{:S(2)}) copy-start(bf16[1,4,32,1024]{3,2,1,0:T(8,128)(2,1)} %param.8) | copy-start | bytes 786436
  125.3 2.8 copy-start.1
  128.1 2.2 copy-start.3
  162.0 3.8 %copy-start.25 = (bf16[32,1024]{1,0:T(8,128)(2,1)}, bf16[32,1024]{1,0:T(8,128)(2,1)S(1)}, u32[]{:S(2)}) copy-start(bf16[32,1024]{1,0:T(8,128)(2,1)S(1)} %fusion.2) | copy-start | bytes 196612
  162.0 3.8 %collective-permute-start = (bf16[32,1024]{1,0:T(8,128)(2,1)S(1)}, bf16[32,1024]{1,0:T(8,128)(2,1)S(1)}, u32[]{:S(2)}, u32[]{:S(2)}) collective-permute-start(bf16[32,1024]{1,0:T(8,128)(2,1)S(1)} %fusion.2), channel_id=1, source_target_pairs={{32,0},{64,32},{96,64},{128,96},{160,128},{192,160},{224,192},{256... | collective-permute-start | bytes 196616 | tf_op jit(solution)/shard_map/ppermute | solution.py:13
  167.4 28.9 %all-to-all-start.2 = ((bf16[32,96,128]{2,1,0:T(8,128)(2,1)}), bf16[32,96,128]{2,1,0:T(8,128)(2,1)}, u32[]{:S(2)}, u32[]{:S(2)}) async-start(bf16[32,96,128]{2,1,0:T(8,128)(2,1)} %reshape.101), calls=%async_computation.2 | async-start | bytes 1572864 | tf_op jit(solution)/shard_map/all_to_all | solution.py:43
  197.7 2.2 copy-start.5
  233.2 3.8 %copy-start.28 = (bf16[32,1024]{1,0:T(8,128)(2,1)}, bf16[32,1024]{1,0:T(8,128)(2,1)S(1)}, u32[]{:S(2)}) copy-start(bf16[32,1024]{1,0:T(8,128)(2,1)S(1)} %add_convert_fusion.7) | copy-start | bytes 196612
  233.2 3.8 %collective-permute-start.1 = (bf16[32,1024]{1,0:T(8,128)(2,1)S(1)}, bf16[32,1024]{1,0:T(8,128)(2,1)S(1)}, u32[]{:S(2)}, u32[]{:S(2)}) collective-permute-start(bf16[32,1024]{1,0:T(8,128)(2,1)S(1)} %add_convert_fusion.7), channel_id=1, source_target_pairs={{32,0},{64,32},{96,64},{128,96},{160,128},{192,160},{224,192},{256... | collective-permute-start | bytes 196616 | tf_op jit(solution)/shard_map/ppermute | solution.py:13
  238.6 28.9 %all-to-all-start.4 = ((bf16[32,96,128]{2,1,0:T(8,128)(2,1)}), bf16[32,96,128]{2,1,0:T(8,128)(2,1)}, u32[]{:S(2)}, u32[]{:S(2)}) async-start(bf16[32,96,128]{2,1,0:T(8,128)(2,1)} %reshape.105), calls=%async_computation.4 | async-start | bytes 1572864 | tf_op jit(solution)/shard_map/all_to_all | solution.py:43
  268.9 2.2 copy-start.7
  304.4 3.8 %copy-start.30 = (bf16[32,1024]{1,0:T(8,128)(2,1)}, bf16[32,1024]{1,0:T(8,128)(2,1)S(1)}, u32[]{:S(2)}) copy-start(bf16[32,1024]{1,0:T(8,128)(2,1)S(1)} %add_convert_fusion.6) | copy-start | bytes 196612
  304.4 3.8 %collective-permute-start.2 = (bf16[32,1024]{1,0:T(8,128)(2,1)S(1)}, bf16[32,1024]{1,0:T(8,128)(2,1)S(1)}, u32[]{:S(2)}, u32[]{:S(2)}) collective-permute-start(bf16[32,1024]{1,0:T(8,128)(2,1)S(1)} %add_convert_fusion.6), channel_id=1, source_target_pairs={{32,0},{64,32},{96,64},{128,96},{160,128},{192,160},{224,192},{256... | collective-permute-start | bytes 196616 | tf_op jit(solution)/shard_map/ppermute | solution.py:13
  309.8 28.9 %all-to-all-start.6 = ((bf16[32,96,128]{2,1,0:T(8,128)(2,1)}), bf16[32,96,128]{2,1,0:T(8,128)(2,1)}, u32[]{:S(2)}, u32[]{:S(2)}) async-start(bf16[32,96,128]{2,1,0:T(8,128)(2,1)} %reshape.109), calls=%async_computation.6 | async-start | bytes 1572864 | tf_op jit(solution)/shard_map/all_to_all | solution.py:43
  342.7 6.9 %copy-start.4 = (bf16[384,1024]{1,0:T(8,128)(2,1)S(1)}, bf16[384,1024]{1,0:T(8,128)(2,1)}, u32[]{:S(2)}) copy-start(bf16[384,1024]{1,0:T(8,128)(2,1)} %copy-done.3) | copy-start | bytes 2359300
  343.9 5.7 %copy-start.15 = (f32[384,384]{1,0:T(8,128)S(1)}, f32[384,384]{1,0:T(8,128)}, u32[]{:S(2)}) copy-start(f32[384,384]{1,0:T(8,128)} %fusion.17) | copy-start | bytes 1769476
  343.9 28.9 %all-to-all-start.7 = ((bf16[32,96,128]{2,1,0:T(8,128)(2,1)}), bf16[32,96,128]{2,1,0:T(8,128)(2,1)}, u32[]{:S(2)}, u32[]{:S(2)}) async-start(bf16[32,96,128]{2,1,0:T(8,128)(2,1)} %reshape.111), calls=%async_computation.7 | async-start | bytes 1572864 | tf_op jit(solution)/shard_map/all_to_all | solution.py:43
  355.8 18.8 %copy-start.26 = (bf16[32,1024]{1,0:T(8,128)(2,1)S(1)}, bf16[32,1024]{1,0:T(8,128)(2,1)}, u32[]{:S(2)}) copy-start(bf16[32,1024]{1,0:T(8,128)(2,1)} %copy-done.25) | copy-start | bytes 196612
  355.8 18.8 %copy-start.29 = (bf16[32,1024]{1,0:T(8,128)(2,1)S(1)}, bf16[32,1024]{1,0:T(8,128)(2,1)}, u32[]{:S(2)}) copy-start(bf16[32,1024]{1,0:T(8,128)(2,1)} %copy-done.28) | copy-start | bytes 196612
  355.8 18.8 %copy-start.31 = (bf16[32,1024]{1,0:T(8,128)(2,1)S(1)}, bf16[32,1024]{1,0:T(8,128)(2,1)}, u32[]{:S(2)}) copy-start(bf16[32,1024]{1,0:T(8,128)(2,1)} %copy-done.30) | copy-start | bytes 196612
  (17 other events, 24.4 us)

commit v4 on v3

--- a/solution.py
+++ b/solution.py
@@ -79,23 +79,31 @@
 
     incoming = jnp.where(is_last, loss_grad[0], carried[0])
     count = ticks_here + 1
+    tokens_here = acts.shape[2]
     chooser = jnp.concatenate([select_all, select_all[:1]], axis=0)
-    sources = jnp.concatenate([acts[0], incoming[None]], axis=0)
+    chooser = chooser.reshape(count, experts, slot_rows, tokens_here).transpose(1, 0, 2, 3)
+    blocks = jnp.eye(count, dtype=jnp.bfloat16)[None, :, None, :, None]
+    chooser = (chooser[:, :, :, None, :] * blocks).reshape(experts, count * slot_rows, -1)
     scale = jnp.concatenate(
         [jnp.ones((ticks_here, select_all.shape[1]), jnp.float32), weight_all[:1]], axis=0
     )
+    scale = scale.reshape(count, experts, slot_rows).transpose(1, 0, 2).reshape(experts, -1)
+    aligned = -(-count * slot_rows // 16) * 16
+    spare = aligned - count * slot_rows
+    chooser = jnp.pad(chooser, ((0, 0), (0, spare), (0, 0)))
+    scale = jnp.pad(scale, ((0, 0), (0, spare)))
+    sources = jnp.concatenate([acts[0], incoming[None]], axis=0).reshape(-1, width)
     picked = lax.dot_general(
-        chooser, sources, (((2,), (1,)), ((0,), (0,))), preferred_element_type=jnp.float32
+        chooser, sources, (((2,), (0,)), ((), ())), preferred_element_type=jnp.float32
     )
-    picked = (picked * scale[:, :, None]).astype(jnp.bfloat16)
-    send = picked.reshape(count, experts, -1, LANES).transpose(1, 0, 2, 3)
-    received = exchange(send.reshape(experts, -1, LANES)).reshape(experts, count, -1, LANES)
-    flat_grad = unpack(received[:, ticks_here], width)
+    send = (picked * scale[:, :, None]).astype(jnp.bfloat16)
+    received = exchange(send)[:, : count * slot_rows].reshape(experts, count, slot_rows, width)
+    flat_grad = received[:, ticks_here].reshape(-1, width)
 
     results = []
     down_sum = jnp.zeros((down_weight.shape[0], width), jnp.float32)
     for moment in range(ticks_here):
-        received_input = unpack(received[:, moment], width)
+        received_input = received[:, moment].reshape(-1, width)
         gate_pre = jnp.dot(received_input, gate_weight, preferred_element_type=jnp.float32)
         up_pre = jnp.dot(received_input, up_weight, preferred_element_type=jnp.float32)
         sigma = jax.nn.sigmoid(gate_pre)

time: 377 us -> 383 us (1.016)
  blocking collectives: 187 us -> 193 us
  waiting for transfers between devices: 79.6 us -> 75.5 us
    reshape x2 -> x3, local copies, waits for them, and re-layouts: 9.84 us -> 0.28 us  [the longest x1 0.16 us: per_device(): chooser.reshape(count, experts, slot_rows, tokens_here)]
    slice x3 -> x9, local copies, waits for them, and re-layouts: 1.92 us -> 9.41 us  [the longest x4 4.82 us: per_device(): received_input = received[:, moment].reshape(-1, width)]
    all_to_all x4, blocking collectives: 187 us -> 193 us  [exchange(): lax.all_to_all(block, 'expert', split_axis=0, concat_axis=0, tiled=True)]
    mul x0 -> x4, local copies, waits for them, and re-layouts: none -> 5.12 us  [per_device(): chooser[:, :, :, None, :] * blocks]
    all_to_all x4, waiting for transfers between devices: 73.9 us -> 69.9 us  [exchange(): lax.all_to_all(block, 'expert', split_axis=0, concat_axis=0, tiled=True)]
  transfers between devices with their start and end apart: 7 -> 7, of which waited for: 7 -> 7; matrix products, arithmetic and copies ran while one was open for 5% -> 6% of each run, Pallas kernels for 0% -> 0%
where the time goes in v4:
time: 383 us; the launch traced here: 382 us
  blocking collectives  193 us (50%)
  waiting for transfers between devices  75.5 us (20%)
  local copies, waits for them, and re-layouts  46.2 us (12%)
  matrix products  30.9 us (8%)
  starting transfers between devices  28.5 us (7%)
  other arithmetic  6.36 us (2%)
    all_to_all x4, blocking collectives, exchange(): lax.all_to_all(block, 'expert', split_axis=0, concat_axis=0, tiled=True)  193 us
    all_to_all x4, waiting for transfers between devices, exchange(): lax.all_to_all(block, 'expert', split_axis=0, concat_axis=0, tiled=True)  69.9 us
    all_to_all x4, starting transfers between devices, exchange(): lax.all_to_all(block, 'expert', split_axis=0, concat_axis=0, tiled=True)  22.8 us
    reshape x7, local copies, waits for them, and re-layouts, unpack(): return block.reshape(-1, width)  9.99 us
    reshape x7, local copies, waits for them, and re-layouts, pack(): return rows.reshape(experts, -1, LANES)  9.27 us
  transfers between devices with their start and end apart: 7, of which 7 were waited for; matrix products, arithmetic and copies ran while one was open for 6% of the time, Pallas kernels for 0%

profile of v4, /device:TPU:18, one launch (start us, length us, event | category | flops | bytes accessed | tf_op | source)
XLA Modules:
  0.0 382.0 jit_solution(2723628577335682031)
XLA Ops:
  1.7 2.3 reduce-window.6
  8.3 3.5 copy.55
  16.3 108.7 %all_to_all.40 = bf16[32,64,1024]{2,1,0:T(8,128)(2,1)S(1)} all-to-all(bf16[32,64,1024]{2,1,0:T(8,128)(2,1)S(1)} %multiply_convert_fusion), channel_id=1, replica_groups=mesh['section'=16,'expert'=32] {'expert'}, dimensions={0} | all-to-all | bytes 8388608 | tf_op jit(solution)/shard_map/all_to_all | solution.py:43
  125.0 2.2 copy.59
  127.2 1.8 fusion.83
  134.0 1.8 fusion.38
  139.4 27.0 %all_to_all.41 = bf16[32,96,128]{2,1,0:T(8,128)(2,1)} all-to-all(bf16[32,96,128]{2,1,0:T(8,128)(2,1)S(1)} %reshape.119), channel_id=1, replica_groups=mesh['section'=16,'expert'=32] {'expert'}, dimensions={0} | all-to-all | bytes 1572864 | tf_op jit(solution)/shard_map/all_to_all | solution.py:43
  168.2 1.9 collective-permute-start
  170.1 1.9 collective-permute-done
  173.7 5.7 %all-to-all-start.2 = ((bf16[32,96,128]{2,1,0:T(8,128)(2,1)}), bf16[32,96,128]{2,1,0:T(8,128)(2,1)}, u32[]{:S(2)}, u32[]{:S(2)}) async-start(bf16[32,96,128]{2,1,0:T(8,128)(2,1)} %reshape.121), calls=%async_computation.2 | async-start | bytes 1572864 | tf_op jit(solution)/shard_map/all_to_all | solution.py:43
  185.0 17.7 %all-to-all-done.2 = bf16[32,96,128]{2,1,0:T(8,128)(2,1)} async-done(((bf16[32,96,128]{2,1,0:T(8,128)(2,1)}), bf16[32,96,128]{2,1,0:T(8,128)(2,1)}, u32[]{:S(2)}, u32[]{:S(2)}) %all-to-all-start.2) | async-done | bytes 786464 | tf_op jit(solution)/shard_map/all_to_all | solution.py:43
  209.3 28.6 %all_to_all.42 = bf16[32,96,128]{2,1,0:T(8,128)(2,1)} all-to-all(bf16[32,96,128]{2,1,0:T(8,128)(2,1)S(1)} %reshape.123), channel_id=1, replica_groups=mesh['section'=16,'expert'=32] {'expert'}, dimensions={0} | all-to-all | bytes 1572864 | tf_op jit(solution)/shard_map/all_to_all | solution.py:43
  239.6 1.9 collective-permute-start.1
  241.6 1.9 collective-permute-done.1
  245.1 5.7 %all-to-all-start.4 = ((bf16[32,96,128]{2,1,0:T(8,128)(2,1)}), bf16[32,96,128]{2,1,0:T(8,128)(2,1)}, u32[]{:S(2)}, u32[]{:S(2)}) async-start(bf16[32,96,128]{2,1,0:T(8,128)(2,1)} %reshape.125), calls=%async_computation.4 | async-start | bytes 1572864 | tf_op jit(solution)/shard_map/all_to_all | solution.py:43
  256.4 17.7 %all-to-all-done.4 = bf16[32,96,128]{2,1,0:T(8,128)(2,1)} async-done(((bf16[32,96,128]{2,1,0:T(8,128)(2,1)}), bf16[32,96,128]{2,1,0:T(8,128)(2,1)}, u32[]{:S(2)}, u32[]{:S(2)}) %all-to-all-start.4) | async-done | bytes 786464 | tf_op jit(solution)/shard_map/all_to_all | solution.py:43
  280.7 28.6 %all_to_all.43 = bf16[32,96,128]{2,1,0:T(8,128)(2,1)} all-to-all(bf16[32,96,128]{2,1,0:T(8,128)(2,1)S(1)} %reshape.127), channel_id=1, replica_groups=mesh['section'=16,'expert'=32] {'expert'}, dimensions={0} | all-to-all | bytes 1572864 | tf_op jit(solution)/shard_map/all_to_all | solution.py:43
  311.0 1.9 collective-permute-start.2
  312.9 1.9 collective-permute-done.2
  316.5 5.7 %all-to-all-start.6 = ((bf16[32,96,128]{2,1,0:T(8,128)(2,1)}), bf16[32,96,128]{2,1,0:T(8,128)(2,1)}, u32[]{:S(2)}, u32[]{:S(2)}) async-start(bf16[32,96,128]{2,1,0:T(8,128)(2,1)} %reshape.129), calls=%async_computation.6 | async-start | bytes 1572864 | tf_op jit(solution)/shard_map/all_to_all | solution.py:43
  327.9 17.6 %all-to-all-done.6 = bf16[32,96,128]{2,1,0:T(8,128)(2,1)} async-done(((bf16[32,96,128]{2,1,0:T(8,128)(2,1)}), bf16[32,96,128]{2,1,0:T(8,128)(2,1)}, u32[]{:S(2)}, u32[]{:S(2)}) %all-to-all-start.6) | async-done | bytes 786464 | tf_op jit(solution)/shard_map/all_to_all | solution.py:43
  350.7 5.5 %all-to-all-start.7 = ((bf16[32,96,128]{2,1,0:T(8,128)(2,1)}), bf16[32,96,128]{2,1,0:T(8,128)(2,1)}, u32[]{:S(2)}, u32[]{:S(2)}) async-start(bf16[32,96,128]{2,1,0:T(8,128)(2,1)} %reshape.131), calls=%async_computation.7 | async-start | bytes 1572864 | tf_op jit(solution)/shard_map/all_to_all | solution.py:43
  356.3 2.0 fusion.44
  362.6 16.9 %all-to-all-done.7 = bf16[32,96,128]{2,1,0:T(8,128)(2,1)} async-done(((bf16[32,96,128]{2,1,0:T(8,128)(2,1)}), bf16[32,96,128]{2,1,0:T(8,128)(2,1)}, u32[]{:S(2)}, u32[]{:S(2)}) %all-to-all-start.7) | async-done | bytes 786464 | tf_op jit(solution)/shard_map/all_to_all | solution.py:43
  (162 shorter events, 69.9 us)
Async XLA Ops:
  0.6 129.0 %copy-start = (bf16[1,1,1024,384]{3,2,1,0:T(8,128)(2,1)S(1)}, bf16[1,1,1024,384]{3,2,1,0:T(8,128)(2,1)}, u32[]{:S(2)}) copy-start(bf16[1,1,1024,384]{3,2,1,0:T(8,128)(2,1)} %param.13) | copy-start | bytes 2359300
  8.3 3.7 copy-start.35
  11.8 2.4 copy-start.34
  11.9 3.1 copy-start.29
  166.5 5.6 %copy-start.16 = (bf16[4,32,1024]{2,1,0:T(8,128)(2,1)S(1)}, bf16[4,32,1024]{2,1,0:T(8,128)(2,1)}, u32[]{:S(2)}) copy-start(bf16[4,32,1024]{2,1,0:T(8,128)(2,1)} %param.10) | copy-start | bytes 786436
  168.2 3.8 %copy-start.27 = (bf16[32,1024]{1,0:T(8,128)(2,1)}, bf16[32,1024]{1,0:T(8,128)(2,1)S(1)}, u32[]{:S(2)}) copy-start(bf16[32,1024]{1,0:T(8,128)(2,1)S(1)} %fusion.2) | copy-start | bytes 196612
  168.2 3.8 collective-permute-start
  173.7 5.8 %copy-start.10 = (bf16[32,1,12,1024]{3,0,2,1:T(8,128)(2,1)S(1)}, bf16[32,1,12,1024]{3,0,2,1:T(8,128)(2,1)}, u32[]{:S(2)}) copy-start(bf16[32,1,12,1024]{3,0,2,1:T(8,128)(2,1)} %get-tuple-element.8) | copy-start | bytes 2359300
  173.7 29.0 %all-to-all-start.2 = ((bf16[32,96,128]{2,1,0:T(8,128)(2,1)}), bf16[32,96,128]{2,1,0:T(8,128)(2,1)}, u32[]{:S(2)}, u32[]{:S(2)}) async-start(bf16[32,96,128]{2,1,0:T(8,128)(2,1)} %reshape.121), calls=%async_computation.2 | async-start | bytes 1572864 | tf_op jit(solution)/shard_map/all_to_all | solution.py:43
  204.1 2.2 copy-start.4
  239.6 3.8 %copy-start.30 = (bf16[32,1024]{1,0:T(8,128)(2,1)}, bf16[32,1024]{1,0:T(8,128)(2,1)S(1)}, u32[]{:S(2)}) copy-start(bf16[32,1024]{1,0:T(8,128)(2,1)S(1)} %add_convert_fusion.7) | copy-start | bytes 196612
  239.6 3.8 collective-permute-start.1
  245.1 5.8 %copy-start.9 = (bf16[32,1,12,1024]{3,0,2,1:T(8,128)(2,1)S(1)}, bf16[32,1,12,1024]{3,0,2,1:T(8,128)(2,1)}, u32[]{:S(2)}) copy-start(bf16[32,1,12,1024]{3,0,2,1:T(8,128)(2,1)} %get-tuple-element.7) | copy-start | bytes 2359300
  245.1 29.0 %all-to-all-start.4 = ((bf16[32,96,128]{2,1,0:T(8,128)(2,1)}), bf16[32,96,128]{2,1,0:T(8,128)(2,1)}, u32[]{:S(2)}, u32[]{:S(2)}) async-start(bf16[32,96,128]{2,1,0:T(8,128)(2,1)} %reshape.125), calls=%async_computation.4 | async-start | bytes 1572864 | tf_op jit(solution)/shard_map/all_to_all | solution.py:43
  275.5 2.2 copy-start.6
  311.0 3.8 %copy-start.32 = (bf16[32,1024]{1,0:T(8,128)(2,1)}, bf16[32,1024]{1,0:T(8,128)(2,1)S(1)}, u32[]{:S(2)}) copy-start(bf16[32,1024]{1,0:T(8,128)(2,1)S(1)} %add_convert_fusion.6) | copy-start | bytes 196612
  311.0 3.8 collective-permute-start.2
  316.5 5.8 %copy-start.8 = (bf16[32,1,12,1024]{3,0,2,1:T(8,128)(2,1)S(1)}, bf16[32,1,12,1024]{3,0,2,1:T(8,128)(2,1)}, u32[]{:S(2)}) copy-start(bf16[32,1,12,1024]{3,0,2,1:T(8,128)(2,1)} %get-tuple-element.6) | copy-start | bytes 2359300
  316.5 29.0 %all-to-all-start.6 = ((bf16[32,96,128]{2,1,0:T(8,128)(2,1)}), bf16[32,96,128]{2,1,0:T(8,128)(2,1)}, u32[]{:S(2)}, u32[]{:S(2)}) async-start(bf16[32,96,128]{2,1,0:T(8,128)(2,1)} %reshape.129), calls=%async_computation.6 | async-start | bytes 1572864 | tf_op jit(solution)/shard_map/all_to_all | solution.py:43
  349.5 6.8 %copy-start.3 = (bf16[384,1024]{1,0:T(8,128)(2,1)S(1)}, bf16[384,1024]{1,0:T(8,128)(2,1)}, u32[]{:S(2)}) copy-start(bf16[384,1024]{1,0:T(8,128)(2,1)} %reshape_squeeze.15) | copy-start | bytes 2359300
  350.7 28.8 %all-to-all-start.7 = ((bf16[32,96,128]{2,1,0:T(8,128)(2,1)}), bf16[32,96,128]{2,1,0:T(8,128)(2,1)}, u32[]{:S(2)}, u32[]{:S(2)}) async-start(bf16[32,96,128]{2,1,0:T(8,128)(2,1)} %reshape.131), calls=%async_computation.7 | async-start | bytes 1572864 | tf_op jit(solution)/shard_map/all_to_all | solution.py:43
  362.6 18.6 %copy-start.28 = (bf16[32,1024]{1,0:T(8,128)(2,1)S(1)}, bf16[32,1024]{1,0:T(8,128)(2,1)}, u32[]{:S(2)}) copy-start(bf16[32,1024]{1,0:T(8,128)(2,1)} %copy-done.27) | copy-start | bytes 196612
  362.6 18.6 %copy-start.31 = (bf16[32,1024]{1,0:T(8,128)(2,1)S(1)}, bf16[32,1024]{1,0:T(8,128)(2,1)}, u32[]{:S(2)}) copy-start(bf16[32,1024]{1,0:T(8,128)(2,1)} %copy-done.30) | copy-start | bytes 196612
  362.6 18.6 %copy-start.33 = (bf16[32,1024]{1,0:T(8,128)(2,1)S(1)}, bf16[32,1024]{1,0:T(8,128)(2,1)}, u32[]{:S(2)}) copy-start(bf16[32,1024]{1,0:T(8,128)(2,1)} %copy-done.32) | copy-start | bytes 196612
  (19 other events, 28.5 us)

commit v5 on v3

--- a/solution.py
+++ b/solution.py
@@ -43,7 +43,7 @@
     return lax.all_to_all(block, "expert", split_axis=0, concat_axis=0, tiled=True)
 
 
-def expert_backward(gate_pre, up_pre, sigma, grad_rows, gate_weight, up_weight, down_weight):
+def expert_backward(gate_pre, up_pre, sigma, grad_rows, both_weight, down_weight):
     contract = (((1,), (1,)), ((), ()))
     active = gate_pre * sigma
     hidden_grad = lax.dot_general(
@@ -53,10 +53,8 @@
         jnp.bfloat16
     )
     up_grad = (hidden_grad * active).astype(jnp.bfloat16)
-    row_grad = lax.dot_general(gate_grad, gate_weight, contract, preferred_element_type=jnp.float32)
-    row_grad = row_grad + lax.dot_general(
-        up_grad, up_weight, contract, preferred_element_type=jnp.float32
-    )
+    both_grad = jnp.concatenate([gate_grad, up_grad], axis=1)
+    row_grad = lax.dot_general(both_grad, both_weight, contract, preferred_element_type=jnp.float32)
     return row_grad.astype(jnp.bfloat16)
 
 
@@ -69,6 +67,8 @@
     gate_weight = w_gate[0, 0]
     up_weight = w_up[0, 0]
     down_weight = w_down[0, 0]
+    both_weight = jnp.concatenate([gate_weight, up_weight], axis=1)
+    hidden_units = gate_weight.shape[1]
     is_last = lax.axis_index("section") == lax.axis_size("section") - 1
     select_all, weight_all = slot_tables(expert_ids[0], probs[0], experts, slot_rows)
     rows_contract = (((0,), (0,)), ((), ()))
@@ -96,12 +96,12 @@
     down_sum = jnp.zeros((down_weight.shape[0], width), jnp.float32)
     for moment in range(ticks_here):
         received_input = unpack(received[:, moment], width)
-        gate_pre = jnp.dot(received_input, gate_weight, preferred_element_type=jnp.float32)
-        up_pre = jnp.dot(received_input, up_weight, preferred_element_type=jnp.float32)
+        both_pre = jnp.dot(received_input, both_weight, preferred_element_type=jnp.float32)
+        gate_pre, up_pre = both_pre[:, :hidden_units], both_pre[:, hidden_units:]
         sigma = jax.nn.sigmoid(gate_pre)
         hidden = (gate_pre * sigma * up_pre).astype(jnp.bfloat16)
         row_grad = expert_backward(
-            gate_pre, up_pre, sigma, flat_grad, gate_weight, up_weight, down_weight
+            gate_pre, up_pre, sigma, flat_grad, both_weight, down_weight
         )
         returned = unpack(exchange(pack(row_grad, experts)), width)
         gathered = lax.dot_general(

time: 377 us -> 363 us (0.963)
  the two profiles are of different devices: /device:TPU:18 before, /device:TPU:26 now
where the time goes in v5:
time: 363 us; the launch traced here: 362 us
  blocking collectives  189 us (52%)
  waiting for transfers between devices  75.9 us (21%)
  matrix products  33.8 us (9%)
  local copies, waits for them, and re-layouts  29.3 us (8%)
  starting transfers between devices  28.5 us (8%)
  other arithmetic  4.15 us (1%)
    all_to_all x4, blocking collectives, exchange(): lax.all_to_all(block, 'expert', split_axis=0, concat_axis=0, tiled=True)  189 us
    all_to_all x4, waiting for transfers between devices, exchange(): lax.all_to_all(block, 'expert', split_axis=0, concat_axis=0, tiled=True)  70.2 us
    all_to_all x4, starting transfers between devices, exchange(): lax.all_to_all(block, 'expert', split_axis=0, concat_axis=0, tiled=True)  22.7 us
    dot_general x4, matrix products, per_device(): jnp.dot(received_input, both_weight, preferred_element_type=jnp.float32)  13.2 us
    reshape x2, local copies, waits for them, and re-layouts, per_device(): send = picked.reshape(count, experts, -1, LANES).transpose(1, 0, 2, 3)  9.84 us
  transfers between devices with their start and end apart: 7, of which 7 were waited for; matrix products, arithmetic and copies ran while one was open for 5% of the time, Pallas kernels for 0%

profile of v5, /device:TPU:26, one launch (start us, length us, event | category | flops | bytes accessed | tf_op | source)
XLA Modules:
  0.0 362.0 jit_solution(5670089844988019056)
XLA Ops:
  2.6 2.3 reduce-window.6
  6.5 3.1 multiply_convert_fusion
  9.6 7.1 %reshape.96 = bf16[5,32,96,128]{3,2,1,0:T(8,128)(2,1)} reshape(bf16[5,384,1024]{2,1,0:T(8,128)(2,1)} %multiply_convert_fusion) | data formatting | bytes 7864320 | tf_op jit(solution)/shard_map/reshape | solution.py:91
  16.6 2.8 copy.43
  19.4 103.1 %all_to_all.40 = bf16[32,480,128]{2,1,0:T(8,128)(2,1)S(1)} all-to-all(bf16[32,480,128]{2,1,0:T(8,128)(2,1)S(1)} %bitcast.128), channel_id=1, replica_groups=mesh['section'=16,'expert'=32] {'expert'}, dimensions={0} | all-to-all | bytes 7864320 | tf_op jit(solution)/shard_map/all_to_all | solution.py:43
  126.1 2.5 fusion.62
  131.5 26.9 %all_to_all.41 = bf16[32,96,128]{2,1,0:T(8,128)(2,1)S(1)} all-to-all(bf16[32,96,128]{2,1,0:T(8,128)(2,1)S(1)} %reshape.99), channel_id=1, replica_groups=mesh['section'=16,'expert'=32] {'expert'}, dimensions={0} | all-to-all | bytes 1572864 | tf_op jit(solution)/shard_map/all_to_all | solution.py:43
  164.5 5.6 %all-to-all-start.2 = ((bf16[32,96,128]{2,1,0:T(8,128)(2,1)}), bf16[32,96,128]{2,1,0:T(8,128)(2,1)S(1)}, u32[]{:S(2)}, u32[]{:S(2)}) async-start(bf16[32,96,128]{2,1,0:T(8,128)(2,1)} %reshape.101), calls=%async_computation.2 | async-start | bytes 1572864 | tf_op jit(solution)/shard_map/all_to_all | solution.py:43
  171.3 3.7 %fusion.61 = f32[384,768]{0,1:T(8,128)} fusion(bf16[384,1024]{1,0:T(8,128)(2,1)} %reshape_squeeze.17, bf16[1024,384]{1,0:T(8,128)(2,1)} %bitcast.135, bf16[1024,384]{1,0:T(8,128)(2,1)} %bitcast.143), kind=kOutput, calls=%fused_computation.106 | convolution fusion | flops 607125504 | bytes 3538944 | tf_op jit(solution)/shard_map/dot_general | solution.py:99
  174.9 17.1 %all-to-all-done.2 = bf16[32,96,128]{2,1,0:T(8,128)(2,1)S(1)} async-done(((bf16[32,96,128]{2,1,0:T(8,128)(2,1)}), bf16[32,96,128]{2,1,0:T(8,128)(2,1)S(1)}, u32[]{:S(2)}, u32[]{:S(2)}) %all-to-all-start.2) | async-done | bytes 786464 | tf_op jit(solution)/shard_map/all_to_all | solution.py:43
  192.4 2.2 multiply_convert_fusion.13
  195.9 29.6 %all_to_all.42 = bf16[32,96,128]{2,1,0:T(8,128)(2,1)S(1)} all-to-all(bf16[32,96,128]{2,1,0:T(8,128)(2,1)S(1)} %reshape.103), channel_id=1, replica_groups=mesh['section'=16,'expert'=32] {'expert'}, dimensions={0} | all-to-all | bytes 1572864 | tf_op jit(solution)/shard_map/all_to_all | solution.py:43
  231.6 5.6 %all-to-all-start.4 = ((bf16[32,96,128]{2,1,0:T(8,128)(2,1)}), bf16[32,96,128]{2,1,0:T(8,128)(2,1)S(1)}, u32[]{:S(2)}, u32[]{:S(2)}) async-start(bf16[32,96,128]{2,1,0:T(8,128)(2,1)} %reshape.105), calls=%async_computation.4 | async-start | bytes 1572864 | tf_op jit(solution)/shard_map/all_to_all | solution.py:43
  238.4 3.7 %fusion.60 = f32[384,768]{0,1:T(8,128)} fusion(bf16[384,1024]{1,0:T(8,128)(2,1)} %reshape_squeeze.18, bf16[1024,384]{1,0:T(8,128)(2,1)} %bitcast.136, bf16[1024,384]{1,0:T(8,128)(2,1)} %bitcast.144), kind=kOutput, calls=%fused_computation.105 | convolution fusion | flops 607125504 | bytes 3538944 | tf_op jit(solution)/shard_map/dot_general | solution.py:99
  242.1 17.4 %all-to-all-done.4 = bf16[32,96,128]{2,1,0:T(8,128)(2,1)S(1)} async-done(((bf16[32,96,128]{2,1,0:T(8,128)(2,1)}), bf16[32,96,128]{2,1,0:T(8,128)(2,1)S(1)}, u32[]{:S(2)}, u32[]{:S(2)}) %all-to-all-start.4) | async-done | bytes 786464 | tf_op jit(solution)/shard_map/all_to_all | solution.py:43
  259.8 2.2 multiply_convert_fusion.11
  263.3 29.4 %all_to_all.43 = bf16[32,96,128]{2,1,0:T(8,128)(2,1)S(1)} all-to-all(bf16[32,96,128]{2,1,0:T(8,128)(2,1)S(1)} %reshape.107), channel_id=1, replica_groups=mesh['section'=16,'expert'=32] {'expert'}, dimensions={0} | all-to-all | bytes 1572864 | tf_op jit(solution)/shard_map/all_to_all | solution.py:43
  298.7 5.6 %all-to-all-start.6 = ((bf16[32,96,128]{2,1,0:T(8,128)(2,1)}), bf16[32,96,128]{2,1,0:T(8,128)(2,1)S(1)}, u32[]{:S(2)}, u32[]{:S(2)}) async-start(bf16[32,96,128]{2,1,0:T(8,128)(2,1)} %reshape.109), calls=%async_computation.6 | async-start | bytes 1572864 | tf_op jit(solution)/shard_map/all_to_all | solution.py:43
  304.6 3.4 fusion.59
  308.1 18.5 %all-to-all-done.6 = bf16[32,96,128]{2,1,0:T(8,128)(2,1)S(1)} async-done(((bf16[32,96,128]{2,1,0:T(8,128)(2,1)}), bf16[32,96,128]{2,1,0:T(8,128)(2,1)S(1)}, u32[]{:S(2)}, u32[]{:S(2)}) %all-to-all-start.6) | async-done | bytes 786464 | tf_op jit(solution)/shard_map/all_to_all | solution.py:43
  326.9 2.0 multiply_convert_fusion.9
  331.1 6.0 %all-to-all-start.7 = ((bf16[32,96,128]{2,1,0:T(8,128)(2,1)}), bf16[32,96,128]{2,1,0:T(8,128)(2,1)S(1)}, u32[]{:S(2)}, u32[]{:S(2)}) async-start(bf16[32,96,128]{2,1,0:T(8,128)(2,1)} %reshape.111), calls=%async_computation.7 | async-start | bytes 1572864 | tf_op jit(solution)/shard_map/all_to_all | solution.py:43
  337.1 2.0 fusion.30
  343.4 17.2 %all-to-all-done.7 = bf16[32,96,128]{2,1,0:T(8,128)(2,1)S(1)} async-done(((bf16[32,96,128]{2,1,0:T(8,128)(2,1)}), bf16[32,96,128]{2,1,0:T(8,128)(2,1)S(1)}, u32[]{:S(2)}, u32[]{:S(2)}) %all-to-all-start.7) | async-done | bytes 786464 | tf_op jit(solution)/shard_map/all_to_all | solution.py:43
  (122 shorter events, 41.7 us)
Async XLA Ops:
  0.6 127.9 %copy-start = (bf16[1,1,384,1024]{3,2,1,0:T(8,128)(2,1)S(1)}, bf16[1,1,384,1024]{3,2,1,0:T(8,128)(2,1)}, u32[]{:S(2)}) copy-start(bf16[1,1,384,1024]{3,2,1,0:T(8,128)(2,1)} %param.15) | copy-start | bytes 2359300
  0.6 5.8 %copy-start.3 = (bf16[4,32,1024]{2,1,0:T(8,128)(2,1)S(1)}, bf16[4,32,1024]{2,1,0:T(8,128)(2,1)}, u32[]{:S(2)}) copy-start(bf16[4,32,1024]{2,1,0:T(8,128)(2,1)} %param.10) | copy-start | bytes 786436
  0.7 5.8 %copy-start.18 = (bf16[1,32,1024]{2,1,0:T(8,128)(2,1)S(1)}, bf16[1,32,1024]{2,1,0:T(8,128)(2,1)}, u32[]{:S(2)}) copy-start(bf16[1,32,1024]{2,1,0:T(8,128)(2,1)} %param.9) | copy-start | bytes 196612
  0.7 5.8 %copy-start.13 = (bf16[1,4,32,1024]{3,2,1,0:T(8,128)(2,1)S(1)}, bf16[1,4,32,1024]{3,2,1,0:T(8,128)(2,1)}, u32[]{:S(2)}) copy-start(bf16[1,4,32,1024]{3,2,1,0:T(8,128)(2,1)} %param.8) | copy-start | bytes 786436
  126.1 2.5 copy-start.4
  159.0 3.8 %copy-start.11 = (bf16[32,1024]{1,0:T(8,128)(2,1)}, bf16[32,1024]{1,0:T(8,128)(2,1)S(1)}, u32[]{:S(2)}) copy-start(bf16[32,1024]{1,0:T(8,128)(2,1)S(1)} %fusion.2) | copy-start | bytes 196612
  159.0 3.8 %collective-permute-start = (bf16[32,1024]{1,0:T(8,128)(2,1)S(1)}, bf16[32,1024]{1,0:T(8,128)(2,1)S(1)}, u32[]{:S(2)}, u32[]{:S(2)}) collective-permute-start(bf16[32,1024]{1,0:T(8,128)(2,1)S(1)} %fusion.2), channel_id=1, source_target_pairs={{32,0},{64,32},{96,64},{128,96},{160,128},{192,160},{224,192},{256... | collective-permute-start | bytes 196616 | tf_op jit(solution)/shard_map/ppermute | solution.py:13
  163.2 6.8 %copy-start.2 = (bf16[32,1,96,128]{3,2,1,0:T(8,128)(2,1)S(1)}, bf16[32,1,96,128]{3,2,1,0:T(8,128)(2,1)}, u32[]{:S(2)}) copy-start(bf16[32,1,96,128]{3,2,1,0:T(8,128)(2,1)} %get-tuple-element.7) | copy-start | bytes 2359300
  164.5 27.6 %all-to-all-start.2 = ((bf16[32,96,128]{2,1,0:T(8,128)(2,1)}), bf16[32,96,128]{2,1,0:T(8,128)(2,1)S(1)}, u32[]{:S(2)}, u32[]{:S(2)}) async-start(bf16[32,96,128]{2,1,0:T(8,128)(2,1)} %reshape.101), calls=%async_computation.2 | async-start | bytes 1572864 | tf_op jit(solution)/shard_map/all_to_all | solution.py:43
  192.4 2.3 copy-start.6
  192.4 2.3 copy-start.20
  226.1 3.8 %copy-start.14 = (bf16[32,1024]{1,0:T(8,128)(2,1)}, bf16[32,1024]{1,0:T(8,128)(2,1)S(1)}, u32[]{:S(2)}) copy-start(bf16[32,1024]{1,0:T(8,128)(2,1)S(1)} %add_convert_fusion.3) | copy-start | bytes 196612
  226.1 3.8 %collective-permute-start.1 = (bf16[32,1024]{1,0:T(8,128)(2,1)S(1)}, bf16[32,1024]{1,0:T(8,128)(2,1)S(1)}, u32[]{:S(2)}, u32[]{:S(2)}) collective-permute-start(bf16[32,1024]{1,0:T(8,128)(2,1)S(1)} %add_convert_fusion.3), channel_id=1, source_target_pairs={{32,0},{64,32},{96,64},{128,96},{160,128},{192,160},{224,192},{256... | collective-permute-start | bytes 196616 | tf_op jit(solution)/shard_map/ppermute | solution.py:13
  230.4 6.8 %copy-start.1 = (bf16[32,1,96,128]{3,2,1,0:T(8,128)(2,1)S(1)}, bf16[32,1,96,128]{3,2,1,0:T(8,128)(2,1)}, u32[]{:S(2)}) copy-start(bf16[32,1,96,128]{3,2,1,0:T(8,128)(2,1)} %get-tuple-element.6) | copy-start | bytes 2359300
  231.6 27.9 %all-to-all-start.4 = ((bf16[32,96,128]{2,1,0:T(8,128)(2,1)}), bf16[32,96,128]{2,1,0:T(8,128)(2,1)S(1)}, u32[]{:S(2)}, u32[]{:S(2)}) async-start(bf16[32,96,128]{2,1,0:T(8,128)(2,1)} %reshape.105), calls=%async_computation.4 | async-start | bytes 1572864 | tf_op jit(solution)/shard_map/all_to_all | solution.py:43
  259.8 2.3 copy-start.8
  293.3 5.5 %copy-start.16 = (bf16[32,1024]{1,0:T(8,128)(2,1)}, bf16[32,1024]{1,0:T(8,128)(2,1)S(1)}, u32[]{:S(2)}) copy-start(bf16[32,1024]{1,0:T(8,128)(2,1)S(1)} %add_convert_fusion.2) | copy-start | bytes 196612
  293.3 3.8 %collective-permute-start.2 = (bf16[32,1024]{1,0:T(8,128)(2,1)S(1)}, bf16[32,1024]{1,0:T(8,128)(2,1)S(1)}, u32[]{:S(2)}, u32[]{:S(2)}) collective-permute-start(bf16[32,1024]{1,0:T(8,128)(2,1)S(1)} %add_convert_fusion.2), channel_id=1, source_target_pairs={{32,0},{64,32},{96,64},{128,96},{160,128},{192,160},{224,192},{256... | collective-permute-start | bytes 196616 | tf_op jit(solution)/shard_map/ppermute | solution.py:13
  298.7 27.9 %all-to-all-start.6 = ((bf16[32,96,128]{2,1,0:T(8,128)(2,1)}), bf16[32,96,128]{2,1,0:T(8,128)(2,1)S(1)}, u32[]{:S(2)}, u32[]{:S(2)}) async-start(bf16[32,96,128]{2,1,0:T(8,128)(2,1)} %reshape.109), calls=%async_computation.6 | async-start | bytes 1572864 | tf_op jit(solution)/shard_map/all_to_all | solution.py:43
  329.9 7.2 %copy-start.5 = (bf16[384,1024]{1,0:T(8,128)(2,1)S(1)}, bf16[384,1024]{1,0:T(8,128)(2,1)}, u32[]{:S(2)}) copy-start(bf16[384,1024]{1,0:T(8,128)(2,1)} %reshape_squeeze.15) | copy-start | bytes 2359300
  331.1 29.6 %all-to-all-start.7 = ((bf16[32,96,128]{2,1,0:T(8,128)(2,1)}), bf16[32,96,128]{2,1,0:T(8,128)(2,1)S(1)}, u32[]{:S(2)}, u32[]{:S(2)}) async-start(bf16[32,96,128]{2,1,0:T(8,128)(2,1)} %reshape.111), calls=%async_computation.7 | async-start | bytes 1572864 | tf_op jit(solution)/shard_map/all_to_all | solution.py:43
  343.4 17.8 %copy-start.12 = (bf16[32,1024]{1,0:T(8,128)(2,1)S(1)}, bf16[32,1024]{1,0:T(8,128)(2,1)}, u32[]{:S(2)}) copy-start(bf16[32,1024]{1,0:T(8,128)(2,1)} %copy-done.11) | copy-start | bytes 196612
  343.4 17.8 %copy-start.15 = (bf16[32,1024]{1,0:T(8,128)(2,1)S(1)}, bf16[32,1024]{1,0:T(8,128)(2,1)}, u32[]{:S(2)}) copy-start(bf16[32,1024]{1,0:T(8,128)(2,1)} %copy-done.14) | copy-start | bytes 196612
  343.4 17.8 %copy-start.17 = (bf16[32,1024]{1,0:T(8,128)(2,1)S(1)}, bf16[32,1024]{1,0:T(8,128)(2,1)}, u32[]{:S(2)}) copy-start(bf16[32,1024]{1,0:T(8,128)(2,1)} %copy-done.16) | copy-start | bytes 196612
  (13 other events, 23.3 us)

commit v6 on v5

--- a/solution.py
+++ b/solution.py
@@ -2,6 +2,7 @@
 import jax.numpy as jnp
 from jax import lax
 from jax.sharding import PartitionSpec as P
+
 
 TOPK = 8
 LANES = 128
@@ -109,9 +110,8 @@
         )
         result = (incoming.astype(jnp.float32) + gathered).astype(jnp.bfloat16)
         results.append(result)
-        down_sum = down_sum + lax.dot_general(
-            hidden, flat_grad, rows_contract, preferred_element_type=jnp.float32
-        )
+        term = lax.dot_general(hidden, flat_grad, rows_contract, preferred_element_type=jnp.float32)
+        down_sum = down_sum + term
         if moment + 1 < ticks_here:
             arriving = passed_along(result, "section", -1)
             incoming = jnp.where(is_last, loss_grad[moment + 1], arriving)

time: 363 us -> 363 us (level)
  the two profiles are of different devices: /device:TPU:26 before, /device:TPU:18 now
where the time goes in v6:
time: 363 us; the launch traced here: 362 us
  blocking collectives  187 us (52%)
  waiting for transfers between devices  78.5 us (22%)
  matrix products  33.8 us (9%)
  local copies, waits for them, and re-layouts  29.3 us (8%)
  starting transfers between devices  28 us (8%)
  other arithmetic  4.15 us (1%)
    all_to_all x4, blocking collectives, exchange(): lax.all_to_all(block, 'expert', split_axis=0, concat_axis=0, tiled=True)  187 us
    all_to_all x4, waiting for transfers between devices, exchange(): lax.all_to_all(block, 'expert', split_axis=0, concat_axis=0, tiled=True)  72.8 us
    all_to_all x4, starting transfers between devices, exchange(): lax.all_to_all(block, 'expert', split_axis=0, concat_axis=0, tiled=True)  22.2 us
    dot_general x4, matrix products, per_device(): jnp.dot(received_input, both_weight, preferred_element_type=jnp.float32)  13.2 us
    reshape x2, local copies, waits for them, and re-layouts, per_device(): send = picked.reshape(count, experts, -1, LANES).transpose(1, 0, 2, 3)  9.84 us
  transfers between devices with their start and end apart: 7, of which 7 were waited for; matrix products, arithmetic and copies ran while one was open for 5% of the time, Pallas kernels for 0%

profile of v6, /device:TPU:18, one launch (start us, length us, event | category | flops | bytes accessed | tf_op | source)
XLA Modules:
  0.0 362.0 jit_solution(5670089844988019056)
XLA Ops:
  2.6 2.3 reduce-window.6
  6.5 3.1 multiply_convert_fusion
  9.6 7.1 %reshape.96 = bf16[5,32,96,128]{3,2,1,0:T(8,128)(2,1)} reshape(bf16[5,384,1024]{2,1,0:T(8,128)(2,1)} %multiply_convert_fusion) | data formatting | bytes 7864320 | tf_op jit(solution)/shard_map/reshape | solution.py:92
  16.6 2.8 copy.43
  19.4 103.1 %all_to_all.40 = bf16[32,480,128]{2,1,0:T(8,128)(2,1)S(1)} all-to-all(bf16[32,480,128]{2,1,0:T(8,128)(2,1)S(1)} %bitcast.128), channel_id=1, replica_groups=mesh['section'=16,'expert'=32] {'expert'}, dimensions={0} | all-to-all | bytes 7864320 | tf_op jit(solution)/shard_map/all_to_all | solution.py:44
  126.1 2.5 fusion.62
  131.5 26.9 %all_to_all.41 = bf16[32,96,128]{2,1,0:T(8,128)(2,1)S(1)} all-to-all(bf16[32,96,128]{2,1,0:T(8,128)(2,1)S(1)} %reshape.99), channel_id=1, replica_groups=mesh['section'=16,'expert'=32] {'expert'}, dimensions={0} | all-to-all | bytes 1572864 | tf_op jit(solution)/shard_map/all_to_all | solution.py:44
  164.5 5.6 %all-to-all-start.2 = ((bf16[32,96,128]{2,1,0:T(8,128)(2,1)}), bf16[32,96,128]{2,1,0:T(8,128)(2,1)S(1)}, u32[]{:S(2)}, u32[]{:S(2)}) async-start(bf16[32,96,128]{2,1,0:T(8,128)(2,1)} %reshape.101), calls=%async_computation.2 | async-start | bytes 1572864 | tf_op jit(solution)/shard_map/all_to_all | solution.py:44
  171.3 3.6 %fusion.61 = f32[384,768]{0,1:T(8,128)} fusion(bf16[384,1024]{1,0:T(8,128)(2,1)} %reshape_squeeze.17, bf16[1024,384]{1,0:T(8,128)(2,1)} %bitcast.135, bf16[1024,384]{1,0:T(8,128)(2,1)} %bitcast.143), kind=kOutput, calls=%fused_computation.106 | convolution fusion | flops 607125504 | bytes 3538944 | tf_op jit(solution)/shard_map/dot_general | solution.py:100
  175.0 18.3 %all-to-all-done.2 = bf16[32,96,128]{2,1,0:T(8,128)(2,1)S(1)} async-done(((bf16[32,96,128]{2,1,0:T(8,128)(2,1)}), bf16[32,96,128]{2,1,0:T(8,128)(2,1)S(1)}, u32[]{:S(2)}, u32[]{:S(2)}) %all-to-all-start.2) | async-done | bytes 786464 | tf_op jit(solution)/shard_map/all_to_all | solution.py:44
  193.6 2.2 multiply_convert_fusion.13
  197.1 28.5 %all_to_all.42 = bf16[32,96,128]{2,1,0:T(8,128)(2,1)S(1)} all-to-all(bf16[32,96,128]{2,1,0:T(8,128)(2,1)S(1)} %reshape.103), channel_id=1, replica_groups=mesh['section'=16,'expert'=32] {'expert'}, dimensions={0} | all-to-all | bytes 1572864 | tf_op jit(solution)/shard_map/all_to_all | solution.py:44
  231.6 5.6 %all-to-all-start.4 = ((bf16[32,96,128]{2,1,0:T(8,128)(2,1)}), bf16[32,96,128]{2,1,0:T(8,128)(2,1)S(1)}, u32[]{:S(2)}, u32[]{:S(2)}) async-start(bf16[32,96,128]{2,1,0:T(8,128)(2,1)} %reshape.105), calls=%async_computation.4 | async-start | bytes 1572864 | tf_op jit(solution)/shard_map/all_to_all | solution.py:44
  238.4 3.7 %fusion.60 = f32[384,768]{0,1:T(8,128)} fusion(bf16[384,1024]{1,0:T(8,128)(2,1)} %reshape_squeeze.18, bf16[1024,384]{1,0:T(8,128)(2,1)} %bitcast.136, bf16[1024,384]{1,0:T(8,128)(2,1)} %bitcast.144), kind=kOutput, calls=%fused_computation.105 | convolution fusion | flops 607125504 | bytes 3538944 | tf_op jit(solution)/shard_map/dot_general | solution.py:100
  242.1 18.3 %all-to-all-done.4 = bf16[32,96,128]{2,1,0:T(8,128)(2,1)S(1)} async-done(((bf16[32,96,128]{2,1,0:T(8,128)(2,1)}), bf16[32,96,128]{2,1,0:T(8,128)(2,1)S(1)}, u32[]{:S(2)}, u32[]{:S(2)}) %all-to-all-start.4) | async-done | bytes 786464 | tf_op jit(solution)/shard_map/all_to_all | solution.py:44
  260.7 2.2 multiply_convert_fusion.11
  264.2 28.5 %all_to_all.43 = bf16[32,96,128]{2,1,0:T(8,128)(2,1)S(1)} all-to-all(bf16[32,96,128]{2,1,0:T(8,128)(2,1)S(1)} %reshape.107), channel_id=1, replica_groups=mesh['section'=16,'expert'=32] {'expert'}, dimensions={0} | all-to-all | bytes 1572864 | tf_op jit(solution)/shard_map/all_to_all | solution.py:44
  298.7 5.6 %all-to-all-start.6 = ((bf16[32,96,128]{2,1,0:T(8,128)(2,1)}), bf16[32,96,128]{2,1,0:T(8,128)(2,1)S(1)}, u32[]{:S(2)}, u32[]{:S(2)}) async-start(bf16[32,96,128]{2,1,0:T(8,128)(2,1)} %reshape.109), calls=%async_computation.6 | async-start | bytes 1572864 | tf_op jit(solution)/shard_map/all_to_all | solution.py:44
  304.7 3.4 fusion.59
  308.1 19.4 %all-to-all-done.6 = bf16[32,96,128]{2,1,0:T(8,128)(2,1)S(1)} async-done(((bf16[32,96,128]{2,1,0:T(8,128)(2,1)}), bf16[32,96,128]{2,1,0:T(8,128)(2,1)S(1)}, u32[]{:S(2)}, u32[]{:S(2)}) %all-to-all-start.6) | async-done | bytes 786464 | tf_op jit(solution)/shard_map/all_to_all | solution.py:44
  327.8 2.0 multiply_convert_fusion.9
  332.0 5.5 %all-to-all-start.7 = ((bf16[32,96,128]{2,1,0:T(8,128)(2,1)}), bf16[32,96,128]{2,1,0:T(8,128)(2,1)S(1)}, u32[]{:S(2)}, u32[]{:S(2)}) async-start(bf16[32,96,128]{2,1,0:T(8,128)(2,1)} %reshape.111), calls=%async_computation.7 | async-start | bytes 1572864 | tf_op jit(solution)/shard_map/all_to_all | solution.py:44
  337.5 2.0 fusion.30
  343.8 16.9 %all-to-all-done.7 = bf16[32,96,128]{2,1,0:T(8,128)(2,1)S(1)} async-done(((bf16[32,96,128]{2,1,0:T(8,128)(2,1)}), bf16[32,96,128]{2,1,0:T(8,128)(2,1)S(1)}, u32[]{:S(2)}, u32[]{:S(2)}) %all-to-all-start.7) | async-done | bytes 786464 | tf_op jit(solution)/shard_map/all_to_all | solution.py:44
  (122 shorter events, 41.7 us)
Async XLA Ops:
  0.6 127.9 %copy-start = (bf16[1,1,384,1024]{3,2,1,0:T(8,128)(2,1)S(1)}, bf16[1,1,384,1024]{3,2,1,0:T(8,128)(2,1)}, u32[]{:S(2)}) copy-start(bf16[1,1,384,1024]{3,2,1,0:T(8,128)(2,1)} %param.15) | copy-start | bytes 2359300
  0.6 5.8 %copy-start.3 = (bf16[4,32,1024]{2,1,0:T(8,128)(2,1)S(1)}, bf16[4,32,1024]{2,1,0:T(8,128)(2,1)}, u32[]{:S(2)}) copy-start(bf16[4,32,1024]{2,1,0:T(8,128)(2,1)} %param.10) | copy-start | bytes 786436
  0.7 5.8 %copy-start.18 = (bf16[1,32,1024]{2,1,0:T(8,128)(2,1)S(1)}, bf16[1,32,1024]{2,1,0:T(8,128)(2,1)}, u32[]{:S(2)}) copy-start(bf16[1,32,1024]{2,1,0:T(8,128)(2,1)} %param.9) | copy-start | bytes 196612
  0.7 5.8 %copy-start.13 = (bf16[1,4,32,1024]{3,2,1,0:T(8,128)(2,1)S(1)}, bf16[1,4,32,1024]{3,2,1,0:T(8,128)(2,1)}, u32[]{:S(2)}) copy-start(bf16[1,4,32,1024]{3,2,1,0:T(8,128)(2,1)} %param.8) | copy-start | bytes 786436
  126.1 2.5 copy-start.4
  159.0 3.8 %copy-start.11 = (bf16[32,1024]{1,0:T(8,128)(2,1)}, bf16[32,1024]{1,0:T(8,128)(2,1)S(1)}, u32[]{:S(2)}) copy-start(bf16[32,1024]{1,0:T(8,128)(2,1)S(1)} %fusion.2) | copy-start | bytes 196612
  159.0 3.8 %collective-permute-start = (bf16[32,1024]{1,0:T(8,128)(2,1)S(1)}, bf16[32,1024]{1,0:T(8,128)(2,1)S(1)}, u32[]{:S(2)}, u32[]{:S(2)}) collective-permute-start(bf16[32,1024]{1,0:T(8,128)(2,1)S(1)} %fusion.2), channel_id=1, source_target_pairs={{32,0},{64,32},{96,64},{128,96},{160,128},{192,160},{224,192},{256... | collective-permute-start | bytes 196616 | tf_op jit(solution)/shard_map/ppermute | solution.py:14
  163.3 6.8 %copy-start.2 = (bf16[32,1,96,128]{3,2,1,0:T(8,128)(2,1)S(1)}, bf16[32,1,96,128]{3,2,1,0:T(8,128)(2,1)}, u32[]{:S(2)}) copy-start(bf16[32,1,96,128]{3,2,1,0:T(8,128)(2,1)} %get-tuple-element.7) | copy-start | bytes 2359300
  164.5 28.7 %all-to-all-start.2 = ((bf16[32,96,128]{2,1,0:T(8,128)(2,1)}), bf16[32,96,128]{2,1,0:T(8,128)(2,1)S(1)}, u32[]{:S(2)}, u32[]{:S(2)}) async-start(bf16[32,96,128]{2,1,0:T(8,128)(2,1)} %reshape.101), calls=%async_computation.2 | async-start | bytes 1572864 | tf_op jit(solution)/shard_map/all_to_all | solution.py:44
  226.1 3.8 %copy-start.14 = (bf16[32,1024]{1,0:T(8,128)(2,1)}, bf16[32,1024]{1,0:T(8,128)(2,1)S(1)}, u32[]{:S(2)}) copy-start(bf16[32,1024]{1,0:T(8,128)(2,1)S(1)} %add_convert_fusion.3) | copy-start | bytes 196612
  226.2 3.8 %collective-permute-start.1 = (bf16[32,1024]{1,0:T(8,128)(2,1)S(1)}, bf16[32,1024]{1,0:T(8,128)(2,1)S(1)}, u32[]{:S(2)}, u32[]{:S(2)}) collective-permute-start(bf16[32,1024]{1,0:T(8,128)(2,1)S(1)} %add_convert_fusion.3), channel_id=1, source_target_pairs={{32,0},{64,32},{96,64},{128,96},{160,128},{192,160},{224,192},{256... | collective-permute-start | bytes 196616 | tf_op jit(solution)/shard_map/ppermute | solution.py:14
  230.4 6.8 %copy-start.1 = (bf16[32,1,96,128]{3,2,1,0:T(8,128)(2,1)S(1)}, bf16[32,1,96,128]{3,2,1,0:T(8,128)(2,1)}, u32[]{:S(2)}) copy-start(bf16[32,1,96,128]{3,2,1,0:T(8,128)(2,1)} %get-tuple-element.6) | copy-start | bytes 2359300
  231.6 28.7 %all-to-all-start.4 = ((bf16[32,96,128]{2,1,0:T(8,128)(2,1)}), bf16[32,96,128]{2,1,0:T(8,128)(2,1)S(1)}, u32[]{:S(2)}, u32[]{:S(2)}) async-start(bf16[32,96,128]{2,1,0:T(8,128)(2,1)} %reshape.105), calls=%async_computation.4 | async-start | bytes 1572864 | tf_op jit(solution)/shard_map/all_to_all | solution.py:44
  260.7 2.3 copy-start.8
  260.7 2.3 copy-start.21
  260.7 2.3 copy-start.25
  293.3 5.5 %copy-start.16 = (bf16[32,1024]{1,0:T(8,128)(2,1)}, bf16[32,1024]{1,0:T(8,128)(2,1)S(1)}, u32[]{:S(2)}) copy-start(bf16[32,1024]{1,0:T(8,128)(2,1)S(1)} %add_convert_fusion.2) | copy-start | bytes 196612
  293.3 3.8 %collective-permute-start.2 = (bf16[32,1024]{1,0:T(8,128)(2,1)S(1)}, bf16[32,1024]{1,0:T(8,128)(2,1)S(1)}, u32[]{:S(2)}, u32[]{:S(2)}) collective-permute-start(bf16[32,1024]{1,0:T(8,128)(2,1)S(1)} %add_convert_fusion.2), channel_id=1, source_target_pairs={{32,0},{64,32},{96,64},{128,96},{160,128},{192,160},{224,192},{256... | collective-permute-start | bytes 196616 | tf_op jit(solution)/shard_map/ppermute | solution.py:14
  298.7 28.7 %all-to-all-start.6 = ((bf16[32,96,128]{2,1,0:T(8,128)(2,1)}), bf16[32,96,128]{2,1,0:T(8,128)(2,1)S(1)}, u32[]{:S(2)}, u32[]{:S(2)}) async-start(bf16[32,96,128]{2,1,0:T(8,128)(2,1)} %reshape.109), calls=%async_computation.6 | async-start | bytes 1572864 | tf_op jit(solution)/shard_map/all_to_all | solution.py:44
  330.7 6.7 %copy-start.5 = (bf16[384,1024]{1,0:T(8,128)(2,1)S(1)}, bf16[384,1024]{1,0:T(8,128)(2,1)}, u32[]{:S(2)}) copy-start(bf16[384,1024]{1,0:T(8,128)(2,1)} %reshape_squeeze.15) | copy-start | bytes 2359300
  332.0 28.7 %all-to-all-start.7 = ((bf16[32,96,128]{2,1,0:T(8,128)(2,1)}), bf16[32,96,128]{2,1,0:T(8,128)(2,1)S(1)}, u32[]{:S(2)}, u32[]{:S(2)}) async-start(bf16[32,96,128]{2,1,0:T(8,128)(2,1)} %reshape.111), calls=%async_computation.7 | async-start | bytes 1572864 | tf_op jit(solution)/shard_map/all_to_all | solution.py:44
  343.8 17.5 %copy-start.12 = (bf16[32,1024]{1,0:T(8,128)(2,1)S(1)}, bf16[32,1024]{1,0:T(8,128)(2,1)}, u32[]{:S(2)}) copy-start(bf16[32,1024]{1,0:T(8,128)(2,1)} %copy-done.11) | copy-start | bytes 196612
  343.8 17.5 %copy-start.15 = (bf16[32,1024]{1,0:T(8,128)(2,1)S(1)}, bf16[32,1024]{1,0:T(8,128)(2,1)}, u32[]{:S(2)}) copy-start(bf16[32,1024]{1,0:T(8,128)(2,1)} %copy-done.14) | copy-start | bytes 196612
  343.8 17.5 %copy-start.17 = (bf16[32,1024]{1,0:T(8,128)(2,1)S(1)}, bf16[32,1024]{1,0:T(8,128)(2,1)}, u32[]{:S(2)}) copy-start(bf16[32,1024]{1,0:T(8,128)(2,1)} %copy-done.16) | copy-start | bytes 196612
  (13 other events, 23.3 us)

commit v7 on v5

--- a/solution.py
+++ b/solution.py
@@ -17,7 +17,13 @@
     ticks_here, tokens_here, choices_here = expert_ids.shape
     onehot = (expert_ids[..., None] == jnp.arange(experts, dtype=jnp.int32)).astype(jnp.int32)
     pairs = onehot.reshape(ticks_here, tokens_here * choices_here, experts)
-    before = jnp.cumsum(pairs, axis=1) - pairs
+    count = tokens_here * choices_here
+    earlier = (
+        jnp.arange(count, dtype=jnp.int32)[None, :] < jnp.arange(count, dtype=jnp.int32)[:, None]
+    ).astype(jnp.bfloat16)
+    before = jnp.einsum(
+        "ij,tje->tie", earlier, pairs.astype(jnp.bfloat16), preferred_element_type=jnp.float32
+    ).astype(jnp.int32)
     position = jnp.sum(before * pairs, axis=2).reshape(ticks_here, tokens_here, choices_here)
     target = expert_ids * slot_rows + position
     slots = jnp.arange(experts * slot_rows, dtype=jnp.int32)

time: 363 us -> 362 us (level)
  no operation moved by 1% of the time
where the time goes in v7:
time: 362 us; the launch traced here: 360 us
  blocking collectives  189 us (52%)
  waiting for transfers between devices  75.9 us (21%)
  matrix products  34 us (9%)
  local copies, waits for them, and re-layouts  29.1 us (8%)
  starting transfers between devices  28.5 us (8%)
    all_to_all x4, blocking collectives, exchange(): lax.all_to_all(block, 'expert', split_axis=0, concat_axis=0, tiled=True)  189 us
    all_to_all x4, waiting for transfers between devices, exchange(): lax.all_to_all(block, 'expert', split_axis=0, concat_axis=0, tiled=True)  70.3 us
    all_to_all x4, starting transfers between devices, exchange(): lax.all_to_all(block, 'expert', split_axis=0, concat_axis=0, tiled=True)  22.7 us
    dot_general x4, matrix products, per_device(): jnp.dot(received_input, both_weight, preferred_element_type=jnp.float32)  13.2 us
    reshape x2, local copies, waits for them, and re-layouts, per_device(): send = picked.reshape(count, experts, -1, LANES).transpose(1, 0, 2, 3)  9.89 us
    dot_general x4, matrix products, expert_backward(): lax.dot_general(grad_rows, down_weight, contract, preferred_element_type=...  7.24 us
  transfers between devices with their start and end apart: 7, of which 7 were waited for; matrix products, arithmetic and copies ran while one was open for 5% of the time, Pallas kernels for 0%

profile of v7, /device:TPU:26, one launch (start us, length us, event | category | flops | bytes accessed | tf_op | source)
XLA Modules:
  0.0 360.4 jit_solution(143306870342182007)
XLA Ops:
  4.7 3.1 multiply_convert_fusion
  7.8 7.1 %reshape.84 = bf16[5,32,96,128]{3,2,1,0:T(8,128)(2,1)} reshape(bf16[5,384,1024]{2,1,0:T(8,128)(2,1)} %multiply_convert_fusion) | data formatting | bytes 7864320 | tf_op jit(solution)/shard_map/reshape | solution.py:97
  14.9 2.8 copy.35
  17.7 103.1 %all_to_all.40 = bf16[32,480,128]{2,1,0:T(8,128)(2,1)S(1)} all-to-all(bf16[32,480,128]{2,1,0:T(8,128)(2,1)S(1)} %bitcast.113), channel_id=1, replica_groups=mesh['section'=16,'expert'=32] {'expert'}, dimensions={0} | all-to-all | bytes 7864320 | tf_op jit(solution)/shard_map/all_to_all | solution.py:49
  120.8 2.0 fusion.63
  124.4 2.5 fusion.62
  129.9 26.9 %all_to_all.41 = bf16[32,96,128]{2,1,0:T(8,128)(2,1)S(1)} all-to-all(bf16[32,96,128]{2,1,0:T(8,128)(2,1)S(1)} %reshape.87), channel_id=1, replica_groups=mesh['section'=16,'expert'=32] {'expert'}, dimensions={0} | all-to-all | bytes 1572864 | tf_op jit(solution)/shard_map/all_to_all | solution.py:49
  162.8 5.6 %all-to-all-start.2 = ((bf16[32,96,128]{2,1,0:T(8,128)(2,1)}), bf16[32,96,128]{2,1,0:T(8,128)(2,1)S(1)}, u32[]{:S(2)}, u32[]{:S(2)}) async-start(bf16[32,96,128]{2,1,0:T(8,128)(2,1)} %reshape.89), calls=%async_computation.2 | async-start | bytes 1572864 | tf_op jit(solution)/shard_map/all_to_all | solution.py:49
  169.6 3.7 %fusion.61 = f32[384,768]{0,1:T(8,128)} fusion(bf16[384,1024]{1,0:T(8,128)(2,1)} %reshape_squeeze.17, bf16[1024,384]{1,0:T(8,128)(2,1)} %bitcast.120, bf16[1024,384]{1,0:T(8,128)(2,1)} %bitcast.128), kind=kOutput, calls=%fused_computation.105 | convolution fusion | flops 607125504 | bytes 3538944 | tf_op jit(solution)/shard_map/dot_general | solution.py:105
  173.3 17.1 %all-to-all-done.2 = bf16[32,96,128]{2,1,0:T(8,128)(2,1)S(1)} async-done(((bf16[32,96,128]{2,1,0:T(8,128)(2,1)}), bf16[32,96,128]{2,1,0:T(8,128)(2,1)S(1)}, u32[]{:S(2)}, u32[]{:S(2)}) %all-to-all-start.2) | async-done | bytes 786464 | tf_op jit(solution)/shard_map/all_to_all | solution.py:49
  190.8 2.2 multiply_convert_fusion.13
  194.2 29.6 %all_to_all.42 = bf16[32,96,128]{2,1,0:T(8,128)(2,1)S(1)} all-to-all(bf16[32,96,128]{2,1,0:T(8,128)(2,1)S(1)} %reshape.91), channel_id=1, replica_groups=mesh['section'=16,'expert'=32] {'expert'}, dimensions={0} | all-to-all | bytes 1572864 | tf_op jit(solution)/shard_map/all_to_all | solution.py:49
  230.0 5.6 %all-to-all-start.4 = ((bf16[32,96,128]{2,1,0:T(8,128)(2,1)}), bf16[32,96,128]{2,1,0:T(8,128)(2,1)S(1)}, u32[]{:S(2)}, u32[]{:S(2)}) async-start(bf16[32,96,128]{2,1,0:T(8,128)(2,1)} %reshape.93), calls=%async_computation.4 | async-start | bytes 1572864 | tf_op jit(solution)/shard_map/all_to_all | solution.py:49
  236.8 3.6 %fusion.60 = f32[384,768]{0,1:T(8,128)} fusion(bf16[384,1024]{1,0:T(8,128)(2,1)} %reshape_squeeze.18, bf16[1024,384]{1,0:T(8,128)(2,1)} %bitcast.121, bf16[1024,384]{1,0:T(8,128)(2,1)} %bitcast.129), kind=kOutput, calls=%fused_computation.104 | convolution fusion | flops 607125504 | bytes 3538944 | tf_op jit(solution)/shard_map/dot_general | solution.py:105
  240.4 17.4 %all-to-all-done.4 = bf16[32,96,128]{2,1,0:T(8,128)(2,1)S(1)} async-done(((bf16[32,96,128]{2,1,0:T(8,128)(2,1)}), bf16[32,96,128]{2,1,0:T(8,128)(2,1)S(1)}, u32[]{:S(2)}, u32[]{:S(2)}) %all-to-all-start.4) | async-done | bytes 786464 | tf_op jit(solution)/shard_map/all_to_all | solution.py:49
  258.2 2.2 multiply_convert_fusion.11
  261.6 29.4 %all_to_all.43 = bf16[32,96,128]{2,1,0:T(8,128)(2,1)S(1)} all-to-all(bf16[32,96,128]{2,1,0:T(8,128)(2,1)S(1)} %reshape.95), channel_id=1, replica_groups=mesh['section'=16,'expert'=32] {'expert'}, dimensions={0} | all-to-all | bytes 1572864 | tf_op jit(solution)/shard_map/all_to_all | solution.py:49
  297.1 5.6 %all-to-all-start.6 = ((bf16[32,96,128]{2,1,0:T(8,128)(2,1)}), bf16[32,96,128]{2,1,0:T(8,128)(2,1)S(1)}, u32[]{:S(2)}, u32[]{:S(2)}) async-start(bf16[32,96,128]{2,1,0:T(8,128)(2,1)} %reshape.97), calls=%async_computation.6 | async-start | bytes 1572864 | tf_op jit(solution)/shard_map/all_to_all | solution.py:49
  303.0 3.4 fusion.59
  306.4 18.5 %all-to-all-done.6 = bf16[32,96,128]{2,1,0:T(8,128)(2,1)S(1)} async-done(((bf16[32,96,128]{2,1,0:T(8,128)(2,1)}), bf16[32,96,128]{2,1,0:T(8,128)(2,1)S(1)}, u32[]{:S(2)}, u32[]{:S(2)}) %all-to-all-start.6) | async-done | bytes 786464 | tf_op jit(solution)/shard_map/all_to_all | solution.py:49
  325.3 2.0 multiply_convert_fusion.9
  329.4 6.0 %all-to-all-start.7 = ((bf16[32,96,128]{2,1,0:T(8,128)(2,1)}), bf16[32,96,128]{2,1,0:T(8,128)(2,1)S(1)}, u32[]{:S(2)}, u32[]{:S(2)}) async-start(bf16[32,96,128]{2,1,0:T(8,128)(2,1)} %reshape.99), calls=%async_computation.7 | async-start | bytes 1572864 | tf_op jit(solution)/shard_map/all_to_all | solution.py:49
  335.5 2.0 fusion.33
  341.8 17.2 %all-to-all-done.7 = bf16[32,96,128]{2,1,0:T(8,128)(2,1)S(1)} async-done(((bf16[32,96,128]{2,1,0:T(8,128)(2,1)}), bf16[32,96,128]{2,1,0:T(8,128)(2,1)S(1)}, u32[]{:S(2)}, u32[]{:S(2)}) %all-to-all-start.7) | async-done | bytes 786464 | tf_op jit(solution)/shard_map/all_to_all | solution.py:49
  (112 shorter events, 40.4 us)
Async XLA Ops:
  0.6 126.3 %copy-start = (bf16[1,1,384,1024]{3,2,1,0:T(8,128)(2,1)S(1)}, bf16[1,1,384,1024]{3,2,1,0:T(8,128)(2,1)}, u32[]{:S(2)}) copy-start(bf16[1,1,384,1024]{3,2,1,0:T(8,128)(2,1)} %param.15) | copy-start | bytes 2359300
  0.6 4.0 %copy-start.13 = (bf16[1,4,32,1024]{3,2,1,0:T(8,128)(2,1)S(1)}, bf16[1,4,32,1024]{3,2,1,0:T(8,128)(2,1)}, u32[]{:S(2)}) copy-start(bf16[1,4,32,1024]{3,2,1,0:T(8,128)(2,1)} %param.8) | copy-start | bytes 786436
  124.4 2.5 copy-start.4
  156.7 4.4 %copy-start.3 = (bf16[4,32,1024]{2,1,0:T(8,128)(2,1)S(1)}, bf16[4,32,1024]{2,1,0:T(8,128)(2,1)}, u32[]{:S(2)}) copy-start(bf16[4,32,1024]{2,1,0:T(8,128)(2,1)} %param.10) | copy-start | bytes 786436
  157.3 3.8 %copy-start.11 = (bf16[32,1024]{1,0:T(8,128)(2,1)}, bf16[32,1024]{1,0:T(8,128)(2,1)S(1)}, u32[]{:S(2)}) copy-start(bf16[32,1024]{1,0:T(8,128)(2,1)S(1)} %fusion.4) | copy-start | bytes 196612
  157.4 3.8 %collective-permute-start = (bf16[32,1024]{1,0:T(8,128)(2,1)S(1)}, bf16[32,1024]{1,0:T(8,128)(2,1)S(1)}, u32[]{:S(2)}, u32[]{:S(2)}) collective-permute-start(bf16[32,1024]{1,0:T(8,128)(2,1)S(1)} %fusion.4), channel_id=1, source_target_pairs={{32,0},{64,32},{96,64},{128,96},{160,128},{192,160},{224,192},{256... | collective-permute-start | bytes 196616 | tf_op jit(solution)/shard_map/ppermute | solution.py:13
  161.6 6.8 %copy-start.2 = (bf16[32,1,96,128]{3,2,1,0:T(8,128)(2,1)S(1)}, bf16[32,1,96,128]{3,2,1,0:T(8,128)(2,1)}, u32[]{:S(2)}) copy-start(bf16[32,1,96,128]{3,2,1,0:T(8,128)(2,1)} %get-tuple-element.7) | copy-start | bytes 2359300
  162.8 27.6 %all-to-all-start.2 = ((bf16[32,96,128]{2,1,0:T(8,128)(2,1)}), bf16[32,96,128]{2,1,0:T(8,128)(2,1)S(1)}, u32[]{:S(2)}, u32[]{:S(2)}) async-start(bf16[32,96,128]{2,1,0:T(8,128)(2,1)} %reshape.89), calls=%async_computation.2 | async-start | bytes 1572864 | tf_op jit(solution)/shard_map/all_to_all | solution.py:49
  190.7 2.3 copy-start.6
  190.8 2.3 copy-start.19
  224.5 3.8 %copy-start.14 = (bf16[32,1024]{1,0:T(8,128)(2,1)}, bf16[32,1024]{1,0:T(8,128)(2,1)S(1)}, u32[]{:S(2)}) copy-start(bf16[32,1024]{1,0:T(8,128)(2,1)S(1)} %add_convert_fusion.3) | copy-start | bytes 196612
  224.5 3.8 %collective-permute-start.1 = (bf16[32,1024]{1,0:T(8,128)(2,1)S(1)}, bf16[32,1024]{1,0:T(8,128)(2,1)S(1)}, u32[]{:S(2)}, u32[]{:S(2)}) collective-permute-start(bf16[32,1024]{1,0:T(8,128)(2,1)S(1)} %add_convert_fusion.3), channel_id=1, source_target_pairs={{32,0},{64,32},{96,64},{128,96},{160,128},{192,160},{224,192},{256... | collective-permute-start | bytes 196616 | tf_op jit(solution)/shard_map/ppermute | solution.py:13
  228.7 6.8 %copy-start.1 = (bf16[32,1,96,128]{3,2,1,0:T(8,128)(2,1)S(1)}, bf16[32,1,96,128]{3,2,1,0:T(8,128)(2,1)}, u32[]{:S(2)}) copy-start(bf16[32,1,96,128]{3,2,1,0:T(8,128)(2,1)} %get-tuple-element.6) | copy-start | bytes 2359300
  230.0 27.9 %all-to-all-start.4 = ((bf16[32,96,128]{2,1,0:T(8,128)(2,1)}), bf16[32,96,128]{2,1,0:T(8,128)(2,1)S(1)}, u32[]{:S(2)}, u32[]{:S(2)}) async-start(bf16[32,96,128]{2,1,0:T(8,128)(2,1)} %reshape.93), calls=%async_computation.4 | async-start | bytes 1572864 | tf_op jit(solution)/shard_map/all_to_all | solution.py:49
  258.2 2.3 copy-start.8
  258.2 2.3 copy-start.20
  291.6 5.5 %copy-start.16 = (bf16[32,1024]{1,0:T(8,128)(2,1)}, bf16[32,1024]{1,0:T(8,128)(2,1)S(1)}, u32[]{:S(2)}) copy-start(bf16[32,1024]{1,0:T(8,128)(2,1)S(1)} %add_convert_fusion.2) | copy-start | bytes 196612
  291.6 3.8 %collective-permute-start.2 = (bf16[32,1024]{1,0:T(8,128)(2,1)S(1)}, bf16[32,1024]{1,0:T(8,128)(2,1)S(1)}, u32[]{:S(2)}, u32[]{:S(2)}) collective-permute-start(bf16[32,1024]{1,0:T(8,128)(2,1)S(1)} %add_convert_fusion.2), channel_id=1, source_target_pairs={{32,0},{64,32},{96,64},{128,96},{160,128},{192,160},{224,192},{256... | collective-permute-start | bytes 196616 | tf_op jit(solution)/shard_map/ppermute | solution.py:13
  297.1 27.9 %all-to-all-start.6 = ((bf16[32,96,128]{2,1,0:T(8,128)(2,1)}), bf16[32,96,128]{2,1,0:T(8,128)(2,1)S(1)}, u32[]{:S(2)}, u32[]{:S(2)}) async-start(bf16[32,96,128]{2,1,0:T(8,128)(2,1)} %reshape.97), calls=%async_computation.6 | async-start | bytes 1572864 | tf_op jit(solution)/shard_map/all_to_all | solution.py:49
  328.2 7.2 %copy-start.5 = (bf16[384,1024]{1,0:T(8,128)(2,1)S(1)}, bf16[384,1024]{1,0:T(8,128)(2,1)}, u32[]{:S(2)}) copy-start(bf16[384,1024]{1,0:T(8,128)(2,1)} %reshape_squeeze.15) | copy-start | bytes 2359300
  329.4 29.6 %all-to-all-start.7 = ((bf16[32,96,128]{2,1,0:T(8,128)(2,1)}), bf16[32,96,128]{2,1,0:T(8,128)(2,1)S(1)}, u32[]{:S(2)}, u32[]{:S(2)}) async-start(bf16[32,96,128]{2,1,0:T(8,128)(2,1)} %reshape.99), calls=%async_computation.7 | async-start | bytes 1572864 | tf_op jit(solution)/shard_map/all_to_all | solution.py:49
  341.8 17.8 %copy-start.12 = (bf16[32,1024]{1,0:T(8,128)(2,1)S(1)}, bf16[32,1024]{1,0:T(8,128)(2,1)}, u32[]{:S(2)}) copy-start(bf16[32,1024]{1,0:T(8,128)(2,1)} %copy-done.11) | copy-start | bytes 196612
  341.8 17.8 %copy-start.15 = (bf16[32,1024]{1,0:T(8,128)(2,1)S(1)}, bf16[32,1024]{1,0:T(8,128)(2,1)}, u32[]{:S(2)}) copy-start(bf16[32,1024]{1,0:T(8,128)(2,1)} %copy-done.14) | copy-start | bytes 196612
  341.8 17.8 %copy-start.17 = (bf16[32,1024]{1,0:T(8,128)(2,1)S(1)}, bf16[32,1024]{1,0:T(8,128)(2,1)}, u32[]{:S(2)}) copy-start(bf16[32,1024]{1,0:T(8,128)(2,1)} %copy-done.16) | copy-start | bytes 196612
  (12 other events, 21.0 us)

commit v8 on v7

--- a/solution.py
+++ b/solution.py
@@ -49,15 +49,12 @@
     return lax.all_to_all(block, "expert", split_axis=0, concat_axis=0, tiled=True)
 
 
-def expert_backward(gate_pre, up_pre, sigma, grad_rows, both_weight, down_weight):
+def expert_backward(gate_factor, active, grad_rows, both_weight, down_weight):
     contract = (((1,), (1,)), ((), ()))
-    active = gate_pre * sigma
     hidden_grad = lax.dot_general(
         grad_rows, down_weight, contract, preferred_element_type=jnp.float32
     )
-    gate_grad = (hidden_grad * up_pre * sigma * (1.0 + gate_pre * (1.0 - sigma))).astype(
-        jnp.bfloat16
-    )
+    gate_grad = (hidden_grad * gate_factor).astype(jnp.bfloat16)
     up_grad = (hidden_grad * active).astype(jnp.bfloat16)
     both_grad = jnp.concatenate([gate_grad, up_grad], axis=1)
     row_grad = lax.dot_general(both_grad, both_weight, contract, preferred_element_type=jnp.float32)
@@ -105,10 +102,11 @@
         both_pre = jnp.dot(received_input, both_weight, preferred_element_type=jnp.float32)
         gate_pre, up_pre = both_pre[:, :hidden_units], both_pre[:, hidden_units:]
         sigma = jax.nn.sigmoid(gate_pre)
-        hidden = (gate_pre * sigma * up_pre).astype(jnp.bfloat16)
-        row_grad = expert_backward(
-            gate_pre, up_pre, sigma, flat_grad, both_weight, down_weight
-        )
+        active = gate_pre * sigma
+        hidden = (active * up_pre).astype(jnp.bfloat16)
+        gate_factor = up_pre * sigma * (1.0 + gate_pre * (1.0 - sigma))
+        gate_factor, active = lax.optimization_barrier((gate_factor, active))
+        row_grad = expert_backward(gate_factor, active, flat_grad, both_weight, down_weight)
         returned = unpack(exchange(pack(row_grad, experts)), width)
         gathered = lax.dot_general(
             select_all[moment], returned, rows_contract, preferred_element_type=jnp.float32

time: 362 us -> 360 us (level)
  other arithmetic: 2.56 us -> 6.97 us
    mul x0 -> x4, other arithmetic: none -> 4.41 us  [per_device(): active = gate_pre * sigma]
  transfers between devices with their start and end apart: 7 -> 7, of which waited for: 7 -> 7; matrix products, arithmetic and copies ran while one was open for 5% -> 6% of each run, Pallas kernels for 0% -> 0%
where the time goes in v8:
time: 360 us; the launch traced here: 359 us
  blocking collectives  189 us (52%)
  waiting for transfers between devices  73.7 us (20%)
  matrix products  30.7 us (9%)
  starting transfers between devices  28.6 us (8%)
  local copies, waits for them, and re-layouts  28.4 us (8%)
  other arithmetic  6.97 us (2%)
    all_to_all x4, blocking collectives, exchange(): lax.all_to_all(block, 'expert', split_axis=0, concat_axis=0, tiled=True)  189 us
    all_to_all x4, waiting for transfers between devices, exchange(): lax.all_to_all(block, 'expert', split_axis=0, concat_axis=0, tiled=True)  68 us
    all_to_all x4, starting transfers between devices, exchange(): lax.all_to_all(block, 'expert', split_axis=0, concat_axis=0, tiled=True)  22.9 us
    dot_general x4, matrix products, per_device(): jnp.dot(received_input, both_weight, preferred_element_type=jnp.float32)  10.3 us
    reshape x2, local copies, waits for them, and re-layouts, per_device(): send = picked.reshape(count, experts, -1, LANES).transpose(1, 0, 2, 3)  9.88 us
  transfers between devices with their start and end apart: 7, of which 7 were waited for; matrix products, arithmetic and copies ran while one was open for 6% of the time, Pallas kernels for 0%

profile of v8, /device:TPU:26, one launch (start us, length us, event | category | flops | bytes accessed | tf_op | source)
XLA Modules:
  0.0 358.7 jit_solution(3295290242836663088)
XLA Ops:
  4.7 3.1 multiply_convert_fusion
  7.8 7.1 %reshape.84 = bf16[5,32,96,128]{3,2,1,0:T(8,128)(2,1)} reshape(bf16[5,384,1024]{2,1,0:T(8,128)(2,1)} %multiply_convert_fusion) | data formatting | bytes 7864320 | tf_op jit(solution)/shard_map/reshape | solution.py:94
  14.9 2.8 copy.35
  17.7 103.1 %all_to_all.40 = bf16[32,480,128]{2,1,0:T(8,128)(2,1)S(1)} all-to-all(bf16[32,480,128]{2,1,0:T(8,128)(2,1)S(1)} %bitcast.113), channel_id=1, replica_groups=mesh['section'=16,'expert'=32] {'expert'}, dimensions={0} | all-to-all | bytes 7864320 | tf_op jit(solution)/shard_map/all_to_all | solution.py:49
  123.0 2.4 fusion.58
  128.4 26.9 %all_to_all.41 = bf16[32,96,128]{2,1,0:T(8,128)(2,1)S(1)} all-to-all(bf16[32,96,128]{2,1,0:T(8,128)(2,1)S(1)} %reshape.87), channel_id=1, replica_groups=mesh['section'=16,'expert'=32] {'expert'}, dimensions={0} | all-to-all | bytes 1572864 | tf_op jit(solution)/shard_map/all_to_all | solution.py:49
  155.9 1.9 collective-permute-start
  161.3 5.6 %all-to-all-start.2 = ((bf16[32,96,128]{2,1,0:T(8,128)(2,1)}), bf16[32,96,128]{2,1,0:T(8,128)(2,1)S(1)}, u32[]{:S(2)}, u32[]{:S(2)}) async-start(bf16[32,96,128]{2,1,0:T(8,128)(2,1)} %reshape.89), calls=%async_computation.2 | async-start | bytes 1572864 | tf_op jit(solution)/shard_map/all_to_all | solution.py:49
  168.1 2.6 fusion.57
  172.1 16.8 %all-to-all-done.2 = bf16[32,96,128]{2,1,0:T(8,128)(2,1)S(1)} async-done(((bf16[32,96,128]{2,1,0:T(8,128)(2,1)}), bf16[32,96,128]{2,1,0:T(8,128)(2,1)S(1)}, u32[]{:S(2)}, u32[]{:S(2)}) %all-to-all-start.2) | async-done | bytes 786464 | tf_op jit(solution)/shard_map/all_to_all | solution.py:49
  189.3 2.1 multiply_convert_fusion.13
  192.6 29.6 %all_to_all.42 = bf16[32,96,128]{2,1,0:T(8,128)(2,1)S(1)} all-to-all(bf16[32,96,128]{2,1,0:T(8,128)(2,1)S(1)} %reshape.91), channel_id=1, replica_groups=mesh['section'=16,'expert'=32] {'expert'}, dimensions={0} | all-to-all | bytes 1572864 | tf_op jit(solution)/shard_map/all_to_all | solution.py:49
  228.4 5.6 %all-to-all-start.4 = ((bf16[32,96,128]{2,1,0:T(8,128)(2,1)}), bf16[32,96,128]{2,1,0:T(8,128)(2,1)S(1)}, u32[]{:S(2)}, u32[]{:S(2)}) async-start(bf16[32,96,128]{2,1,0:T(8,128)(2,1)} %reshape.93), calls=%async_computation.4 | async-start | bytes 1572864 | tf_op jit(solution)/shard_map/all_to_all | solution.py:49
  235.2 2.6 fusion.56
  239.2 17.0 %all-to-all-done.4 = bf16[32,96,128]{2,1,0:T(8,128)(2,1)S(1)} async-done(((bf16[32,96,128]{2,1,0:T(8,128)(2,1)}), bf16[32,96,128]{2,1,0:T(8,128)(2,1)S(1)}, u32[]{:S(2)}, u32[]{:S(2)}) %all-to-all-start.4) | async-done | bytes 786464 | tf_op jit(solution)/shard_map/all_to_all | solution.py:49
  256.6 2.1 multiply_convert_fusion.11
  260.0 29.4 %all_to_all.43 = bf16[32,96,128]{2,1,0:T(8,128)(2,1)S(1)} all-to-all(bf16[32,96,128]{2,1,0:T(8,128)(2,1)S(1)} %reshape.95), channel_id=1, replica_groups=mesh['section'=16,'expert'=32] {'expert'}, dimensions={0} | all-to-all | bytes 1572864 | tf_op jit(solution)/shard_map/all_to_all | solution.py:49
  295.4 5.7 %all-to-all-start.6 = ((bf16[32,96,128]{2,1,0:T(8,128)(2,1)}), bf16[32,96,128]{2,1,0:T(8,128)(2,1)S(1)}, u32[]{:S(2)}, u32[]{:S(2)}) async-start(bf16[32,96,128]{2,1,0:T(8,128)(2,1)} %reshape.97), calls=%async_computation.6 | async-start | bytes 1572864 | tf_op jit(solution)/shard_map/all_to_all | solution.py:49
  302.3 2.6 fusion.55
  306.4 17.0 %all-to-all-done.6 = bf16[32,96,128]{2,1,0:T(8,128)(2,1)S(1)} async-done(((bf16[32,96,128]{2,1,0:T(8,128)(2,1)}), bf16[32,96,128]{2,1,0:T(8,128)(2,1)S(1)}, u32[]{:S(2)}, u32[]{:S(2)}) %all-to-all-start.6) | async-done | bytes 786464 | tf_op jit(solution)/shard_map/all_to_all | solution.py:49
  323.7 2.0 multiply_convert_fusion.9
  327.8 6.0 %all-to-all-start.7 = ((bf16[32,96,128]{2,1,0:T(8,128)(2,1)}), bf16[32,96,128]{2,1,0:T(8,128)(2,1)S(1)}, u32[]{:S(2)}, u32[]{:S(2)}) async-start(bf16[32,96,128]{2,1,0:T(8,128)(2,1)} %reshape.99), calls=%async_computation.7 | async-start | bytes 1572864 | tf_op jit(solution)/shard_map/all_to_all | solution.py:49
  333.8 2.0 fusion.33
  340.1 17.2 %all-to-all-done.7 = bf16[32,96,128]{2,1,0:T(8,128)(2,1)S(1)} async-done(((bf16[32,96,128]{2,1,0:T(8,128)(2,1)}), bf16[32,96,128]{2,1,0:T(8,128)(2,1)S(1)}, u32[]{:S(2)}, u32[]{:S(2)}) %all-to-all-start.7) | async-done | bytes 786464 | tf_op jit(solution)/shard_map/all_to_all | solution.py:49
  (120 shorter events, 44.0 us)
Async XLA Ops:
  0.6 125.0 %copy-start = (bf16[1,1,384,1024]{3,2,1,0:T(8,128)(2,1)S(1)}, bf16[1,1,384,1024]{3,2,1,0:T(8,128)(2,1)}, u32[]{:S(2)}) copy-start(bf16[1,1,384,1024]{3,2,1,0:T(8,128)(2,1)} %param.15) | copy-start | bytes 2359300
  0.6 4.0 %copy-start.18 = (bf16[1,4,32,1024]{3,2,1,0:T(8,128)(2,1)S(1)}, bf16[1,4,32,1024]{3,2,1,0:T(8,128)(2,1)}, u32[]{:S(2)}) copy-start(bf16[1,4,32,1024]{3,2,1,0:T(8,128)(2,1)} %param.8) | copy-start | bytes 786436
  155.2 4.4 %copy-start.15 = (bf16[4,32,1024]{2,1,0:T(8,128)(2,1)S(1)}, bf16[4,32,1024]{2,1,0:T(8,128)(2,1)}, u32[]{:S(2)}) copy-start(bf16[4,32,1024]{2,1,0:T(8,128)(2,1)} %param.10) | copy-start | bytes 786436
  155.8 3.8 %copy-start.16 = (bf16[32,1024]{1,0:T(8,128)(2,1)}, bf16[32,1024]{1,0:T(8,128)(2,1)S(1)}, u32[]{:S(2)}) copy-start(bf16[32,1024]{1,0:T(8,128)(2,1)S(1)} %fusion.4) | copy-start | bytes 196612
  155.9 3.8 %collective-permute-start = (bf16[32,1024]{1,0:T(8,128)(2,1)S(1)}, bf16[32,1024]{1,0:T(8,128)(2,1)S(1)}, u32[]{:S(2)}, u32[]{:S(2)}) collective-permute-start(bf16[32,1024]{1,0:T(8,128)(2,1)S(1)} %fusion.4), channel_id=1, source_target_pairs={{32,0},{64,32},{96,64},{128,96},{160,128},{192,160},{224,192},{256... | collective-permute-start | bytes 196616 | tf_op jit(solution)/shard_map/ppermute | solution.py:13
  160.1 6.8 %copy-start.7 = (bf16[32,1,96,128]{3,2,1,0:T(8,128)(2,1)S(1)}, bf16[32,1,96,128]{3,2,1,0:T(8,128)(2,1)}, u32[]{:S(2)}) copy-start(bf16[32,1,96,128]{3,2,1,0:T(8,128)(2,1)} %get-tuple-element.23) | copy-start | bytes 2359300
  161.3 27.6 %all-to-all-start.2 = ((bf16[32,96,128]{2,1,0:T(8,128)(2,1)}), bf16[32,96,128]{2,1,0:T(8,128)(2,1)S(1)}, u32[]{:S(2)}, u32[]{:S(2)}) async-start(bf16[32,96,128]{2,1,0:T(8,128)(2,1)} %reshape.89), calls=%async_computation.2 | async-start | bytes 1572864 | tf_op jit(solution)/shard_map/all_to_all | solution.py:49
  189.2 2.2 copy-start.1
  189.3 2.2 copy-start.24
  189.3 2.2 copy-start.28
  222.9 3.8 %copy-start.19 = (bf16[32,1024]{1,0:T(8,128)(2,1)}, bf16[32,1024]{1,0:T(8,128)(2,1)S(1)}, u32[]{:S(2)}) copy-start(bf16[32,1024]{1,0:T(8,128)(2,1)S(1)} %add_convert_fusion.3) | copy-start | bytes 196612
  222.9 3.8 %collective-permute-start.1 = (bf16[32,1024]{1,0:T(8,128)(2,1)S(1)}, bf16[32,1024]{1,0:T(8,128)(2,1)S(1)}, u32[]{:S(2)}, u32[]{:S(2)}) collective-permute-start(bf16[32,1024]{1,0:T(8,128)(2,1)S(1)} %add_convert_fusion.3), channel_id=1, source_target_pairs={{32,0},{64,32},{96,64},{128,96},{160,128},{192,160},{224,192},{256... | collective-permute-start | bytes 196616 | tf_op jit(solution)/shard_map/ppermute | solution.py:13
  227.1 6.8 %copy-start.6 = (bf16[32,1,96,128]{3,2,1,0:T(8,128)(2,1)S(1)}, bf16[32,1,96,128]{3,2,1,0:T(8,128)(2,1)}, u32[]{:S(2)}) copy-start(bf16[32,1,96,128]{3,2,1,0:T(8,128)(2,1)} %get-tuple-element.22) | copy-start | bytes 2359300
  228.4 27.9 %all-to-all-start.4 = ((bf16[32,96,128]{2,1,0:T(8,128)(2,1)}), bf16[32,96,128]{2,1,0:T(8,128)(2,1)S(1)}, u32[]{:S(2)}, u32[]{:S(2)}) async-start(bf16[32,96,128]{2,1,0:T(8,128)(2,1)} %reshape.93), calls=%async_computation.4 | async-start | bytes 1572864 | tf_op jit(solution)/shard_map/all_to_all | solution.py:49
  256.6 2.2 copy-start.3
  256.6 2.2 copy-start.25
  289.9 5.5 %copy-start.21 = (bf16[32,1024]{1,0:T(8,128)(2,1)}, bf16[32,1024]{1,0:T(8,128)(2,1)S(1)}, u32[]{:S(2)}) copy-start(bf16[32,1024]{1,0:T(8,128)(2,1)S(1)} %add_convert_fusion.2) | copy-start | bytes 196612
  289.9 3.8 %collective-permute-start.2 = (bf16[32,1024]{1,0:T(8,128)(2,1)S(1)}, bf16[32,1024]{1,0:T(8,128)(2,1)S(1)}, u32[]{:S(2)}, u32[]{:S(2)}) collective-permute-start(bf16[32,1024]{1,0:T(8,128)(2,1)S(1)} %add_convert_fusion.2), channel_id=1, source_target_pairs={{32,0},{64,32},{96,64},{128,96},{160,128},{192,160},{224,192},{256... | collective-permute-start | bytes 196616 | tf_op jit(solution)/shard_map/ppermute | solution.py:13
  295.4 5.7 %copy-start.5 = (bf16[32,1,96,128]{3,2,1,0:T(8,128)(2,1)S(1)}, bf16[32,1,96,128]{3,2,1,0:T(8,128)(2,1)}, u32[]{:S(2)}) copy-start(bf16[32,1,96,128]{3,2,1,0:T(8,128)(2,1)} %get-tuple-element.21) | copy-start | bytes 2359300
  295.4 28.0 %all-to-all-start.6 = ((bf16[32,96,128]{2,1,0:T(8,128)(2,1)}), bf16[32,96,128]{2,1,0:T(8,128)(2,1)S(1)}, u32[]{:S(2)}, u32[]{:S(2)}) async-start(bf16[32,96,128]{2,1,0:T(8,128)(2,1)} %reshape.97), calls=%async_computation.6 | async-start | bytes 1572864 | tf_op jit(solution)/shard_map/all_to_all | solution.py:49
  327.8 29.6 %all-to-all-start.7 = ((bf16[32,96,128]{2,1,0:T(8,128)(2,1)}), bf16[32,96,128]{2,1,0:T(8,128)(2,1)S(1)}, u32[]{:S(2)}, u32[]{:S(2)}) async-start(bf16[32,96,128]{2,1,0:T(8,128)(2,1)} %reshape.99), calls=%async_computation.7 | async-start | bytes 1572864 | tf_op jit(solution)/shard_map/all_to_all | solution.py:49
  340.1 17.8 %copy-start.17 = (bf16[32,1024]{1,0:T(8,128)(2,1)S(1)}, bf16[32,1024]{1,0:T(8,128)(2,1)}, u32[]{:S(2)}) copy-start(bf16[32,1024]{1,0:T(8,128)(2,1)} %copy-done.16) | copy-start | bytes 196612
  340.1 17.8 %copy-start.20 = (bf16[32,1024]{1,0:T(8,128)(2,1)S(1)}, bf16[32,1024]{1,0:T(8,128)(2,1)}, u32[]{:S(2)}) copy-start(bf16[32,1024]{1,0:T(8,128)(2,1)} %copy-done.19) | copy-start | bytes 196612
  340.1 17.9 %copy-start.22 = (bf16[32,1024]{1,0:T(8,128)(2,1)S(1)}, bf16[32,1024]{1,0:T(8,128)(2,1)}, u32[]{:S(2)}) copy-start(bf16[32,1024]{1,0:T(8,128)(2,1)} %copy-done.21) | copy-start | bytes 196612
  (14 other events, 22.1 us)

commit v9 on v8

--- a/solution.py
+++ b/solution.py
@@ -51,9 +51,7 @@
 
 def expert_backward(gate_factor, active, grad_rows, both_weight, down_weight):
     contract = (((1,), (1,)), ((), ()))
-    hidden_grad = lax.dot_general(
-        grad_rows, down_weight, contract, preferred_element_type=jnp.float32
-    )
+    hidden_grad = jnp.dot(grad_rows, down_weight, preferred_element_type=jnp.float32)
     gate_grad = (hidden_grad * gate_factor).astype(jnp.bfloat16)
     up_grad = (hidden_grad * active).astype(jnp.bfloat16)
     both_grad = jnp.concatenate([gate_grad, up_grad], axis=1)
@@ -70,6 +68,7 @@
     gate_weight = w_gate[0, 0]
     up_weight = w_up[0, 0]
     down_weight = w_down[0, 0]
+    down_across = lax.optimization_barrier(down_weight.T)
     both_weight = jnp.concatenate([gate_weight, up_weight], axis=1)
     hidden_units = gate_weight.shape[1]
     is_last = lax.axis_index("section") == lax.axis_size("section") - 1
@@ -106,7 +105,7 @@
         hidden = (active * up_pre).astype(jnp.bfloat16)
         gate_factor = up_pre * sigma * (1.0 + gate_pre * (1.0 - sigma))
         gate_factor, active = lax.optimization_barrier((gate_factor, active))
-        row_grad = expert_backward(gate_factor, active, flat_grad, both_weight, down_weight)
+        row_grad = expert_backward(gate_factor, active, flat_grad, both_weight, down_across)
         returned = unpack(exchange(pack(row_grad, experts)), width)
         gathered = lax.dot_general(
             select_all[moment], returned, rows_contract, preferred_element_type=jnp.float32

time: 360 us -> 366 us (1.017)
  blocking collectives: 189 us -> 88.7 us
  waiting for transfers between devices: 73.7 us -> 162 us
  starting transfers between devices: 28.6 us -> 42.1 us
  local copies, waits for them, and re-layouts: 28.4 us -> 32.4 us
    all_to_all x4 -> x3, blocking collectives: 189 us -> 88.7 us  [exchange(): lax.all_to_all(block, 'expert', split_axis=0, concat_axis=0, tiled=True)]
    all_to_all x4 -> x5, waiting for transfers between devices: 68 us -> 156 us  [exchange(): lax.all_to_all(block, 'expert', split_axis=0, concat_axis=0, tiled=True)]
    all_to_all x4 -> x5, starting transfers between devices: 22.9 us -> 36.4 us  [exchange(): lax.all_to_all(block, 'expert', split_axis=0, concat_axis=0, tiled=True)]
  transfers between devices with their start and end apart: 7 -> 8, of which waited for: 7 -> 8; matrix products, arithmetic and copies ran while one was open for 6% -> 6% of each run, Pallas kernels for 0% -> 0%
where the time goes in v9:
time: 366 us; the launch traced here: 364 us
  waiting for transfers between devices  162 us (44%)
  blocking collectives  88.7 us (24%)
  starting transfers between devices  42.1 us (12%)
  local copies, waits for them, and re-layouts  32.4 us (9%)
  matrix products  30.7 us (8%)
  other arithmetic  7.01 us (2%)
    all_to_all x5, waiting for transfers between devices, exchange(): lax.all_to_all(block, 'expert', split_axis=0, concat_axis=0, tiled=True)  156 us
    all_to_all x3, blocking collectives, exchange(): lax.all_to_all(block, 'expert', split_axis=0, concat_axis=0, tiled=True)  88.7 us
    all_to_all x5, starting transfers between devices, exchange(): lax.all_to_all(block, 'expert', split_axis=0, concat_axis=0, tiled=True)  36.4 us
    reshape x2, local copies, waits for them, and re-layouts, per_device(): send = picked.reshape(count, experts, -1, LANES).transpose(1, 0, 2, 3)  11.7 us
    dot_general x4, matrix products, per_device(): jnp.dot(received_input, both_weight, preferred_element_type=jnp.float32)  10.3 us
  transfers between devices with their start and end apart: 8, of which 8 were waited for; matrix products, arithmetic and copies ran while one was open for 6% of the time, Pallas kernels for 0%

profile of v9, /device:TPU:26, one launch (start us, length us, event | category | flops | bytes accessed | tf_op | source)
XLA Modules:
  0.0 364.2 jit_solution(14433799276229387639)
XLA Ops:
  4.7 3.1 multiply_convert_fusion
  7.8 7.0 %reshape.84 = bf16[5,32,96,128]{3,2,1,0:T(8,128)(2,1)} reshape(bf16[5,384,1024]{2,1,0:T(8,128)(2,1)} %multiply_convert_fusion) | data formatting | bytes 7864320 | tf_op jit(solution)/shard_map/reshape | solution.py:93
  14.9 4.7 %copy.35 = bf16[5,32,96,128]{3,2,0,1:T(8,128)(2,1)} copy(bf16[5,32,96,128]{3,2,1,0:T(8,128)(2,1)} %reshape.84) | data formatting | bytes 7864320 | tf_op jit(solution)/shard_map/reshape | solution.py:93
  19.6 13.5 %all-to-all-start = ((bf16[32,480,128]{2,1,0:T(8,128)(2,1)}), bf16[32,480,128]{2,1,0:T(8,128)(2,1)}, u32[]{:S(2)}, u32[]{:S(2)}) async-start(bf16[32,480,128]{2,1,0:T(8,128)(2,1)} %bitcast.106), calls=%async_computation | async-start | bytes 7864320 | tf_op jit(solution)/shard_map/all_to_all | solution.py:49
  33.1 88.3 %all-to-all-done = bf16[32,480,128]{2,1,0:T(8,128)(2,1)} async-done(((bf16[32,480,128]{2,1,0:T(8,128)(2,1)}), bf16[32,480,128]{2,1,0:T(8,128)(2,1)}, u32[]{:S(2)}, u32[]{:S(2)}) %all-to-all-start) | async-done | bytes 3932192 | tf_op jit(solution)/shard_map/all_to_all | solution.py:49
  121.3 3.7 %fusion.51 = (bf16[32,1,96,128]{3,2,1,0:T(8,128)(2,1)}, bf16[32,1,96,128]{3,2,1,0:T(8,128)(2,1)}, bf16[32,1,96,128]{3,2,1,0:T(8,128)(2,1)}, bf16[32,1,96,128]{3,2,1,0:T(8,128)(2,1)S(1)}, bf16[32,1,96,128]{3,2,1,0:T(8,128)(2,1)S(1)}) fusion(bf16[32,5,96,128]{3,2,1,0:T(8,128)(2,1)} %bitcast.9), kind=kLoop, calls=%fused_computation.99 | loop fusion | bytes 7864320 | tf_op jit(solution)/shard_map/slice | solution.py:100
  125.7 2.4 fusion.50
  131.0 29.7 %all_to_all.40 = bf16[32,96,128]{2,1,0:T(8,128)(2,1)S(1)} all-to-all(bf16[32,96,128]{2,1,0:T(8,128)(2,1)S(1)} %reshape.87), channel_id=1, replica_groups=mesh['section'=16,'expert'=32] {'expert'}, dimensions={0} | all-to-all | bytes 1572864 | tf_op jit(solution)/shard_map/all_to_all | solution.py:49
  166.8 5.6 %all-to-all-start.2 = ((bf16[32,96,128]{2,1,0:T(8,128)(2,1)}), bf16[32,96,128]{2,1,0:T(8,128)(2,1)S(1)}, u32[]{:S(2)}, u32[]{:S(2)}) async-start(bf16[32,96,128]{2,1,0:T(8,128)(2,1)} %reshape.89), calls=%async_computation.2 | async-start | bytes 1572864 | tf_op jit(solution)/shard_map/all_to_all | solution.py:49
  173.6 2.6 fusion.49
  177.7 16.7 %all-to-all-done.2 = bf16[32,96,128]{2,1,0:T(8,128)(2,1)S(1)} async-done(((bf16[32,96,128]{2,1,0:T(8,128)(2,1)}), bf16[32,96,128]{2,1,0:T(8,128)(2,1)S(1)}, u32[]{:S(2)}, u32[]{:S(2)}) %all-to-all-start.2) | async-done | bytes 786464 | tf_op jit(solution)/shard_map/all_to_all | solution.py:49
  194.8 2.1 multiply_convert_fusion.13
  198.1 29.7 %all_to_all.41 = bf16[32,96,128]{2,1,0:T(8,128)(2,1)S(1)} all-to-all(bf16[32,96,128]{2,1,0:T(8,128)(2,1)S(1)} %reshape.91), channel_id=1, replica_groups=mesh['section'=16,'expert'=32] {'expert'}, dimensions={0} | all-to-all | bytes 1572864 | tf_op jit(solution)/shard_map/all_to_all | solution.py:49
  233.9 5.6 %all-to-all-start.4 = ((bf16[32,96,128]{2,1,0:T(8,128)(2,1)}), bf16[32,96,128]{2,1,0:T(8,128)(2,1)S(1)}, u32[]{:S(2)}, u32[]{:S(2)}) async-start(bf16[32,96,128]{2,1,0:T(8,128)(2,1)} %reshape.93), calls=%async_computation.4 | async-start | bytes 1572864 | tf_op jit(solution)/shard_map/all_to_all | solution.py:49
  240.7 2.6 fusion.48
  244.7 17.0 %all-to-all-done.4 = bf16[32,96,128]{2,1,0:T(8,128)(2,1)S(1)} async-done(((bf16[32,96,128]{2,1,0:T(8,128)(2,1)}), bf16[32,96,128]{2,1,0:T(8,128)(2,1)S(1)}, u32[]{:S(2)}, u32[]{:S(2)}) %all-to-all-start.4) | async-done | bytes 786464 | tf_op jit(solution)/shard_map/all_to_all | solution.py:49
  262.1 2.1 multiply_convert_fusion.11
  265.4 29.4 %all_to_all.42 = bf16[32,96,128]{2,1,0:T(8,128)(2,1)S(1)} all-to-all(bf16[32,96,128]{2,1,0:T(8,128)(2,1)S(1)} %reshape.95), channel_id=1, replica_groups=mesh['section'=16,'expert'=32] {'expert'}, dimensions={0} | all-to-all | bytes 1572864 | tf_op jit(solution)/shard_map/all_to_all | solution.py:49
  300.9 5.7 %all-to-all-start.6 = ((bf16[32,96,128]{2,1,0:T(8,128)(2,1)}), bf16[32,96,128]{2,1,0:T(8,128)(2,1)S(1)}, u32[]{:S(2)}, u32[]{:S(2)}) async-start(bf16[32,96,128]{2,1,0:T(8,128)(2,1)} %reshape.97), calls=%async_computation.6 | async-start | bytes 1572864 | tf_op jit(solution)/shard_map/all_to_all | solution.py:49
  307.8 2.6 fusion.47
  311.9 17.0 %all-to-all-done.6 = bf16[32,96,128]{2,1,0:T(8,128)(2,1)S(1)} async-done(((bf16[32,96,128]{2,1,0:T(8,128)(2,1)}), bf16[32,96,128]{2,1,0:T(8,128)(2,1)S(1)}, u32[]{:S(2)}, u32[]{:S(2)}) %all-to-all-start.6) | async-done | bytes 786464 | tf_op jit(solution)/shard_map/all_to_all | solution.py:49
  333.3 6.0 %all-to-all-start.7 = ((bf16[32,96,128]{2,1,0:T(8,128)(2,1)}), bf16[32,96,128]{2,1,0:T(8,128)(2,1)S(1)}, u32[]{:S(2)}, u32[]{:S(2)}) async-start(bf16[32,96,128]{2,1,0:T(8,128)(2,1)} %reshape.99), calls=%async_computation.7 | async-start | bytes 1572864 | tf_op jit(solution)/shard_map/all_to_all | solution.py:49
  339.3 2.0 fusion.25
  345.6 17.2 %all-to-all-done.7 = bf16[32,96,128]{2,1,0:T(8,128)(2,1)S(1)} async-done(((bf16[32,96,128]{2,1,0:T(8,128)(2,1)}), bf16[32,96,128]{2,1,0:T(8,128)(2,1)S(1)}, u32[]{:S(2)}, u32[]{:S(2)}) %all-to-all-start.7) | async-done | bytes 786464 | tf_op jit(solution)/shard_map/all_to_all | solution.py:49
  (121 shorter events, 46.5 us)
Async XLA Ops:
  0.6 32.4 %copy-start = (bf16[1,1,384,1024]{3,2,1,0:T(8,128)(2,1)S(1)}, bf16[1,1,384,1024]{3,2,1,0:T(8,128)(2,1)}, u32[]{:S(2)}) copy-start(bf16[1,1,384,1024]{3,2,1,0:T(8,128)(2,1)} %param.15) | copy-start | bytes 2359300
  0.6 4.0 %copy-start.18 = (bf16[1,4,32,1024]{3,2,1,0:T(8,128)(2,1)S(1)}, bf16[1,4,32,1024]{3,2,1,0:T(8,128)(2,1)}, u32[]{:S(2)}) copy-start(bf16[1,4,32,1024]{3,2,1,0:T(8,128)(2,1)} %param.8) | copy-start | bytes 786436
  19.6 101.8 %all-to-all-start = ((bf16[32,480,128]{2,1,0:T(8,128)(2,1)}), bf16[32,480,128]{2,1,0:T(8,128)(2,1)}, u32[]{:S(2)}, u32[]{:S(2)}) async-start(bf16[32,480,128]{2,1,0:T(8,128)(2,1)} %bitcast.106), calls=%async_computation | async-start | bytes 7864320 | tf_op jit(solution)/shard_map/all_to_all | solution.py:49
  160.7 4.4 %copy-start.15 = (bf16[4,32,1024]{2,1,0:T(8,128)(2,1)S(1)}, bf16[4,32,1024]{2,1,0:T(8,128)(2,1)}, u32[]{:S(2)}) copy-start(bf16[4,32,1024]{2,1,0:T(8,128)(2,1)} %param.10) | copy-start | bytes 786436
  161.3 3.8 %copy-start.16 = (bf16[32,1024]{1,0:T(8,128)(2,1)}, bf16[32,1024]{1,0:T(8,128)(2,1)S(1)}, u32[]{:S(2)}) copy-start(bf16[32,1024]{1,0:T(8,128)(2,1)S(1)} %fusion.4) | copy-start | bytes 196612
  161.3 3.8 %collective-permute-start = (bf16[32,1024]{1,0:T(8,128)(2,1)S(1)}, bf16[32,1024]{1,0:T(8,128)(2,1)S(1)}, u32[]{:S(2)}, u32[]{:S(2)}) collective-permute-start(bf16[32,1024]{1,0:T(8,128)(2,1)S(1)} %fusion.4), channel_id=1, source_target_pairs={{32,0},{64,32},{96,64},{128,96},{160,128},{192,160},{224,192},{256... | collective-permute-start | bytes 196616 | tf_op jit(solution)/shard_map/ppermute | solution.py:13
  165.6 6.8 %copy-start.7 = (bf16[32,1,96,128]{3,2,1,0:T(8,128)(2,1)S(1)}, bf16[32,1,96,128]{3,2,1,0:T(8,128)(2,1)}, u32[]{:S(2)}) copy-start(bf16[32,1,96,128]{3,2,1,0:T(8,128)(2,1)} %get-tuple-element.23) | copy-start | bytes 2359300
  166.8 27.6 %all-to-all-start.2 = ((bf16[32,96,128]{2,1,0:T(8,128)(2,1)}), bf16[32,96,128]{2,1,0:T(8,128)(2,1)S(1)}, u32[]{:S(2)}, u32[]{:S(2)}) async-start(bf16[32,96,128]{2,1,0:T(8,128)(2,1)} %reshape.89), calls=%async_computation.2 | async-start | bytes 1572864 | tf_op jit(solution)/shard_map/all_to_all | solution.py:49
  194.7 2.2 copy-start.1
  194.7 2.2 copy-start.24
  228.4 3.8 %copy-start.19 = (bf16[32,1024]{1,0:T(8,128)(2,1)}, bf16[32,1024]{1,0:T(8,128)(2,1)S(1)}, u32[]{:S(2)}) copy-start(bf16[32,1024]{1,0:T(8,128)(2,1)S(1)} %add_convert_fusion.3) | copy-start | bytes 196612
  228.4 3.8 %collective-permute-start.1 = (bf16[32,1024]{1,0:T(8,128)(2,1)S(1)}, bf16[32,1024]{1,0:T(8,128)(2,1)S(1)}, u32[]{:S(2)}, u32[]{:S(2)}) collective-permute-start(bf16[32,1024]{1,0:T(8,128)(2,1)S(1)} %add_convert_fusion.3), channel_id=1, source_target_pairs={{32,0},{64,32},{96,64},{128,96},{160,128},{192,160},{224,192},{256... | collective-permute-start | bytes 196616 | tf_op jit(solution)/shard_map/ppermute | solution.py:13
  232.6 6.8 %copy-start.6 = (bf16[32,1,96,128]{3,2,1,0:T(8,128)(2,1)S(1)}, bf16[32,1,96,128]{3,2,1,0:T(8,128)(2,1)}, u32[]{:S(2)}) copy-start(bf16[32,1,96,128]{3,2,1,0:T(8,128)(2,1)} %get-tuple-element.22) | copy-start | bytes 2359300
  233.9 27.9 %all-to-all-start.4 = ((bf16[32,96,128]{2,1,0:T(8,128)(2,1)}), bf16[32,96,128]{2,1,0:T(8,128)(2,1)S(1)}, u32[]{:S(2)}, u32[]{:S(2)}) async-start(bf16[32,96,128]{2,1,0:T(8,128)(2,1)} %reshape.93), calls=%async_computation.4 | async-start | bytes 1572864 | tf_op jit(solution)/shard_map/all_to_all | solution.py:49
  262.1 2.2 copy-start.3
  262.1 2.2 copy-start.25
  295.4 5.5 %copy-start.21 = (bf16[32,1024]{1,0:T(8,128)(2,1)}, bf16[32,1024]{1,0:T(8,128)(2,1)S(1)}, u32[]{:S(2)}) copy-start(bf16[32,1024]{1,0:T(8,128)(2,1)S(1)} %add_convert_fusion.2) | copy-start | bytes 196612
  295.4 3.8 %collective-permute-start.2 = (bf16[32,1024]{1,0:T(8,128)(2,1)S(1)}, bf16[32,1024]{1,0:T(8,128)(2,1)S(1)}, u32[]{:S(2)}, u32[]{:S(2)}) collective-permute-start(bf16[32,1024]{1,0:T(8,128)(2,1)S(1)} %add_convert_fusion.2), channel_id=1, source_target_pairs={{32,0},{64,32},{96,64},{128,96},{160,128},{192,160},{224,192},{256... | collective-permute-start | bytes 196616 | tf_op jit(solution)/shard_map/ppermute | solution.py:13
  300.9 5.7 %copy-start.5 = (bf16[32,1,96,128]{3,2,1,0:T(8,128)(2,1)S(1)}, bf16[32,1,96,128]{3,2,1,0:T(8,128)(2,1)}, u32[]{:S(2)}) copy-start(bf16[32,1,96,128]{3,2,1,0:T(8,128)(2,1)} %get-tuple-element.21) | copy-start | bytes 2359300
  300.9 28.0 %all-to-all-start.6 = ((bf16[32,96,128]{2,1,0:T(8,128)(2,1)}), bf16[32,96,128]{2,1,0:T(8,128)(2,1)S(1)}, u32[]{:S(2)}, u32[]{:S(2)}) async-start(bf16[32,96,128]{2,1,0:T(8,128)(2,1)} %reshape.97), calls=%async_computation.6 | async-start | bytes 1572864 | tf_op jit(solution)/shard_map/all_to_all | solution.py:49
  333.3 29.6 %all-to-all-start.7 = ((bf16[32,96,128]{2,1,0:T(8,128)(2,1)}), bf16[32,96,128]{2,1,0:T(8,128)(2,1)S(1)}, u32[]{:S(2)}, u32[]{:S(2)}) async-start(bf16[32,96,128]{2,1,0:T(8,128)(2,1)} %reshape.99), calls=%async_computation.7 | async-start | bytes 1572864 | tf_op jit(solution)/shard_map/all_to_all | solution.py:49
  345.6 17.8 %copy-start.17 = (bf16[32,1024]{1,0:T(8,128)(2,1)S(1)}, bf16[32,1024]{1,0:T(8,128)(2,1)}, u32[]{:S(2)}) copy-start(bf16[32,1024]{1,0:T(8,128)(2,1)} %copy-done.16) | copy-start | bytes 196612
  345.6 17.8 %copy-start.20 = (bf16[32,1024]{1,0:T(8,128)(2,1)S(1)}, bf16[32,1024]{1,0:T(8,128)(2,1)}, u32[]{:S(2)}) copy-start(bf16[32,1024]{1,0:T(8,128)(2,1)} %copy-done.19) | copy-start | bytes 196612
  345.6 17.9 %copy-start.22 = (bf16[32,1024]{1,0:T(8,128)(2,1)S(1)}, bf16[32,1024]{1,0:T(8,128)(2,1)}, u32[]{:S(2)}) copy-start(bf16[32,1024]{1,0:T(8,128)(2,1)} %copy-done.21) | copy-start | bytes 196612
  (15 other events, 24.3 us)
